TPU v7x, 128 devices: a whole 4x4x4 slice. The times are simulated.
128 devices in a mesh: dp: 32 (over y, z, core), group: 4 (over x).
Axes of the slice: x: 4, y: 4, z: 4, core: 2. Of those that a mesh axis runs over, the one named last changes fastest.
Arguments:
- gradients: bfloat16 [128, 2, 2048, 512], P(('dp', 'group'))
- errors: float32 [128, 2, 2048, 512], P(('dp', 'group')), may hold values from -4 to 4
- warm_right: float32 [2, 512, 32], replicated, may hold values from -6 to 6
- norm_grads: float32 [128, 2, 2048], P(('dp', 'group'))
- norm_weights: float32 [2, 2048], replicated, may hold values from 0.5 to 1.5
- norm_moment: float32 [2, 2048], replicated, may hold values from -4 to 4
- owners: int32 [128], replicated, may hold values from 0 to 127, as said below
- slot_weights: bfloat16 [128, 2, 32, 512], P(('dp', 'group')), may hold values from -6 to 6
- slot_moment: float32 [128, 2, 32, 512], P(('dp', 'group')), may hold values from -4 to 4
Outputs:
- new_errors: float32 [128, 2, 2048, 512], P(('dp', 'group'))
- new_slot_moment: float32 [128, 2, 32, 512], P(('dp', 'group'))
- new_weights: bfloat16 [2, 2048, 512], replicated
- new_norm_weights: float32 [2, 2048], replicated
- new_norm_moment: float32 [2, 2048], replicated
Inputs may be any that keep to these rules, and one draw needn't show every extreme that they name: `owners`: each replica owns at most 2 pieces and some replica owns exactly 2; a replica's pieces occupy its slots in increasing piece order, the other slots hold nothing that is read.
All inputs are finite; a program needn't handle non-finite values.
Results may differ from a plain program's by a relative error of at most 0.0004.
Values may be sent and summed in bfloat16 or wider, within the bound.
No kernel may reach another device: no remote copies, remote signals or barrier semaphores. Data moves between devices by JAX's collectives and lax.ppermute only.
A program may use at most 128 MiB of HBM per device.

v0:
```python
import jax
import jax.numpy as jnp
from jax import lax
from jax.sharding import PartitionSpec as P

momentum_decay = 0.9
step_rate = 0.5


def orthonormal(factor):
    gram = jnp.einsum("...dr,...ds->...rs", factor, factor, precision=lax.Precision.HIGHEST)
    lower_factor = jnp.linalg.cholesky(gram)
    solved = jax.scipy.linalg.solve_triangular(
        lower_factor, jnp.swapaxes(factor, -1, -2), lower=True
    )
    return jnp.swapaxes(solved, -1, -2)


def times_right(merged, right_basis):
    return jnp.einsum("...dk,...kr->...dr", merged, right_basis, precision=lax.Precision.HIGHEST)


def times_left(merged, left_basis):
    return jnp.einsum("...dk,...dr->...kr", merged, left_basis, precision=lax.Precision.HIGHEST)


def stacked_rounds(merged, warm_right, norm_local, replicas):
    left_sum, norm_sum = lax.psum((times_right(merged, warm_right), norm_local), ("dp", "group"))
    left_one = orthonormal(left_sum)
    right_one = lax.psum(times_left(merged, left_one), ("dp", "group")) / replicas
    left_two = orthonormal(lax.psum(times_right(merged, right_one), ("dp", "group")))
    right_two = lax.psum(times_left(merged, left_two), ("dp", "group")) / replicas
    return (left_two, right_two, norm_sum)


def on_device(
    gradients,
    errors,
    warm_right,
    norm_grads,
    norm_weights,
    norm_moment,
    owners,
    slot_weights,
    slot_moment,
):
    replicas = lax.axis_size(("dp", "group"))
    merged = gradients[0].astype(jnp.float32) + errors[0]
    left_two, right_two, norm_sum = stacked_rounds(merged, warm_right, norm_grads[0], replicas)
    update = jnp.einsum("mdr,mkr->mdk", left_two, right_two, precision=lax.Precision.HIGHEST)
    new_errors = (merged - update)[None]
    new_norm_moment = momentum_decay * norm_moment + norm_sum / replicas
    new_norm_weights = norm_weights - step_rate * new_norm_moment
    piece_count = owners.shape[0]
    slot_count = slot_moment.shape[1]
    piece_rows = slot_moment.shape[2]
    features = slot_moment.shape[3]
    positions = jnp.arange(piece_count, dtype=jnp.int32)
    same_owner = owners[:, None] == owners[None, :]
    earlier = positions[:, None] < positions[None, :]
    slot_of = jnp.sum((same_owner & earlier).astype(jnp.int32), axis=0)
    my_index = lax.axis_index(("dp", "group"))
    owned = owners == my_index
    slot_range = jnp.arange(slot_count, dtype=jnp.int32)
    selector = (owned[:, None] & (slot_of[:, None] == slot_range[None, :])).astype(jnp.float32)
    pieces = update.reshape(piece_count, piece_rows, features)
    slot_update = jnp.einsum("js,jrk->srk", selector, pieces, precision=lax.Precision.HIGHEST)
    used = jnp.sum(selector, axis=0)[:, None, None] > 0.5
    old_moment = slot_moment[0]
    moment_slots = jnp.where(used, momentum_decay * old_moment + slot_update, old_moment)
    weight_slots = (slot_weights[0].astype(jnp.float32) - step_rate * moment_slots).astype(
        jnp.bfloat16
    )
    every_slot = lax.all_gather(weight_slots[None], ("dp", "group"), axis=0, tiled=True)
    chosen = every_slot[owners, slot_of]
    new_weights = chosen.reshape(2, piece_count * piece_rows // 2, features)
    return (new_errors, moment_slots[None], new_weights, new_norm_weights, new_norm_moment)


def solution(mesh):
    placed = (
        P(("dp", "group"), None, None, None),
        P(("dp", "group"), None, None, None),
        P(),
        P(("dp", "group"), None, None),
        P(),
        P(),
        P(),
        P(("dp", "group"), None, None, None),
        P(("dp", "group"), None, None, None),
    )
    return jax.shard_map(
        on_device,
        mesh=mesh,
        in_specs=placed,
        out_specs=(
            P(("dp", "group"), None, None, None),
            P(("dp", "group"), None, None, None),
            P(),
            P(),
            P(),
        ),
        check_vma=False,
    )
```

profile of v0, /device:TPU:0, one launch (start us, length us, event | category | flops | bytes accessed | tf_op | source)
XLA Modules:
  0.0 767.0 jit_solution(10844296189444193883)
XLA Ops:
  7.2 0.8 copy-done
  8.1 11.7 %fusion.6 = f32[2,2048,32]{1,2,0:T(8,128)} fusion(f32[2,512,32]{1,2,0:T(8,128)S(1)} %copy-done, f32[1,2,2048,512]{3,2,1,0:T(8,128)} %param.13, bf16[1,2,2048,512]{3,2,1,0:T(8,128)(2,1)} %param.12), kind=kOutput, calls=%fused_computation.8 | convolution fusion | flops 809500672 | bytes 13238272 | tf_op jit(solution)/shard_map/...dk,...kr->...dr/dot_general | solution.py:20
  19.9 148.4 %all-reduce.5.cloned.1.call-done = f32[2,2048,32]{1,2,0:T(8,128)} async-done(((f32[2,2048,32]{1,2,0:T(8,128)}), f32[2,2048,32]{1,2,0:T(8,128)}) %all-reduce.5.cloned.1.call-update) | async-done | bytes 524304 | tf_op jit(solution)/shard_map/psum | solution.py:28
  168.4 1.8 fusion.44
  170.2 5.9 custom-call.10
  176.1 0.1 compare_reduce_fusion.1
  176.3 4.9 custom-call.11
  181.3 1.7 fusion.19
  183.0 9.1 %fusion.4 = f32[2,512,32]{1,2,0:T(8,128)} fusion(f32[2,32,2048]{2,1,0:T(8,128)S(1)} %fusion.19, f32[1,2,2048,512]{3,2,1,0:T(8,128)} %param.13, bf16[1,2,2048,512]{3,2,1,0:T(8,128)(2,1)} %param.12), kind=kOutput, calls=%fused_computation.6 | convolution fusion | flops 809500672 | bytes 13238272 | tf_op jit(solution)/shard_map/...dk,...dr->...kr/dot_general | solution.py:24
  192.1 0.5 all-reduce.9.cloned.1.call-start
  192.6 141.0 %all-reduce.7.cloned.1.call-done = f32[2,512,32]{1,2,0:T(8,128)} async-done(((f32[2,512,32]{1,2,0:T(8,128)}), f32[2,512,32]{1,2,0:T(8,128)}) %all-reduce.7.cloned.1.call-update) | async-done | bytes 131088 | tf_op jit(solution)/shard_map/psum | solution.py:30
  333.6 13.6 %fusion.2 = f32[2,2048,32]{1,2,0:T(8,128)} fusion(f32[2,512,32]{1,2,0:T(8,128)} %all-reduce.7.cloned.1.call-done, f32[1,2,2048,512]{3,2,1,0:T(8,128)} %param.13, bf16[1,2,2048,512]{3,2,1,0:T(8,128)(2,1)} %param.12), kind=kOutput, calls=%fused_computation.4 | convolution fusion | flops 809533440 | bytes 13238272 | tf_op jit(solution)/shard_map/...dk,...kr->...dr/dot_general | solution.py:20
  347.4 0.1 convert_reduce_fusion
  347.5 0.1 convert_reduce_fusion.1
  347.6 143.1 %all-reduce.9.cloned.1.call-done = f32[2,2048,32]{1,2,0:T(8,128)} async-done(((f32[2,2048,32]{1,2,0:T(8,128)}), f32[2,2048,32]{1,2,0:T(8,128)}) %all-reduce.9.cloned.1.call-update) | async-done | bytes 524304 | tf_op jit(solution)/shard_map/psum | solution.py:31
  490.7 1.8 fusion.45
  492.5 5.9 custom-call.12
  498.4 0.1 compare_reduce_fusion
  498.6 4.9 custom-call.13
  503.6 1.7 fusion.17
  505.3 9.1 %fusion = f32[2,512,32]{1,2,0:T(8,128)} fusion(f32[2,32,2048]{2,1,0:T(8,128)S(1)} %fusion.17, f32[1,2,2048,512]{3,2,1,0:T(8,128)} %param.13, bf16[1,2,2048,512]{3,2,1,0:T(8,128)(2,1)} %param.12), kind=kOutput, calls=%fused_computation.2 | convolution fusion | flops 809500672 | bytes 13238272 | tf_op jit(solution)/shard_map/...dk,...dr->...kr/dot_general | solution.py:24
  514.4 0.2 all-gather.3.cloned.1.call-start
  514.7 141.3 %all-reduce.11.cloned.1.call-done = f32[2,512,32]{1,2,0:T(8,128)} async-done(((f32[2,512,32]{1,2,0:T(8,128)}), f32[2,512,32]{1,2,0:T(8,128)}) %all-reduce.11.cloned.1.call-update) | async-done | bytes 131088 | tf_op jit(solution)/shard_map/psum | solution.py:32
  656.0 7.6 fusion.22
  663.6 3.4 copy-done.1
  667.0 7.8 %fusion.21 = (bf16[2,32,512]{2,0,1:T(2,128)(2,1)S(1)}, f32[2,32,512]{2,0,1:T(2,128)S(1)}) fusion(bf16[1,2,32,512]{3,2,1,0:T(8,128)(2,1)S(1)} %copy-done.3, f32[128,32,512]{2,1,0:T(8,128)S(1)} %bitcast.76, pred[128]{0:T(512)(128)(4,1)S(1)} %broadcast_compare_fusion.1, s32[128]{0:T(128)S(1)} %convert_reduce_fusion, f32[1,2,32,512]{3,2,1,0:T(8,128)S(1)} %copy-done.2, ...), kind=kOutput, calls=%fused_computation.21 | convolution fusion | flops 50561536 | bytes 8782466 | tf_op jit(solution)/shard_map/js,jrk->srk/dot_general | solution.py:67
  674.8 0.6 copy.46
  675.5 64.4 %psum.39 = f32[2,2048]{1,0:T(2,128)S(1)} all-reduce(f32[2,2048]{1,0:T(2,128)S(1)} %bitcast.80), channel_id=1, replica_groups=mesh['dp'=32,'group'=4] {'dp','group'}, use_global_device_ids=true, to_apply=%region_8.11 | all-reduce | flops 4096 | bytes 32768 | tf_op jit(solution)/shard_map/psum | solution.py:28
  739.9 0.6 multiply_subtract_fusion
  740.5 0.7 copy.47
  741.2 12.8 %fusion.8 = f32[1,2,2048,512]{3,2,1,0:T(8,128)} fusion(f32[2,2048,512]{2,1,0:T(8,128)} %copy-done.1, f32[1,2,2048,512]{3,2,1,0:T(8,128)} %param.13, bf16[1,2,2048,512]{3,2,1,0:T(8,128)(2,1)} %param.12), kind=kLoop, calls=%fused_computation.10 | loop fusion | flops 6291456 | bytes 29360128 | tf_op jit(solution)/shard_map/broadcast_in_dim | solution.py:51
  754.0 6.3 gather_fusion
  (36 shorter events, 0.7 us)
Async XLA Ops:
  7.2 0.9 copy-start
  7.2 161.2 %all-reduce.5.cloned.1.call-start = ((), (), s32[]{:S(2)}) async-start(), calls=%async_computation | async-start | bytes 1048576 | tf_op jit(solution)/shard_map/psum | solution.py:28
  19.8 313.8 %all-reduce.7.cloned.1.call-start = ((), (), s32[]{:S(2)}) async-start(), calls=%async_computation.1 | async-start | bytes 262144 | tf_op jit(solution)/shard_map/psum | solution.py:30
  192.1 155.3 %copy-start.7 = (s32[128]{0:T(128)S(1)}, s32[128]{0:T(128)}, u32[]{:S(2)}) copy-start(s32[128]{0:T(128)} %param.18) | copy-start | bytes 1540
  192.1 298.5 %all-reduce.9.cloned.1.call-start = ((), (), s32[]{:S(2)}) async-start(), calls=%async_computation.2 | async-start | bytes 1048576 | tf_op jit(solution)/shard_map/psum | solution.py:31
  347.3 308.7 %all-reduce.11.cloned.1.call-start = ((), (), s32[]{:S(2)}) async-start(), calls=%async_computation.3 | async-start | bytes 262144 | tf_op jit(solution)/shard_map/psum | solution.py:32
  505.3 161.8 %copy-start.2 = (f32[1,2,32,512]{3,2,1,0:T(8,128)S(1)}, f32[1,2,32,512]{3,2,1,0:T(8,128)}, u32[]{:S(2)}) copy-start(f32[1,2,32,512]{3,2,1,0:T(8,128)} %param.20) | copy-start | bytes 393220
  505.3 161.8 %copy-start.3 = (bf16[1,2,32,512]{3,2,1,0:T(8,128)(2,1)S(1)}, bf16[1,2,32,512]{3,2,1,0:T(8,128)(2,1)}, u32[]{:S(2)}) copy-start(bf16[1,2,32,512]{3,2,1,0:T(8,128)(2,1)} %param.19) | copy-start | bytes 196612
  514.4 239.5 %all-gather.3.cloned.1.call-start = ((), (), s32[]{:S(2)}) async-start(), calls=%async_computation.4 | async-start | bytes 8454144 | tf_op jit(solution)/shard_map/all_gather | solution.py:74
  514.7 160.8 %copy-start.6 = (f32[1,2,2048]{2,1,0:T(2,128)S(1)}, f32[1,2,2048]{2,1,0:T(2,128)}, u32[]{:S(2)}) copy-start(f32[1,2,2048]{2,1,0:T(2,128)} %param.15) | copy-start | bytes 49156
  514.7 225.2 %copy-start.4 = (f32[2,2048]{1,0:T(2,128)S(1)}, f32[2,2048]{1,0:T(2,128)}, u32[]{:S(2)}) copy-start(f32[2,2048]{1,0:T(2,128)} %param.16) | copy-start | bytes 49156
  514.7 225.2 %copy-start.5 = (f32[2,2048]{1,0:T(2,128)S(1)}, f32[2,2048]{1,0:T(2,128)}, u32[]{:S(2)}) copy-start(f32[2,2048]{1,0:T(2,128)} %param.17) | copy-start | bytes 49156
  663.6 3.4 copy-start.1
Sparse Core Ops, SparseCore 0:
  19.9 148.3 all-reduce.4
  192.2 141.3 all-reduce.6
  347.4 143.1 all-reduce.8
  514.6 141.3 all-reduce.10
  675.6 67.2 all-gather.2
where the time goes:
time: 774 us; the launch traced here: 767 us
  waiting for transfers between devices  574 us (74%)
  matrix products  66 us (9%)
  blocking collectives  64.4 us (8%)
  other arithmetic  35.7 us (5%)
  between operations  14.2 us (2%)
  local copies, waits for them, and re-layouts  12 us (2%)
    psum x1, waiting for transfers between devices, stacked_rounds(): lax.psum((times_right(merged, warm_right), norm_local), ('dp', 'group'))  148 us
    psum x1, waiting for transfers between devices, stacked_rounds(): lax.psum(times_right(merged, right_one), ('dp', 'group'))  143 us
    psum x1, waiting for transfers between devices, stacked_rounds(): lax.psum(times_left(merged, left_two), ('dp', 'group')) / replicas  141 us
    psum x1, waiting for transfers between devices, stacked_rounds(): lax.psum(times_left(merged, left_one), ('dp', 'group')) / replicas  141 us
    psum x1, blocking collectives, stacked_rounds(): lax.psum((times_right(merged, warm_right), norm_local), ('dp', 'group'))  64.4 us
    dot_general x2, matrix products, times_right(): jnp.einsum('...dk,...kr->...dr', merged, right_basis, precision=lax.Preci...  25.4 us
    dot_general x2, matrix products, times_left(): jnp.einsum('...dk,...dr->...kr', merged, left_basis, precision=lax.Precis...  18.3 us
  transfers between devices with their start and end apart: 5, of which 4 were waited for; matrix products, arithmetic and copies ran while one was open for 2% of the time, Pallas kernels for 0%

commit v1 on v0

--- a/solution.py
+++ b/solution.py
@@ -5,32 +5,79 @@
 
 momentum_decay = 0.9
 step_rate = 0.5
+HI = lax.Precision.HIGHEST
 
 
-def orthonormal(factor):
-    gram = jnp.einsum("...dr,...ds->...rs", factor, factor, precision=lax.Precision.HIGHEST)
-    lower_factor = jnp.linalg.cholesky(gram)
-    solved = jax.scipy.linalg.solve_triangular(
-        lower_factor, jnp.swapaxes(factor, -1, -2), lower=True
-    )
-    return jnp.swapaxes(solved, -1, -2)
+def pair_steps(dp_size, group_size):
+    dp = lax.axis_index("dp")
+    g = lax.axis_index("group")
+    steps = []
+    steps.append(("dp", [(i, i ^ 1) for i in range(dp_size)], dp & 1))
+    steps.append(("group", [(i, i ^ 1) for i in range(group_size)], (g ^ (g // 2)) & 1))
+    steps.append(("group", [(i, group_size - 1 - i) for i in range(group_size)], g // (group_size // 2)))
+    z_size = 4
+    y_size = dp_size // (2 * z_size)
+
+    def dp_of(y, z, c):
+        return (y * z_size + z) * 2 + c
+
+    zc = (dp // 2) % z_size
+    yc = dp // (2 * z_size)
+    perm_z1, perm_z2, perm_y1, perm_y2 = [], [], [], []
+    for y in range(y_size):
+        for z in range(z_size):
+            for c in range(2):
+                src = dp_of(y, z, c)
+                perm_z1.append((src, dp_of(y, z ^ 1, c)))
+                perm_z2.append((src, dp_of(y, z_size - 1 - z, c)))
+                perm_y1.append((src, dp_of(y ^ 1, z, c)))
+                perm_y2.append((src, dp_of(y_size - 1 - y, z, c)))
+    steps.append(("dp", perm_z1, (zc ^ (zc // 2)) & 1))
+    steps.append(("dp", perm_z2, zc // (z_size // 2)))
+    steps.append(("dp", perm_y1, (yc ^ (yc // 2)) & 1))
+    steps.append(("dp", perm_y2, yc // (y_size // 2)))
+    return steps
 
 
-def times_right(merged, right_basis):
-    return jnp.einsum("...dk,...kr->...dr", merged, right_basis, precision=lax.Precision.HIGHEST)
+def sum_doubling(x, steps):
+    for axis, perm, _ in steps:
+        x = x + lax.ppermute(x, axis, perm)
+    return x
 
 
-def times_left(merged, left_basis):
-    return jnp.einsum("...dk,...dr->...kr", merged, left_basis, precision=lax.Precision.HIGHEST)
+def sum_halving(x, steps, extra=None):
+    bits = []
+    for axis, perm, bit in steps:
+        half = x.shape[0] // 2
+        keep = lax.dynamic_slice_in_dim(x, bit * half, half)
+        send = lax.dynamic_slice_in_dim(x, (1 - bit) * half, half)
+        if extra is None:
+            got = lax.ppermute(send, axis, perm)
+        else:
+            got, got_extra = lax.ppermute((send, extra), axis, perm)
+            extra = extra + got_extra
+        x = keep + got
+        bits.append(bit)
+    for (axis, perm, _), bit in zip(reversed(steps), reversed(bits)):
+        got = lax.ppermute(x, axis, perm)
+        low = jnp.where(bit == 0, x, got)
+        high = jnp.where(bit == 0, got, x)
+        x = jnp.concatenate([low, high])
+    return x, extra
 
 
-def stacked_rounds(merged, warm_right, norm_local, replicas):
-    left_sum, norm_sum = lax.psum((times_right(merged, warm_right), norm_local), ("dp", "group"))
-    left_one = orthonormal(left_sum)
-    right_one = lax.psum(times_left(merged, left_one), ("dp", "group")) / replicas
-    left_two = orthonormal(lax.psum(times_right(merged, right_one), ("dp", "group")))
-    right_two = lax.psum(times_left(merged, left_two), ("dp", "group")) / replicas
-    return (left_two, right_two, norm_sum)
+def orth_t(ft):
+    gram = jnp.einsum("mrd,msd->mrs", ft, ft, precision=HI)
+    lower_factor = jnp.linalg.cholesky(gram)
+    return jax.scipy.linalg.solve_triangular(lower_factor, ft, lower=True)
+
+
+def left_t(merged, right_t):
+    return jnp.einsum("mdk,mrk->mrd", merged, right_t, precision=HI)
+
+
+def right_t_of(merged, left_tr):
+    return jnp.einsum("mdk,mrd->mrk", merged, left_tr, precision=HI)
 
 
 def on_device(
@@ -44,10 +91,21 @@
     slot_weights,
     slot_moment,
 ):
-    replicas = lax.axis_size(("dp", "group"))
+    dp_size = lax.axis_size("dp")
+    group_size = lax.axis_size("group")
+    replicas = dp_size * group_size
+    steps = pair_steps(dp_size, group_size)
     merged = gradients[0].astype(jnp.float32) + errors[0]
-    left_two, right_two, norm_sum = stacked_rounds(merged, warm_right, norm_grads[0], replicas)
-    update = jnp.einsum("mdr,mkr->mdk", left_two, right_two, precision=lax.Precision.HIGHEST)
+    lshape = (merged.shape[0], warm_right.shape[2], merged.shape[1])
+
+    p1 = left_t(merged, jnp.swapaxes(warm_right, 1, 2))
+    p1_sum, norm_sum = sum_halving(p1.reshape(-1), steps, norm_grads[0])
+    left_one = orth_t(p1_sum.reshape(lshape))
+    right_one = sum_doubling(right_t_of(merged, left_one), steps) / replicas
+    p2_sum, _ = sum_halving(left_t(merged, right_one).reshape(-1), steps)
+    left_two = orth_t(p2_sum.reshape(lshape))
+    right_two = sum_doubling(right_t_of(merged, left_two), steps) / replicas
+    update = jnp.einsum("mrd,mrk->mdk", left_two, right_two, precision=HI)
     new_errors = (merged - update)[None]
     new_norm_moment = momentum_decay * norm_moment + norm_sum / replicas
     new_norm_weights = norm_weights - step_rate * new_norm_moment
@@ -64,7 +122,7 @@
     slot_range = jnp.arange(slot_count, dtype=jnp.int32)
     selector = (owned[:, None] & (slot_of[:, None] == slot_range[None, :])).astype(jnp.float32)
     pieces = update.reshape(piece_count, piece_rows, features)
-    slot_update = jnp.einsum("js,jrk->srk", selector, pieces, precision=lax.Precision.HIGHEST)
+    slot_update = jnp.einsum("js,jrk->srk", selector, pieces, precision=HI)
     used = jnp.sum(selector, axis=0)[:, None, None] > 0.5
     old_moment = slot_moment[0]
     moment_slots = jnp.where(used, momentum_decay * old_moment + slot_update, old_moment)

time: 774 us -> 377 us (0.49)
  waiting for transfers between devices: 574 us -> 176 us
  starting transfers between devices: 0.84 us -> 73.9 us
  blocking collectives: 64.4 us -> 0 us
  matrix products: 66 us -> 55.7 us
    psum x4 -> x0, waiting for transfers between devices: 574 us -> none  [the longest x1 148 us: stacked_rounds(): lax.psum((times_right(merged, warm_right), norm_local), ('dp', 'group'))]
    ppermute x0 -> x49, waiting for transfers between devices: none -> 147 us  [the longest x14 52.1 us: sum_doubling(): x = x + lax.ppermute(x, axis, perm)]
    ppermute x0 -> x49, starting transfers between devices: none -> 73.8 us  [the longest x14 25.2 us: sum_halving(): got, got_extra = lax.ppermute((send, extra), axis, perm)]
    psum x1 -> x0, blocking collectives: 64.4 us -> none  [stacked_rounds(): lax.psum((times_right(merged, warm_right), norm_local), ('dp', 'group'))]
    all_gather x1, waiting for transfers between devices: 0.01 us -> 28.8 us  [on_device(): lax.all_gather(weight_slots[None], ('dp', 'group'), axis=0, tiled=True)]
    dot_general x8, matrix products: 62.6 us -> 54.4 us  [the longest x2 20.8 us: left_t(): return jnp.einsum('mdk,mrk->mrd', merged, right_t, precision=HI)]
  transfers between devices with their start and end apart: 5 -> 50, of which waited for: 4 -> 50; matrix products, arithmetic and copies ran while one was open for 2% -> 4% of each run, Pallas kernels for 0% -> 0%
where the time goes in v1:
time: 377 us; the launch traced here: 370 us
  waiting for transfers between devices  176 us (47%)
  starting transfers between devices  73.9 us (20%)
  matrix products  55.7 us (15%)
  other arithmetic  36.5 us (10%)
  between operations  15 us (4%)
  local copies, waits for them, and re-layouts  12.6 us (3%)
    ppermute x14, waiting for transfers between devices, sum_doubling(): x = x + lax.ppermute(x, axis, perm)  52.1 us
    ppermute x14, waiting for transfers between devices, sum_halving(): got = lax.ppermute(x, axis, perm)  40.5 us
    ppermute x14, waiting for transfers between devices, sum_halving(): got, got_extra = lax.ppermute((send, extra), axis, perm)  33.7 us
    all_gather x1, waiting for transfers between devices, on_device(): lax.all_gather(weight_slots[None], ('dp', 'group'), axis=0, tiled=True)  28.8 us
    ppermute x14, starting transfers between devices, sum_halving(): got, got_extra = lax.ppermute((send, extra), axis, perm)  25.2 us
    ppermute x7, waiting for transfers between devices, sum_halving(): got = lax.ppermute(send, axis, perm)  20.8 us
    dot_general x2, matrix products, left_t(): return jnp.einsum('mdk,mrk->mrd', merged, right_t, precision=HI)  20.8 us
    ppermute x14, starting transfers between devices, sum_halving(): got = lax.ppermute(x, axis, perm)  19.6 us
  transfers between devices with their start and end apart: 50, of which 50 were waited for; matrix products, arithmetic and copies ran while one was open for 4% of the time, Pallas kernels for 0%

profile of v1, /device:TPU:0, one launch (start us, length us, event | category | flops | bytes accessed | tf_op | source)
XLA Modules:
  0.0 369.7 jit_solution(3116109516913692296)
XLA Ops:
  8.1 11.0 %fusion.6 = f32[2,2048,32]{1,2,0:T(8,128)S(1)} fusion(f32[2,512,32]{1,2,0:T(8,128)S(1)} %copy-done, f32[1,2,2048,512]{3,2,1,0:T(8,128)} %param.13, bf16[1,2,2048,512]{3,2,1,0:T(8,128)(2,1)} %param.12), kind=kOutput, calls=%fused_computation.8 | convolution fusion | flops 809500672 | bytes 13238272 | tf_op jit(solution)/shard_map/mdk,mrk->mrd/dot_general | solution.py:76
  22.6 3.9 %collective-permute-done.1 = f32[32768]{0:T(1024)S(1)} collective-permute-done((f32[32768]{0:T(1024)S(1)}, f32[32768]{0:T(1024)S(1)}, u32[]{:S(2)}, u32[]{:S(2)}) %collective-permute-start.1) | collective-permute-done | bytes 131104 | tf_op jit(solution)/shard_map/ppermute | solution.py:57
  36.1 4.2 %collective-permute-start.4 = (f32[4096]{0:T(1024)S(1)}, f32[4096]{0:T(1024)S(1)}, u32[]{:S(2)}, u32[]{:S(2)}) collective-permute-start(f32[4096]{0:T(1024)S(1)} %dynamic_slice.93), channel_id=1, source_target_pairs={{0,24},{4,28},{8,16},{12,20},{16,8},{20,12},{24,0},{28,4},{32,56},... | collective-permute-start | bytes 49160 | tf_op jit(solution)/shard_map/ppermute | solution.py:57
  55.4 3.6 collective-permute-done.8
  64.2 3.9 %collective-permute-done.10 = f32[8192]{0:T(1024)S(1)} collective-permute-done((f32[8192]{0:T(1024)S(1)}, f32[8192]{0:T(1024)S(1)}, u32[]{:S(2)}, u32[]{:S(2)}) %collective-permute-start.10) | collective-permute-done | bytes 32800 | tf_op jit(solution)/shard_map/ppermute | solution.py:62
  73.8 4.9 %collective-permute-done.12 = f32[32768]{0:T(1024)S(1)} collective-permute-done((f32[32768]{0:T(1024)S(1)}, f32[32768]{0:T(1024)S(1)}, u32[]{:S(2)}, u32[]{:S(2)}) %collective-permute-start.12) | collective-permute-done | bytes 131104 | tf_op jit(solution)/shard_map/ppermute | solution.py:62
  81.6 5.9 %custom-call.10 = f32[2,32,32]{2,1,0:T(8,128)S(1)} custom-call(f32[2,32,32]{2,1,0:T(8,128)S(1)} %fusion.31), custom_call_target="Cholesky" | custom-call | tf_op jit(solution)/shard_map/jit(cholesky)/cholesky | solution.py:71
  87.7 4.9 %custom-call.11 = f32[2,1,32,32]{2,3,1,0:T(8,128)S(1)} custom-call(f32[2,1,32,32]{3,2,1,0:T(8,128)S(1)} %select_bitcast_fusion.1), custom_call_target="InvertDiagBlocksLowerTriangular" | custom-call | tf_op jit(solution)/shard_map/jit(_solve_triangular)/vmap()/triangular_solve | solution.py:72
  93.3 9.6 %fusion.4 = f32[2,32,512]{2,1,0:T(8,128)S(1)} fusion(f32[2,32,2048]{2,1,0:T(8,128)S(1)} %fusion.29, f32[1,2,2048,512]{3,2,1,0:T(8,128)} %param.13, bf16[1,2,2048,512]{3,2,1,0:T(8,128)(2,1)} %param.12), kind=kOutput, calls=%fused_computation.6 | convolution fusion | flops 809500672 | bytes 13238272 | tf_op jit(solution)/shard_map/mdk,mrd->mrk/dot_general | solution.py:80
  104.4 5.5 %collective-permute-done.15 = f32[2,32,512]{2,1,0:T(8,128)S(1)} collective-permute-done((f32[2,32,512]{2,1,0:T(8,128)S(1)}, f32[2,32,512]{2,1,0:T(8,128)S(1)}, u32[]{:S(2)}, u32[]{:S(2)}) %collective-permute-start.15) | collective-permute-done | bytes 131104 | tf_op jit(solution)/shard_map/ppermute | solution.py:44
  116.4 5.0 %collective-permute-done.17 = f32[2,32,512]{2,1,0:T(8,128)S(1)} collective-permute-done((f32[2,32,512]{2,1,0:T(8,128)S(1)}, f32[2,32,512]{2,1,0:T(8,128)S(1)}, u32[]{:S(2)}, u32[]{:S(2)}) %collective-permute-start.17) | collective-permute-done | bytes 131104 | tf_op jit(solution)/shard_map/ppermute | solution.py:44
  127.7 5.0 %collective-permute-done.19 = f32[2,32,512]{2,1,0:T(8,128)S(1)} collective-permute-done((f32[2,32,512]{2,1,0:T(8,128)S(1)}, f32[2,32,512]{2,1,0:T(8,128)S(1)}, u32[]{:S(2)}, u32[]{:S(2)}) %collective-permute-start.19) | collective-permute-done | bytes 131104 | tf_op jit(solution)/shard_map/ppermute | solution.py:44
  139.0 9.9 %fusion.2 = f32[2,32,2048]{2,1,0:T(8,128)S(1)} fusion(f32[2,32,512]{2,1,0:T(8,128)S(1)} %add.242, f32[2,32,512]{2,1,0:T(8,128)S(1)} %collective-permute-done.20, f32[1,2,2048,512]{3,2,1,0:T(8,128)} %param.13, bf16[1,2,2048,512]{3,2,1,0:T(8,128)(2,1)S(1)} %copy-done.1), kind=kOutput, calls=%fused_computation.4 | convolution fusion | flops 809566208 | bytes 13369344 | tf_op jit(solution)/shard_map/mdk,mrk->mrd/dot_general | solution.py:76
  150.7 5.5 %collective-permute-done.22 = f32[32768]{0:T(1024)S(1)} collective-permute-done((f32[32768]{0:T(1024)S(1)}, f32[32768]{0:T(1024)S(1)}, u32[]{:S(2)}, u32[]{:S(2)}) %collective-permute-start.22) | collective-permute-done | bytes 131104 | tf_op jit(solution)/shard_map/ppermute | solution.py:55
  162.0 3.9 %collective-permute-done.24 = f32[8192]{0:T(1024)S(1)} collective-permute-done((f32[8192]{0:T(1024)S(1)}, f32[8192]{0:T(1024)S(1)}, u32[]{:S(2)}, u32[]{:S(2)}) %collective-permute-start.24) | collective-permute-done | bytes 32800 | tf_op jit(solution)/shard_map/ppermute | solution.py:55
  170.9 3.6 collective-permute-done.26
  193.5 3.9 %collective-permute-done.31 = f32[8192]{0:T(1024)S(1)} collective-permute-done((f32[8192]{0:T(1024)S(1)}, f32[8192]{0:T(1024)S(1)}, u32[]{:S(2)}, u32[]{:S(2)}) %collective-permute-start.31) | collective-permute-done | bytes 32800 | tf_op jit(solution)/shard_map/ppermute | solution.py:62
  203.2 5.0 %collective-permute-done.33 = f32[32768]{0:T(1024)S(1)} collective-permute-done((f32[32768]{0:T(1024)S(1)}, f32[32768]{0:T(1024)S(1)}, u32[]{:S(2)}, u32[]{:S(2)}) %collective-permute-start.33) | collective-permute-done | bytes 131104 | tf_op jit(solution)/shard_map/ppermute | solution.py:62
  210.7 5.9 %custom-call.12 = f32[2,32,32]{2,1,0:T(8,128)S(1)} custom-call(f32[2,32,32]{2,1,0:T(8,128)S(1)} %fusion.28), custom_call_target="Cholesky" | custom-call | tf_op jit(solution)/shard_map/jit(cholesky)/cholesky | solution.py:71
  216.8 4.9 %custom-call.13 = f32[2,1,32,32]{2,3,1,0:T(8,128)S(1)} custom-call(f32[2,1,32,32]{3,2,1,0:T(8,128)S(1)} %select_bitcast_fusion), custom_call_target="InvertDiagBlocksLowerTriangular" | custom-call | tf_op jit(solution)/shard_map/jit(_solve_triangular)/vmap()/triangular_solve | solution.py:72
  222.3 8.2 %fusion = f32[2,32,512]{2,1,0:T(8,128)S(1)} fusion(f32[2,32,2048]{2,1,0:T(8,128)S(1)} %fusion.26, f32[1,2,2048,512]{3,2,1,0:T(8,128)} %param.13, bf16[1,2,2048,512]{3,2,1,0:T(8,128)(2,1)} %param.12), kind=kOutput, calls=%fused_computation.2 | convolution fusion | flops 809500672 | bytes 13238272 | tf_op jit(solution)/shard_map/mdk,mrd->mrk/dot_general | solution.py:80
  232.1 5.5 %collective-permute-done.36 = f32[2,32,512]{2,1,0:T(8,128)S(1)} collective-permute-done((f32[2,32,512]{2,1,0:T(8,128)S(1)}, f32[2,32,512]{2,1,0:T(8,128)S(1)}, u32[]{:S(2)}, u32[]{:S(2)}) %collective-permute-start.36) | collective-permute-done | bytes 131104 | tf_op jit(solution)/shard_map/ppermute | solution.py:44
  244.1 4.9 %collective-permute-done.38 = f32[2,32,512]{2,1,0:T(8,128)S(1)} collective-permute-done((f32[2,32,512]{2,1,0:T(8,128)S(1)}, f32[2,32,512]{2,1,0:T(8,128)S(1)}, u32[]{:S(2)}, u32[]{:S(2)}) %collective-permute-start.38) | collective-permute-done | bytes 131104 | tf_op jit(solution)/shard_map/ppermute | solution.py:44
  255.7 4.7 %collective-permute-done.40 = f32[2,32,512]{2,1,0:T(8,128)S(1)} collective-permute-done((f32[2,32,512]{2,1,0:T(8,128)S(1)}, f32[2,32,512]{2,1,0:T(8,128)S(1)}, u32[]{:S(2)}, u32[]{:S(2)}) %collective-permute-start.40) | collective-permute-done | bytes 131104 | tf_op jit(solution)/shard_map/ppermute | solution.py:44
  266.8 6.7 %fusion.18 = f32[2,2048,512]{2,1,0:T(8,128)S(1)} fusion(f32[2,32,2048]{2,1,0:T(8,128)S(1)} %fusion.26, f32[2,32,512]{2,1,0:T(8,128)S(1)} %add.256, f32[2,32,512]{2,1,0:T(8,128)S(1)} %collective-permute-done.41), kind=kOutput, calls=%fused_computation.25 | convolution fusion | flops 805371904 | bytes 9175040 | tf_op jit(solution)/shard_map/mrd,mrk->mdk/dot_general | solution.py:108
  277.0 7.8 %fusion.17 = (bf16[2,32,512]{2,0,1:T(2,128)(2,1)S(1)}, f32[2,32,512]{2,0,1:T(2,128)S(1)}) fusion(bf16[1,2,32,512]{3,2,1,0:T(8,128)(2,1)S(1)} %copy-done.4, f32[128,32,512]{2,1,0:T(8,128)S(1)} %bitcast.78, pred[128]{0:T(512)(128)(4,1)S(1)} %broadcast_compare_fusion.1, s32[128]{0:T(128)S(1)} %convert_reduce_fusion, f32[1,2,32,512]{3,2,1,0:T(8,128)S(1)} %copy-done.3, ...), kind=kOutput, calls=%fused_computation.23 | convolution fusion | flops 50561536 | bytes 8782466 | tf_op jit(solution)/shard_map/js,jrk->srk/dot_general | solution.py:125
  286.8 3.7 %collective-permute-done.43 = f32[2,2048]{1,0:T(2,128)S(1)} collective-permute-done((f32[2,2048]{1,0:T(2,128)S(1)}, f32[2,2048]{1,0:T(2,128)S(1)}, u32[]{:S(2)}, u32[]{:S(2)}) %collective-permute-start.43) | collective-permute-done | bytes 16416 | tf_op jit(solution)/shard_map/ppermute | solution.py:57
  295.7 3.7 %collective-permute-done.45 = f32[2,2048]{1,0:T(2,128)S(1)} collective-permute-done((f32[2,2048]{1,0:T(2,128)S(1)}, f32[2,2048]{1,0:T(2,128)S(1)}, u32[]{:S(2)}, u32[]{:S(2)}) %collective-permute-start.45) | collective-permute-done | bytes 16416 | tf_op jit(solution)/shard_map/ppermute | solution.py:57
  304.6 3.7 %collective-permute-done.47 = f32[2,2048]{1,0:T(2,128)S(1)} collective-permute-done((f32[2,2048]{1,0:T(2,128)S(1)}, f32[2,2048]{1,0:T(2,128)S(1)}, u32[]{:S(2)}, u32[]{:S(2)}) %collective-permute-start.47) | collective-permute-done | bytes 16416 | tf_op jit(solution)/shard_map/ppermute | solution.py:57
  314.7 12.8 %fusion.8 = f32[1,2,2048,512]{3,2,1,0:T(8,128)} fusion(f32[2,2048,512]{2,1,0:T(8,128)} %copy-done.2, f32[1,2,2048,512]{3,2,1,0:T(8,128)} %param.13, bf16[1,2,2048,512]{3,2,1,0:T(8,128)(2,1)} %param.12), kind=kLoop, calls=%fused_computation.10 | loop fusion | flops 6291456 | bytes 29360128 | tf_op jit(solution)/shard_map/broadcast_in_dim | solution.py:109
  327.5 28.8 %all-gather.3.cloned.1.call-done = bf16[256,32,512]{2,1,0:T(8,128)(2,1)} async-done(((bf16[2,32,512]{2,1,0:T(8,128)(2,1)}), bf16[256,32,512]{2,1,0:T(8,128)(2,1)}) %all-gather.3.cloned.1.call-update) | async-done | bytes 8388624 | tf_op jit(solution)/shard_map/all_gather | solution.py:132
  356.4 6.3 %gather_fusion = bf16[128,32,512]{2,1,0:T(8,128)(2,1)} fusion(bf16[128,2,32,512]{3,2,1,0:T(8,128)(2,1)} %bitcast.82, s32[128]{0:T(128)S(1)} %fusion.41), kind=kCustom, calls=%fused_computation | custom fusion | bytes 8389632 | tf_op jit(solution)/shard_map/gather | solution.py:133
  (205 shorter events, 147.6 us)
Async XLA Ops:
  7.2 349.2 %all-gather.3.cloned.1.call-start = ((), (), s32[]{:S(2)}) async-start(), calls=%async_computation | async-start | bytes 8454144 | tf_op jit(solution)/shard_map/all_gather | solution.py:132
  20.9 5.6 %collective-permute-start.1 = (f32[32768]{0:T(1024)S(1)}, f32[32768]{0:T(1024)S(1)}, u32[]{:S(2)}, u32[]{:S(2)}) collective-permute-start(f32[32768]{0:T(1024)S(1)} %dynamic_slice.87), channel_id=1, source_target_pairs={{0,1},{1,0},{2,3},{3,2},{4,5},{5,4},{6,7},{7,6},{8,9},{9,8},{10,11... | collective-permute-start | bytes 393224 | tf_op jit(solution)/shard_map/ppermute | solution.py:57
  26.5 5.6 %collective-permute-start.2 = (f32[16384]{0:T(1024)S(1)}, f32[16384]{0:T(1024)S(1)}, u32[]{:S(2)}, u32[]{:S(2)}) collective-permute-start(f32[16384]{0:T(1024)S(1)} %dynamic_slice.89), channel_id=1, source_target_pairs={{0,3},{1,2},{2,1},{3,0},{4,7},{5,6},{6,5},{7,4},{8,11},{9,10},{10,... | collective-permute-start | bytes 196616 | tf_op jit(solution)/shard_map/ppermute | solution.py:57
  36.1 5.9 %collective-permute-start.4 = (f32[4096]{0:T(1024)S(1)}, f32[4096]{0:T(1024)S(1)}, u32[]{:S(2)}, u32[]{:S(2)}) collective-permute-start(f32[4096]{0:T(1024)S(1)} %dynamic_slice.93), channel_id=1, source_target_pairs={{0,24},{4,28},{8,16},{12,20},{16,8},{20,12},{24,0},{28,4},{32,56},... | collective-permute-start | bytes 49160 | tf_op jit(solution)/shard_map/ppermute | solution.py:57
  45.7 4.8 %collective-permute-start.6 = (f32[1024]{0:T(1024)S(1)}, f32[1024]{0:T(1024)S(1)}, u32[]{:S(2)}, u32[]{:S(2)}) collective-permute-start(f32[1024]{0:T(1024)S(1)} %dynamic_slice.97), channel_id=1, source_target_pairs={{0,96},{4,100},{8,104},{12,108},{16,112},{20,116},{24,120},{28,124... | collective-permute-start | bytes 12296 | tf_op jit(solution)/shard_map/ppermute | solution.py:57
  50.6 4.8 %collective-permute-start.7 = (f32[1024]{0:T(1024)S(1)}, f32[1024]{0:T(1024)S(1)}, u32[]{:S(2)}, u32[]{:S(2)}) collective-permute-start(f32[1024]{0:T(1024)S(1)} %dynamic-slice_add_fusion.13), channel_id=1, source_target_pairs={{0,96},{4,100},{8,104},{12,108},{16,112},{20,116},{24,120},{28,124... | collective-permute-start | bytes 12296 | tf_op jit(solution)/shard_map/ppermute | solution.py:62
  59.1 5.0 %collective-permute-start.9 = (f32[4096]{0:T(1024)S(1)}, f32[4096]{0:T(1024)S(1)}, u32[]{:S(2)}, u32[]{:S(2)}) collective-permute-start(f32[4096]{0:T(1024)S(1)} %pad_maximum_fusion.8), channel_id=1, source_target_pairs={{0,24},{4,28},{8,16},{12,20},{16,8},{20,12},{24,0},{28,4},{32,56},... | collective-permute-start | bytes 49160 | tf_op jit(solution)/shard_map/ppermute | solution.py:62
  68.1 5.6 %collective-permute-start.11 = (f32[16384]{0:T(1024)S(1)}, f32[16384]{0:T(1024)S(1)}, u32[]{:S(2)}, u32[]{:S(2)}) collective-permute-start(f32[16384]{0:T(1024)S(1)} %pad_maximum_fusion.4), channel_id=1, source_target_pairs={{0,3},{1,2},{2,1},{3,0},{4,7},{5,6},{6,5},{7,4},{8,11},{9,10},{10,... | collective-permute-start | bytes 196616 | tf_op jit(solution)/shard_map/ppermute | solution.py:62
  73.7 5.0 %collective-permute-start.12 = (f32[32768]{0:T(1024)S(1)}, f32[32768]{0:T(1024)S(1)}, u32[]{:S(2)}, u32[]{:S(2)}) collective-permute-start(f32[32768]{0:T(1024)S(1)} %pad_maximum_fusion.2), channel_id=1, source_target_pairs={{0,1},{1,0},{2,3},{3,2},{4,5},{5,4},{6,7},{7,6},{8,9},{9,8},{10,11... | collective-permute-start | bytes 393224 | tf_op jit(solution)/shard_map/ppermute | solution.py:62
  104.3 5.6 %collective-permute-start.15 = (f32[2,32,512]{2,1,0:T(8,128)S(1)}, f32[2,32,512]{2,1,0:T(8,128)S(1)}, u32[]{:S(2)}, u32[]{:S(2)}) collective-permute-start(f32[2,32,512]{2,1,0:T(8,128)S(1)} %add.237), channel_id=1, source_target_pairs={{0,1},{1,0},{2,3},{3,2},{4,5},{5,4},{6,7},{7,6},{8,9},{9,8},{10,11... | collective-permute-start | bytes 393224 | tf_op jit(solution)/shard_map/ppermute | solution.py:44
  110.0 6.3 %collective-permute-start.16 = (f32[2,32,512]{2,1,0:T(8,128)S(1)}, f32[2,32,512]{2,1,0:T(8,128)S(1)}, u32[]{:S(2)}, u32[]{:S(2)}) collective-permute-start(f32[2,32,512]{2,1,0:T(8,128)S(1)} %add.238), channel_id=1, source_target_pairs={{0,3},{1,2},{2,1},{3,0},{4,7},{5,6},{6,5},{7,4},{8,11},{9,10},{10,... | collective-permute-start | bytes 393224 | tf_op jit(solution)/shard_map/ppermute | solution.py:44
  116.3 5.0 %collective-permute-start.17 = (f32[2,32,512]{2,1,0:T(8,128)S(1)}, f32[2,32,512]{2,1,0:T(8,128)S(1)}, u32[]{:S(2)}, u32[]{:S(2)}) collective-permute-start(f32[2,32,512]{2,1,0:T(8,128)S(1)} %add.239), channel_id=1, source_target_pairs={{0,8},{4,12},{8,0},{12,4},{16,24},{20,28},{24,16},{28,20},{32,40},... | collective-permute-start | bytes 393224 | tf_op jit(solution)/shard_map/ppermute | solution.py:44
  121.3 6.3 %collective-permute-start.18 = (f32[2,32,512]{2,1,0:T(8,128)S(1)}, f32[2,32,512]{2,1,0:T(8,128)S(1)}, u32[]{:S(2)}, u32[]{:S(2)}) collective-permute-start(f32[2,32,512]{2,1,0:T(8,128)S(1)} %add.240), channel_id=1, source_target_pairs={{0,24},{4,28},{8,16},{12,20},{16,8},{20,12},{24,0},{28,4},{32,56},... | collective-permute-start | bytes 393224 | tf_op jit(solution)/shard_map/ppermute | solution.py:44
  127.6 5.0 %collective-permute-start.19 = (f32[2,32,512]{2,1,0:T(8,128)S(1)}, f32[2,32,512]{2,1,0:T(8,128)S(1)}, u32[]{:S(2)}, u32[]{:S(2)}) collective-permute-start(f32[2,32,512]{2,1,0:T(8,128)S(1)} %add.241), channel_id=1, source_target_pairs={{0,32},{4,36},{8,40},{12,44},{16,48},{20,52},{24,56},{28,60},{32,0... | collective-permute-start | bytes 393224 | tf_op jit(solution)/shard_map/ppermute | solution.py:44
  132.7 6.3 %collective-permute-start.20 = (f32[2,32,512]{2,1,0:T(8,128)S(1)}, f32[2,32,512]{2,1,0:T(8,128)S(1)}, u32[]{:S(2)}, u32[]{:S(2)}) collective-permute-start(f32[2,32,512]{2,1,0:T(8,128)S(1)} %add.242), channel_id=1, source_target_pairs={{0,96},{4,100},{8,104},{12,108},{16,112},{20,116},{24,120},{28,124... | collective-permute-start | bytes 393224 | tf_op jit(solution)/shard_map/ppermute | solution.py:44
  150.6 5.6 %collective-permute-start.22 = (f32[32768]{0:T(1024)S(1)}, f32[32768]{0:T(1024)S(1)}, u32[]{:S(2)}, u32[]{:S(2)}) collective-permute-start(f32[32768]{0:T(1024)S(1)} %dynamic_slice.101), channel_id=1, source_target_pairs={{0,1},{1,0},{2,3},{3,2},{4,5},{5,4},{6,7},{7,6},{8,9},{9,8},{10,11... | collective-permute-start | bytes 393224 | tf_op jit(solution)/shard_map/ppermute | solution.py:55
  156.3 5.6 %collective-permute-start.23 = (f32[16384]{0:T(1024)S(1)}, f32[16384]{0:T(1024)S(1)}, u32[]{:S(2)}, u32[]{:S(2)}) collective-permute-start(f32[16384]{0:T(1024)S(1)} %dynamic_slice.103), channel_id=1, source_target_pairs={{0,3},{1,2},{2,1},{3,0},{4,7},{5,6},{6,5},{7,4},{8,11},{9,10},{10,... | collective-permute-start | bytes 196616 | tf_op jit(solution)/shard_map/ppermute | solution.py:55
  165.9 5.0 %collective-permute-start.25 = (f32[4096]{0:T(1024)S(1)}, f32[4096]{0:T(1024)S(1)}, u32[]{:S(2)}, u32[]{:S(2)}) collective-permute-start(f32[4096]{0:T(1024)S(1)} %dynamic_slice.107), channel_id=1, source_target_pairs={{0,24},{4,28},{8,16},{12,20},{16,8},{20,12},{24,0},{28,4},{32,56},... | collective-permute-start | bytes 49160 | tf_op jit(solution)/shard_map/ppermute | solution.py:55
  174.6 4.8 %collective-permute-start.27 = (f32[1024]{0:T(1024)S(1)}, f32[1024]{0:T(1024)S(1)}, u32[]{:S(2)}, u32[]{:S(2)}) collective-permute-start(f32[1024]{0:T(1024)S(1)} %dynamic_slice.111), channel_id=1, source_target_pairs={{0,96},{4,100},{8,104},{12,108},{16,112},{20,116},{24,120},{28,124... | collective-permute-start | bytes 12296 | tf_op jit(solution)/shard_map/ppermute | solution.py:55
  179.4 4.8 %collective-permute-start.28 = (f32[1024]{0:T(1024)S(1)}, f32[1024]{0:T(1024)S(1)}, u32[]{:S(2)}, u32[]{:S(2)}) collective-permute-start(f32[1024]{0:T(1024)S(1)} %dynamic-slice_add_fusion.12), channel_id=1, source_target_pairs={{0,96},{4,100},{8,104},{12,108},{16,112},{20,116},{24,120},{28,124... | collective-permute-start | bytes 12296 | tf_op jit(solution)/shard_map/ppermute | solution.py:62
  188.4 5.0 %collective-permute-start.30 = (f32[4096]{0:T(1024)S(1)}, f32[4096]{0:T(1024)S(1)}, u32[]{:S(2)}, u32[]{:S(2)}) collective-permute-start(f32[4096]{0:T(1024)S(1)} %pad_maximum_fusion.9), channel_id=1, source_target_pairs={{0,24},{4,28},{8,16},{12,20},{16,8},{20,12},{24,0},{28,4},{32,56},... | collective-permute-start | bytes 49160 | tf_op jit(solution)/shard_map/ppermute | solution.py:62
  197.5 5.6 %collective-permute-start.32 = (f32[16384]{0:T(1024)S(1)}, f32[16384]{0:T(1024)S(1)}, u32[]{:S(2)}, u32[]{:S(2)}) collective-permute-start(f32[16384]{0:T(1024)S(1)} %pad_maximum_fusion.5), channel_id=1, source_target_pairs={{0,3},{1,2},{2,1},{3,0},{4,7},{5,6},{6,5},{7,4},{8,11},{9,10},{10,... | collective-permute-start | bytes 196616 | tf_op jit(solution)/shard_map/ppermute | solution.py:62
  203.1 5.0 %collective-permute-start.33 = (f32[32768]{0:T(1024)S(1)}, f32[32768]{0:T(1024)S(1)}, u32[]{:S(2)}, u32[]{:S(2)}) collective-permute-start(f32[32768]{0:T(1024)S(1)} %pad_maximum_fusion.3), channel_id=1, source_target_pairs={{0,1},{1,0},{2,3},{3,2},{4,5},{5,4},{6,7},{7,6},{8,9},{9,8},{10,11... | collective-permute-start | bytes 393224 | tf_op jit(solution)/shard_map/ppermute | solution.py:62
  232.1 5.6 %collective-permute-start.36 = (f32[2,32,512]{2,1,0:T(8,128)S(1)}, f32[2,32,512]{2,1,0:T(8,128)S(1)}, u32[]{:S(2)}, u32[]{:S(2)}) collective-permute-start(f32[2,32,512]{2,1,0:T(8,128)S(1)} %add.251), channel_id=1, source_target_pairs={{0,1},{1,0},{2,3},{3,2},{4,5},{5,4},{6,7},{7,6},{8,9},{9,8},{10,11... | collective-permute-start | bytes 393224 | tf_op jit(solution)/shard_map/ppermute | solution.py:44
  237.7 6.3 %collective-permute-start.37 = (f32[2,32,512]{2,1,0:T(8,128)S(1)}, f32[2,32,512]{2,1,0:T(8,128)S(1)}, u32[]{:S(2)}, u32[]{:S(2)}) collective-permute-start(f32[2,32,512]{2,1,0:T(8,128)S(1)} %add.252), channel_id=1, source_target_pairs={{0,3},{1,2},{2,1},{3,0},{4,7},{5,6},{6,5},{7,4},{8,11},{9,10},{10,... | collective-permute-start | bytes 393224 | tf_op jit(solution)/shard_map/ppermute | solution.py:44
  244.0 5.0 %collective-permute-start.38 = (f32[2,32,512]{2,1,0:T(8,128)S(1)}, f32[2,32,512]{2,1,0:T(8,128)S(1)}, u32[]{:S(2)}, u32[]{:S(2)}) collective-permute-start(f32[2,32,512]{2,1,0:T(8,128)S(1)} %add.253), channel_id=1, source_target_pairs={{0,8},{4,12},{8,0},{12,4},{16,24},{20,28},{24,16},{28,20},{32,40},... | collective-permute-start | bytes 393224 | tf_op jit(solution)/shard_map/ppermute | solution.py:44
  249.1 6.3 %collective-permute-start.39 = (f32[2,32,512]{2,1,0:T(8,128)S(1)}, f32[2,32,512]{2,1,0:T(8,128)S(1)}, u32[]{:S(2)}, u32[]{:S(2)}) collective-permute-start(f32[2,32,512]{2,1,0:T(8,128)S(1)} %add.254), channel_id=1, source_target_pairs={{0,24},{4,28},{8,16},{12,20},{16,8},{20,12},{24,0},{28,4},{32,56},... | collective-permute-start | bytes 393224 | tf_op jit(solution)/shard_map/ppermute | solution.py:44
  255.3 5.0 %collective-permute-start.40 = (f32[2,32,512]{2,1,0:T(8,128)S(1)}, f32[2,32,512]{2,1,0:T(8,128)S(1)}, u32[]{:S(2)}, u32[]{:S(2)}) collective-permute-start(f32[2,32,512]{2,1,0:T(8,128)S(1)} %add.255), channel_id=1, source_target_pairs={{0,32},{4,36},{8,40},{12,44},{16,48},{20,52},{24,56},{28,60},{32,0... | collective-permute-start | bytes 393224 | tf_op jit(solution)/shard_map/ppermute | solution.py:44
  260.4 6.4 %collective-permute-start.41 = (f32[2,32,512]{2,1,0:T(8,128)S(1)}, f32[2,32,512]{2,1,0:T(8,128)S(1)}, u32[]{:S(2)}, u32[]{:S(2)}) collective-permute-start(f32[2,32,512]{2,1,0:T(8,128)S(1)} %add.256), channel_id=1, source_target_pairs={{0,96},{4,100},{8,104},{12,108},{16,112},{20,116},{24,120},{28,124... | collective-permute-start | bytes 393224 | tf_op jit(solution)/shard_map/ppermute | solution.py:44
  290.5 5.0 %collective-permute-start.44 = (f32[2,2048]{1,0:T(2,128)S(1)}, f32[2,2048]{1,0:T(2,128)S(1)}, u32[]{:S(2)}, u32[]{:S(2)}) collective-permute-start(f32[2,2048]{1,0:T(2,128)S(1)} %add.265), channel_id=1, source_target_pairs={{0,3},{1,2},{2,1},{3,0},{4,7},{5,6},{6,5},{7,4},{8,11},{9,10},{10,... | collective-permute-start | bytes 49160 | tf_op jit(solution)/shard_map/ppermute | solution.py:57
  299.4 5.1 %collective-permute-start.46 = (f32[2,2048]{1,0:T(2,128)S(1)}, f32[2,2048]{1,0:T(2,128)S(1)}, u32[]{:S(2)}, u32[]{:S(2)}) collective-permute-start(f32[2,2048]{1,0:T(2,128)S(1)} %add.267), channel_id=1, source_target_pairs={{0,24},{4,28},{8,16},{12,20},{16,8},{20,12},{24,0},{28,4},{32,56},... | collective-permute-start | bytes 49160 | tf_op jit(solution)/shard_map/ppermute | solution.py:57
  308.3 5.0 %collective-permute-start.48 = (f32[2,2048]{1,0:T(2,128)S(1)}, f32[2,2048]{1,0:T(2,128)S(1)}, u32[]{:S(2)}, u32[]{:S(2)}) collective-permute-start(f32[2,2048]{1,0:T(2,128)S(1)} %add.269), channel_id=1, source_target_pairs={{0,96},{4,100},{8,104},{12,108},{16,112},{20,116},{24,120},{28,124... | collective-permute-start | bytes 49160 | tf_op jit(solution)/shard_map/ppermute | solution.py:57
  (27 other events, 360.4 us)
Sparse Core Ops, SparseCore 0:
  285.5 70.7 all-gather.2

commit v2 on v0

v2 whole, which is shorter than its diff:
```python
import jax
import jax.numpy as jnp
from jax import lax
from jax.sharding import PartitionSpec as P

momentum_decay = 0.9
step_rate = 0.5
HI = lax.Precision.HIGHEST


def radix4_rounds(dp_size, group_size):
    z_size = 4
    y_size = dp_size // (2 * z_size)

    def dp_of(y, z, c):
        return (y * z_size + z) * 2 + c

    rounds = [[("dp", [(i, i ^ 1) for i in range(dp_size)])]]
    rounds.append([("group", [(i, i ^ s) for i in range(group_size)]) for s in (1, 2, 3)])
    for along_z in (True, False):
        parts = []
        for s in (1, 2, 3):
            perm = []
            for y in range(y_size):
                for z in range(z_size):
                    for c in range(2):
                        dst = dp_of(y, z ^ s, c) if along_z else dp_of(y ^ s, z, c)
                        perm.append((dp_of(y, z, c), dst))
            parts.append(("dp", perm))
        rounds.append(parts)
    return rounds


def sum_radix4(x, rounds):
    for parts in rounds:
        if len(parts) == 1:
            x = x + lax.ppermute(x, parts[0][0], parts[0][1])
        else:
            r1, r2, r3 = [lax.ppermute(x, axis, perm) for axis, perm in parts]
            x = (x + r1) + (r2 + r3)
    return x


def sum_all_to_all(x, count):
    axes = ("dp", "group")
    rows = lax.all_to_all(x.reshape(count, -1), axes, 0, 0, tiled=False)
    mine = jnp.sum(rows, axis=0)
    spread = jnp.broadcast_to(mine[None], (count,) + mine.shape)
    return lax.all_to_all(spread, axes, 0, 0, tiled=False).reshape(-1)


def orth_t(ft):
    gram = jnp.einsum("mrd,msd->mrs", ft, ft, precision=HI)
    lower_factor = jnp.linalg.cholesky(gram)
    return jax.scipy.linalg.solve_triangular(lower_factor, ft, lower=True)


def left_t(merged, right_t):
    return jnp.einsum("mdk,mrk->mrd", merged, right_t, precision=HI)


def right_t_of(merged, left_tr):
    return jnp.einsum("mdk,mrd->mrk", merged, left_tr, precision=HI)


def on_device(
    gradients,
    errors,
    warm_right,
    norm_grads,
    norm_weights,
    norm_moment,
    owners,
    slot_weights,
    slot_moment,
):
    dp_size = lax.axis_size("dp")
    group_size = lax.axis_size("group")
    replicas = dp_size * group_size
    rounds = radix4_rounds(dp_size, group_size)

    old_moment = slot_moment[0]
    carried = slot_weights[0].astype(jnp.float32) - (step_rate * momentum_decay) * old_moment
    every_carried = lax.all_gather(carried[None], ("dp", "group"), axis=0, tiled=True)

    merged = gradients[0].astype(jnp.float32) + errors[0]
    lshape = (merged.shape[0], warm_right.shape[2], merged.shape[1])
    p1 = left_t(merged, jnp.swapaxes(warm_right, 1, 2))
    norm_local = norm_grads[0]
    joined = jnp.concatenate([p1.reshape(-1), norm_local.reshape(-1)])
    joined_sum = sum_all_to_all(joined, replicas)
    p1_sum = joined_sum[: p1.size].reshape(lshape)
    norm_sum = joined_sum[p1.size :].reshape(norm_local.shape)
    left_one = orth_t(p1_sum)
    right_one = sum_radix4(right_t_of(merged, left_one), rounds) / replicas
    p2_sum = sum_all_to_all(left_t(merged, right_one).reshape(-1), replicas)
    left_two = orth_t(p2_sum.reshape(lshape))
    right_two = sum_radix4(right_t_of(merged, left_two), rounds) / replicas
    update = jnp.einsum("mrd,mrk->mdk", left_two, right_two, precision=HI)
    new_errors = (merged - update)[None]
    new_norm_moment = momentum_decay * norm_moment + norm_sum / replicas
    new_norm_weights = norm_weights - step_rate * new_norm_moment
    piece_count = owners.shape[0]
    slot_count = slot_moment.shape[1]
    piece_rows = slot_moment.shape[2]
    features = slot_moment.shape[3]
    positions = jnp.arange(piece_count, dtype=jnp.int32)
    same_owner = owners[:, None] == owners[None, :]
    earlier = positions[:, None] < positions[None, :]
    slot_of = jnp.sum((same_owner & earlier).astype(jnp.int32), axis=0)
    my_index = lax.axis_index(("dp", "group"))
    owned = owners == my_index
    slot_range = jnp.arange(slot_count, dtype=jnp.int32)
    selector = (owned[:, None] & (slot_of[:, None] == slot_range[None, :])).astype(jnp.float32)
    pieces = update.reshape(piece_count, piece_rows, features)
    slot_update = jnp.einsum("js,jrk->srk", selector, pieces, precision=HI)
    used = jnp.sum(selector, axis=0)[:, None, None] > 0.5
    moment_slots = jnp.where(used, momentum_decay * old_moment + slot_update, old_moment)
    chosen = every_carried[owners, slot_of] - step_rate * pieces
    new_weights = chosen.astype(jnp.bfloat16).reshape(2, piece_count * piece_rows // 2, features)
    return (new_errors, moment_slots[None], new_weights, new_norm_weights, new_norm_moment)


def solution(mesh):
    placed = (
        P(("dp", "group"), None, None, None),
        P(("dp", "group"), None, None, None),
        P(),
        P(("dp", "group"), None, None),
        P(),
        P(),
        P(),
        P(("dp", "group"), None, None, None),
        P(("dp", "group"), None, None, None),
    )
    return jax.shard_map(
        on_device,
        mesh=mesh,
        in_specs=placed,
        out_specs=(
            P(("dp", "group"), None, None, None),
            P(("dp", "group"), None, None, None),
            P(),
            P(),
            P(),
        ),
        check_vma=False,
    )
```

time: 774 us -> 285 us (0.37)
  waiting for transfers between devices: 574 us -> 63.5 us
  starting transfers between devices: 0.84 us -> 35.8 us
  blocking collectives: 64.4 us -> 45.4 us
  matrix products: 66 us -> 55.6 us
  other arithmetic: 35.7 us -> 44.3 us
  local copies, waits for them, and re-layouts: 12 us -> 20.1 us
    psum x4 -> x0, waiting for transfers between devices: 574 us -> none  [the longest x1 148 us: stacked_rounds(): lax.psum((times_right(merged, warm_right), norm_local), ('dp', 'group'))]
    psum x1 -> x0, blocking collectives: 64.4 us -> none  [stacked_rounds(): lax.psum((times_right(merged, warm_right), norm_local), ('dp', 'group'))]
    all_to_all x0 -> x2, blocking collectives: none -> 45.4 us  [sum_all_to_all(): rows = lax.all_to_all(x.reshape(count, -1), axes, 0, 0, tiled=False)]
    ppermute x0 -> x20, waiting for transfers between devices: none -> 34 us  [the longest x18 31.7 us: sum_radix4(): r1, r2, r3 = [lax.ppermute(x, axis, perm) for axis, perm in parts]]
    all_to_all x0 -> x2, waiting for transfers between devices: none -> 29.5 us  [sum_all_to_all(): return lax.all_to_all(spread, axes, 0, 0, tiled=False).reshape(-1)]
    ppermute x0 -> x20, starting transfers between devices: none -> 26.1 us  [the longest x18 25.6 us: sum_radix4(): r1, r2, r3 = [lax.ppermute(x, axis, perm) for axis, perm in parts]]
    convert_element_type x0 -> x1, other arithmetic: none -> 16.2 us  [on_device(): chosen.astype(jnp.bfloat16)]
    broadcast_in_dim x1 -> x0, other arithmetic: 12.8 us -> none  [on_device(): new_errors = (merged - update)[None]]
  transfers between devices with their start and end apart: 5 -> 23, of which waited for: 4 -> 16; matrix products, arithmetic and copies ran while one was open for 2% -> 31% of each run, Pallas kernels for 0% -> 0%
where the time goes in v2:
time: 285 us; the launch traced here: 279 us
  waiting for transfers between devices  63.5 us (22%)
  matrix products  55.6 us (20%)
  blocking collectives  45.4 us (16%)
  other arithmetic  44.3 us (16%)
  starting transfers between devices  35.8 us (13%)
  local copies, waits for them, and re-layouts  20.1 us (7%)
  between operations  14.6 us (5%)
    all_to_all x2, blocking collectives, sum_all_to_all(): rows = lax.all_to_all(x.reshape(count, -1), axes, 0, 0, tiled=False)  45.4 us
    ppermute x18, waiting for transfers between devices, sum_radix4(): r1, r2, r3 = [lax.ppermute(x, axis, perm) for axis, perm in parts]  31.7 us
    all_to_all x2, waiting for transfers between devices, sum_all_to_all(): return lax.all_to_all(spread, axes, 0, 0, tiled=False).reshape(-1)  29.5 us
    ppermute x18, starting transfers between devices, sum_radix4(): r1, r2, r3 = [lax.ppermute(x, axis, perm) for axis, perm in parts]  25.6 us
    dot_general x2, matrix products, left_t(): return jnp.einsum('mdk,mrk->mrd', merged, right_t, precision=HI)  20.9 us
    dot_general x2, matrix products, right_t_of(): return jnp.einsum('mdk,mrd->mrk', merged, left_tr, precision=HI)  17.7 us
    convert_element_type x1, other arithmetic, on_device(): chosen.astype(jnp.bfloat16)  16.2 us
    another operation x7, other arithmetic, orth_t(): lower_factor = jnp.linalg.cholesky(gram)  12 us
  transfers between devices with their start and end apart: 23, of which 16 were waited for; matrix products, arithmetic and copies ran while one was open for 31% of the time, Pallas kernels for 0%

profile of v2, /device:TPU:0, one launch (start us, length us, event | category | flops | bytes accessed | tf_op | source)
XLA Modules:
  0.0 279.1 jit_solution(4521712738148130512)
XLA Ops:
  7.2 1.6 multiply_subtract_fusion
  9.6 11.0 %fusion.7 = f32[2,2048,32]{1,2,0:T(8,128)S(1)} fusion(f32[2,512,32]{1,2,0:T(8,128)S(1)} %copy-done, f32[1,2,2048,512]{3,2,1,0:T(8,128)} %param.13, bf16[1,2,2048,512]{3,2,1,0:T(8,128)(2,1)} %param.12), kind=kOutput, calls=%fused_computation.10 | convolution fusion | flops 809500672 | bytes 13238272 | tf_op jit(solution)/shard_map/mdk,mrk->mrd/dot_general | solution.py:59
  21.5 24.9 %all_to_all.32 = f32[128,1,1056]{2,1,0:T(1,128)S(1)} all-to-all(f32[128,1,1056]{2,1,0:T(1,128)S(1)} %all_to_all.26), channel_id=1, replica_groups=mesh['dp'=32,'group'=4] {'dp','group'}, dimensions={0} | all-to-all | bytes 1081344 | tf_op jit(solution)/shard_map/all_to_all | solution.py:46
  47.9 5.0 %all-to-all-start.1 = ((f32[128,1,1056]{2,1,0:T(1,128)}), f32[128,1,1056]{2,1,0:T(1,128)S(1)}, u32[]{:S(2)}, u32[]{:S(2)}) async-start(f32[128,1,1056]{2,1,0:T(1,128)} %broadcast_in_dim.19), calls=%async_computation.1 | async-start | bytes 1179648 | tf_op jit(solution)/shard_map/all_to_all | solution.py:49
  52.9 16.4 %all-to-all-done.1 = f32[128,1,1056]{2,1,0:T(1,128)S(1)} async-done(((f32[128,1,1056]{2,1,0:T(1,128)}), f32[128,1,1056]{2,1,0:T(1,128)S(1)}, u32[]{:S(2)}, u32[]{:S(2)}) %all-to-all-start.1) | async-done | bytes 540704 | tf_op jit(solution)/shard_map/all_to_all | solution.py:49
  72.1 5.9 %custom-call.10 = f32[2,32,32]{2,1,0:T(8,128)S(1)} custom-call(f32[2,32,32]{2,1,0:T(8,128)S(1)} %fusion.38), custom_call_target="Cholesky" | custom-call | tf_op jit(solution)/shard_map/jit(cholesky)/cholesky | solution.py:54
  78.2 4.9 %custom-call.11 = f32[2,1,32,32]{2,3,1,0:T(8,128)S(1)} custom-call(f32[2,1,32,32]{3,2,1,0:T(8,128)S(1)} %select_bitcast_fusion.1), custom_call_target="InvertDiagBlocksLowerTriangular" | custom-call | tf_op jit(solution)/shard_map/jit(_solve_triangular)/vmap()/triangular_solve | solution.py:55
  83.8 9.5 %fusion.5 = f32[2,32,512]{2,1,0:T(8,128)S(1)} fusion(f32[2,32,2048]{2,1,0:T(8,128)S(1)} %fusion.36, f32[1,2,2048,512]{3,2,1,0:T(8,128)} %param.13, bf16[1,2,2048,512]{3,2,1,0:T(8,128)(2,1)} %param.12), kind=kOutput, calls=%fused_computation.8 | convolution fusion | flops 809500672 | bytes 13238272 | tf_op jit(solution)/shard_map/mdk,mrd->mrk/dot_general | solution.py:63
  98.9 6.3 %collective-permute-done.3 = f32[2,32,512]{2,1,0:T(8,128)S(1)} collective-permute-done((f32[2,32,512]{2,1,0:T(8,128)S(1)}, f32[2,32,512]{2,1,0:T(8,128)S(1)}, u32[]{:S(2)}, u32[]{:S(2)}) %collective-permute-start.3) | collective-permute-done | bytes 131104 | tf_op jit(solution)/shard_map/ppermute | solution.py:39
  105.2 3.0 %collective-permute-start.6 = (f32[2,32,512]{2,1,0:T(8,128)S(1)}, f32[2,32,512]{2,1,0:T(8,128)S(1)}, u32[]{:S(2)}, u32[]{:S(2)}) collective-permute-start(f32[2,32,512]{2,1,0:T(8,128)S(1)} %add_add_fusion.3), channel_id=1, source_target_pairs={{0,24},{4,28},{8,16},{12,20},{16,8},{20,12},{24,0},{28,4},{32,56},... | collective-permute-start | bytes 393224 | tf_op jit(solution)/shard_map/ppermute | solution.py:39
  109.4 4.4 %collective-permute-done.6 = f32[2,32,512]{2,1,0:T(8,128)S(1)} collective-permute-done((f32[2,32,512]{2,1,0:T(8,128)S(1)}, f32[2,32,512]{2,1,0:T(8,128)S(1)}, u32[]{:S(2)}, u32[]{:S(2)}) %collective-permute-start.6) | collective-permute-done | bytes 131104 | tf_op jit(solution)/shard_map/ppermute | solution.py:39
  113.8 2.2 collective-permute-done.5
  116.1 2.0 collective-permute-start.9
  119.0 1.7 collective-permute-start.7
  120.7 3.3 %collective-permute-done.9 = f32[2,32,512]{2,1,0:T(8,128)S(1)} collective-permute-done((f32[2,32,512]{2,1,0:T(8,128)S(1)}, f32[2,32,512]{2,1,0:T(8,128)S(1)}, u32[]{:S(2)}, u32[]{:S(2)}) %collective-permute-start.9) | collective-permute-done | bytes 131104 | tf_op jit(solution)/shard_map/ppermute | solution.py:39
  125.0 9.9 %fusion.3 = f32[2,32,2048]{2,1,0:T(8,128)S(1)} fusion(f32[2,32,512]{2,1,0:T(8,128)S(1)} %collective-permute-done.8, f32[2,32,512]{2,1,0:T(8,128)S(1)} %collective-permute-done.9, f32[2,32,512]{2,1,0:T(8,128)S(1)} %add_add_fusion.2, f32[2,32,512]{2,1,0:T(8,128)S(1)} %collective-permute-done.7, f32[1,2,2048,512]{3,2,1,0:T(8,128)} %param.13, ...), kind=kOutput, calls=%fused_computation.6 | convolution fusion | flops 809631744 | bytes 13631488 | tf_op jit(solution)/shard_map/mdk,mrk->mrd/dot_general | solution.py:59
  135.6 20.5 %all_to_all.33 = f32[128,1,1024]{2,1,0:T(1,128)S(1)} all-to-all(f32[128,1,1024]{2,1,0:T(1,128)S(1)} %all_to_all.27), channel_id=1, replica_groups=mesh['dp'=32,'group'=4] {'dp','group'}, dimensions={0} | all-to-all | bytes 1048576 | tf_op jit(solution)/shard_map/all_to_all | solution.py:46
  157.5 4.6 %all-to-all-start.3 = ((f32[128,1,1024]{2,1,0:T(1,128)}), f32[128,1,1024]{2,1,0:T(1,128)S(1)}, u32[]{:S(2)}, u32[]{:S(2)}) async-start(f32[128,1,1024]{2,1,0:T(1,128)} %broadcast_in_dim.20), calls=%async_computation.3 | async-start | bytes 1048576 | tf_op jit(solution)/shard_map/all_to_all | solution.py:49
  162.2 13.1 %all-to-all-done.3 = f32[128,1,1024]{2,1,0:T(1,128)S(1)} async-done(((f32[128,1,1024]{2,1,0:T(1,128)}), f32[128,1,1024]{2,1,0:T(1,128)S(1)}, u32[]{:S(2)}, u32[]{:S(2)}) %all-to-all-start.3) | async-done | bytes 524320 | tf_op jit(solution)/shard_map/all_to_all | solution.py:49
  177.4 5.9 %custom-call.12 = f32[2,32,32]{2,1,0:T(8,128)S(1)} custom-call(f32[2,32,32]{2,1,0:T(8,128)S(1)} %fusion.35), custom_call_target="Cholesky" | custom-call | tf_op jit(solution)/shard_map/jit(cholesky)/cholesky | solution.py:54
  183.5 4.9 %custom-call.13 = f32[2,1,32,32]{2,3,1,0:T(8,128)S(1)} custom-call(f32[2,1,32,32]{3,2,1,0:T(8,128)S(1)} %select_bitcast_fusion), custom_call_target="InvertDiagBlocksLowerTriangular" | custom-call | tf_op jit(solution)/shard_map/jit(_solve_triangular)/vmap()/triangular_solve | solution.py:55
  189.0 8.2 %fusion.1 = f32[2,32,512]{2,1,0:T(8,128)S(1)} fusion(f32[2,32,2048]{2,1,0:T(8,128)S(1)} %fusion.33, f32[1,2,2048,512]{3,2,1,0:T(8,128)} %param.13, bf16[1,2,2048,512]{3,2,1,0:T(8,128)(2,1)} %param.12), kind=kOutput, calls=%fused_computation.4 | convolution fusion | flops 809500672 | bytes 13238272 | tf_op jit(solution)/shard_map/mdk,mrd->mrk/dot_general | solution.py:63
  198.7 1.8 collective-permute-start.13
  203.0 5.6 %collective-permute-done.13 = f32[2,32,512]{2,1,0:T(8,128)S(1)} collective-permute-done((f32[2,32,512]{2,1,0:T(8,128)S(1)}, f32[2,32,512]{2,1,0:T(8,128)S(1)}, u32[]{:S(2)}, u32[]{:S(2)}) %collective-permute-start.13) | collective-permute-done | bytes 131104 | tf_op jit(solution)/shard_map/ppermute | solution.py:39
  210.2 1.9 collective-permute-start.15
  214.0 4.0 %collective-permute-done.16 = f32[2,32,512]{2,1,0:T(8,128)S(1)} collective-permute-done((f32[2,32,512]{2,1,0:T(8,128)S(1)}, f32[2,32,512]{2,1,0:T(8,128)S(1)}, u32[]{:S(2)}, u32[]{:S(2)}) %collective-permute-start.16) | collective-permute-done | bytes 131104 | tf_op jit(solution)/shard_map/ppermute | solution.py:39
  219.8 1.6 collective-permute-start.18
  227.2 6.7 %fusion.21 = f32[2,2048,512]{2,1,0:T(8,128)S(1)} fusion(f32[2,32,2048]{2,1,0:T(8,128)S(1)} %fusion.33, f32[2,32,512]{2,1,0:T(8,128)S(1)} %collective-permute-done.18, f32[2,32,512]{2,1,0:T(8,128)S(1)} %collective-permute-done.19, f32[2,32,512]{2,1,0:T(8,128)S(1)} %add_add_fusion, f32[2,32,512]{2,1,0:T(8,128)S(1)} %collective-permute-done.17), kind=kOutput, calls=%fused_computation.22 | convolution fusion | flops 805437440 | bytes 9437184 | tf_op jit(solution)/shard_map/mrd,mrk->mdk/dot_general | solution.py:99
  233.9 3.4 %copy-done.3 = f32[2,2048,512]{2,1,0:T(8,128)} copy-done((f32[2,2048,512]{2,1,0:T(8,128)}, f32[2,2048,512]{2,1,0:T(8,128)S(1)}, u32[]{:S(2)}) %copy-start.3) | copy-done | bytes 8388632
  237.3 7.7 %fusion.18 = f32[1,2,32,512]{3,1,2,0:T(2,128)S(1)} fusion(f32[128,32,512]{2,1,0:T(8,128)S(1)} %bitcast.75, f32[1,2,32,512]{3,2,1,0:T(8,128)S(1)} %copy-done.4, pred[2]{0:T(512)(128)(4,1)S(1)} %broadcast_compare_fusion, pred[128]{0:T(512)(128)(4,1)S(1)} %broadcast_compare_fusion.1, s32[128]{0:T(128)S(1)} %convert_reduce_fusion), kind=kOutput, calls=%fused_computation.18 | convolution fusion | flops 50430464 | bytes 8651394 | tf_op jit(solution)/shard_map/js,jrk->srk/dot_general | solution.py:116
  245.7 10.1 %gather_fusion = f32[128,32,512]{2,1,0:T(8,128)} fusion(f32[128,2,32,512]{3,2,1,0:T(8,128)} %all-gather.2.cloned.1.call-done, s32[128]{0:T(128)S(1)} %fusion.49), kind=kCustom, calls=%fused_computation | custom fusion | bytes 16778240 | tf_op jit(solution)/shard_map/gather | solution.py:119
  255.8 16.2 %fusion = (bf16[2,2048,512]{2,1,0:T(8,128)(2,1)}, f32[1,2,2048,512]{3,2,1,0:T(8,128)}) fusion(f32[2,2048,512]{2,1,0:T(8,128)} %copy-done.3, f32[1,2,2048,512]{3,2,1,0:T(8,128)} %param.13, bf16[1,2,2048,512]{3,2,1,0:T(8,128)(2,1)} %param.12, f32[2,2048,512]{2,1,0:T(8,128)} %bitcast.76), kind=kLoop, calls=%fused_computation.2 | loop fusion | flops 12582912 | bytes 41943040 | tf_op jit(solution)/shard_map/convert_element_type | solution.py:120
  (91 shorter events, 36.5 us)
Async XLA Ops:
  7.2 2.4 copy-start
  7.2 238.6 %all-gather.2.cloned.1.call-start = ((), (), s32[]{:S(2)}) async-start(), calls=%async_computation.4 | async-start | bytes 16908288 | tf_op jit(solution)/shard_map/all_gather | solution.py:84
  47.9 21.5 %all-to-all-start.1 = ((f32[128,1,1056]{2,1,0:T(1,128)}), f32[128,1,1056]{2,1,0:T(1,128)S(1)}, u32[]{:S(2)}, u32[]{:S(2)}) async-start(f32[128,1,1056]{2,1,0:T(1,128)} %broadcast_in_dim.19), calls=%async_computation.1 | async-start | bytes 1179648 | tf_op jit(solution)/shard_map/all_to_all | solution.py:49
  83.1 41.9 %copy-start.2 = (bf16[1,2,2048,512]{3,2,1,0:T(8,128)(2,1)S(1)}, bf16[1,2,2048,512]{3,2,1,0:T(8,128)(2,1)}, u32[]{:S(2)}) copy-start(bf16[1,2,2048,512]{3,2,1,0:T(8,128)(2,1)} %param.12) | copy-start | bytes 12582916
  93.3 1.4 collective-permute-start
  94.7 10.5 %collective-permute-start.3 = (f32[2,32,512]{2,1,0:T(8,128)S(1)}, f32[2,32,512]{2,1,0:T(8,128)S(1)}, u32[]{:S(2)}, u32[]{:S(2)}) collective-permute-start(f32[2,32,512]{2,1,0:T(8,128)S(1)} %add.105), channel_id=1, source_target_pairs={{0,3},{1,2},{2,1},{3,0},{4,7},{5,6},{6,5},{7,4},{8,11},{9,10},{10,... | collective-permute-start | bytes 393224 | tf_op jit(solution)/shard_map/ppermute | solution.py:39
  96.2 9.0 %collective-permute-start.2 = (f32[2,32,512]{2,1,0:T(8,128)S(1)}, f32[2,32,512]{2,1,0:T(8,128)S(1)}, u32[]{:S(2)}, u32[]{:S(2)}) collective-permute-start(f32[2,32,512]{2,1,0:T(8,128)S(1)} %add.105), channel_id=1, source_target_pairs={{0,2},{1,3},{2,0},{3,1},{4,6},{5,7},{6,4},{7,5},{8,10},{9,11},{10,... | collective-permute-start | bytes 393224 | tf_op jit(solution)/shard_map/ppermute | solution.py:39
  97.4 7.7 %collective-permute-start.1 = (f32[2,32,512]{2,1,0:T(8,128)S(1)}, f32[2,32,512]{2,1,0:T(8,128)S(1)}, u32[]{:S(2)}, u32[]{:S(2)}) collective-permute-start(f32[2,32,512]{2,1,0:T(8,128)S(1)} %add.105), channel_id=1, source_target_pairs={{0,1},{1,0},{2,3},{3,2},{4,5},{5,4},{6,7},{7,6},{8,9},{9,8},{10,11... | collective-permute-start | bytes 393224 | tf_op jit(solution)/shard_map/ppermute | solution.py:39
  105.2 8.6 %collective-permute-start.6 = (f32[2,32,512]{2,1,0:T(8,128)S(1)}, f32[2,32,512]{2,1,0:T(8,128)S(1)}, u32[]{:S(2)}, u32[]{:S(2)}) collective-permute-start(f32[2,32,512]{2,1,0:T(8,128)S(1)} %add_add_fusion.3), channel_id=1, source_target_pairs={{0,24},{4,28},{8,16},{12,20},{16,8},{20,12},{24,0},{28,4},{32,56},... | collective-permute-start | bytes 393224 | tf_op jit(solution)/shard_map/ppermute | solution.py:39
  108.2 7.9 %collective-permute-start.5 = (f32[2,32,512]{2,1,0:T(8,128)S(1)}, f32[2,32,512]{2,1,0:T(8,128)S(1)}, u32[]{:S(2)}, u32[]{:S(2)}) collective-permute-start(f32[2,32,512]{2,1,0:T(8,128)S(1)} %add_add_fusion.3), channel_id=1, source_target_pairs={{0,16},{4,20},{8,24},{12,28},{16,0},{20,4},{24,8},{28,12},{32,48},... | collective-permute-start | bytes 393224 | tf_op jit(solution)/shard_map/ppermute | solution.py:39
  108.8 7.2 %collective-permute-start.4 = (f32[2,32,512]{2,1,0:T(8,128)S(1)}, f32[2,32,512]{2,1,0:T(8,128)S(1)}, u32[]{:S(2)}, u32[]{:S(2)}) collective-permute-start(f32[2,32,512]{2,1,0:T(8,128)S(1)} %add_add_fusion.3), channel_id=1, source_target_pairs={{0,8},{4,12},{8,0},{12,4},{16,24},{20,28},{24,16},{28,20},{32,40},... | collective-permute-start | bytes 393224 | tf_op jit(solution)/shard_map/ppermute | solution.py:39
  116.1 46.0 %copy-start.7 = (s32[128]{0:T(128)S(1)}, s32[128]{0:T(128)}, u32[]{:S(2)}) copy-start(s32[128]{0:T(128)} %param.18) | copy-start | bytes 1540
  116.1 7.9 %collective-permute-start.9 = (f32[2,32,512]{2,1,0:T(8,128)S(1)}, f32[2,32,512]{2,1,0:T(8,128)S(1)}, u32[]{:S(2)}, u32[]{:S(2)}) collective-permute-start(f32[2,32,512]{2,1,0:T(8,128)S(1)} %add_add_fusion.2), channel_id=1, source_target_pairs={{0,96},{4,100},{8,104},{12,108},{16,112},{20,116},{24,120},{28,124... | collective-permute-start | bytes 393224 | tf_op jit(solution)/shard_map/ppermute | solution.py:39
  118.1 6.9 %collective-permute-start.8 = (f32[2,32,512]{2,1,0:T(8,128)S(1)}, f32[2,32,512]{2,1,0:T(8,128)S(1)}, u32[]{:S(2)}, u32[]{:S(2)}) collective-permute-start(f32[2,32,512]{2,1,0:T(8,128)S(1)} %add_add_fusion.2), channel_id=1, source_target_pairs={{0,64},{4,68},{8,72},{12,76},{16,80},{20,84},{24,88},{28,92},{32,9... | collective-permute-start | bytes 393224 | tf_op jit(solution)/shard_map/ppermute | solution.py:39
  119.0 6.0 %collective-permute-start.7 = (f32[2,32,512]{2,1,0:T(8,128)S(1)}, f32[2,32,512]{2,1,0:T(8,128)S(1)}, u32[]{:S(2)}, u32[]{:S(2)}) collective-permute-start(f32[2,32,512]{2,1,0:T(8,128)S(1)} %add_add_fusion.2), channel_id=1, source_target_pairs={{0,32},{4,36},{8,40},{12,44},{16,48},{20,52},{24,56},{28,60},{32,0... | collective-permute-start | bytes 393224 | tf_op jit(solution)/shard_map/ppermute | solution.py:39
  157.5 17.8 %all-to-all-start.3 = ((f32[128,1,1024]{2,1,0:T(1,128)}), f32[128,1,1024]{2,1,0:T(1,128)S(1)}, u32[]{:S(2)}, u32[]{:S(2)}) async-start(f32[128,1,1024]{2,1,0:T(1,128)} %broadcast_in_dim.20), calls=%async_computation.3 | async-start | bytes 1048576 | tf_op jit(solution)/shard_map/all_to_all | solution.py:49
  188.4 34.6 %copy-start.5 = (f32[2,2048]{1,0:T(2,128)S(1)}, f32[2,2048]{1,0:T(2,128)}, u32[]{:S(2)}) copy-start(f32[2,2048]{1,0:T(2,128)} %param.16) | copy-start | bytes 49156
  188.4 34.6 %copy-start.6 = (f32[2,2048]{1,0:T(2,128)S(1)}, f32[2,2048]{1,0:T(2,128)}, u32[]{:S(2)}) copy-start(f32[2,2048]{1,0:T(2,128)} %param.17) | copy-start | bytes 49156
  197.3 40.0 %copy-start.4 = (f32[1,2,32,512]{3,2,1,0:T(8,128)S(1)}, f32[1,2,32,512]{3,2,1,0:T(8,128)}, u32[]{:S(2)}) copy-start(f32[1,2,32,512]{3,2,1,0:T(8,128)} %param.20) | copy-start | bytes 393220
  197.3 1.4 collective-permute-start.10
  198.7 9.9 %collective-permute-start.13 = (f32[2,32,512]{2,1,0:T(8,128)S(1)}, f32[2,32,512]{2,1,0:T(8,128)S(1)}, u32[]{:S(2)}, u32[]{:S(2)}) collective-permute-start(f32[2,32,512]{2,1,0:T(8,128)S(1)} %add.115), channel_id=1, source_target_pairs={{0,3},{1,2},{2,1},{3,0},{4,7},{5,6},{6,5},{7,4},{8,11},{9,10},{10,... | collective-permute-start | bytes 393224 | tf_op jit(solution)/shard_map/ppermute | solution.py:39
  200.5 8.1 %collective-permute-start.12 = (f32[2,32,512]{2,1,0:T(8,128)S(1)}, f32[2,32,512]{2,1,0:T(8,128)S(1)}, u32[]{:S(2)}, u32[]{:S(2)}) collective-permute-start(f32[2,32,512]{2,1,0:T(8,128)S(1)} %add.115), channel_id=1, source_target_pairs={{0,2},{1,3},{2,0},{3,1},{4,6},{5,7},{6,4},{7,5},{8,10},{9,11},{10,... | collective-permute-start | bytes 393224 | tf_op jit(solution)/shard_map/ppermute | solution.py:39
  201.5 7.8 %collective-permute-start.11 = (f32[2,32,512]{2,1,0:T(8,128)S(1)}, f32[2,32,512]{2,1,0:T(8,128)S(1)}, u32[]{:S(2)}, u32[]{:S(2)}) collective-permute-start(f32[2,32,512]{2,1,0:T(8,128)S(1)} %add.115), channel_id=1, source_target_pairs={{0,1},{1,0},{2,3},{3,2},{4,5},{5,4},{6,7},{7,6},{8,9},{9,8},{10,11... | collective-permute-start | bytes 393224 | tf_op jit(solution)/shard_map/ppermute | solution.py:39
  209.3 8.7 %collective-permute-start.16 = (f32[2,32,512]{2,1,0:T(8,128)S(1)}, f32[2,32,512]{2,1,0:T(8,128)S(1)}, u32[]{:S(2)}, u32[]{:S(2)}) collective-permute-start(f32[2,32,512]{2,1,0:T(8,128)S(1)} %add_add_fusion.1), channel_id=1, source_target_pairs={{0,24},{4,28},{8,16},{12,20},{16,8},{20,12},{24,0},{28,4},{32,56},... | collective-permute-start | bytes 393224 | tf_op jit(solution)/shard_map/ppermute | solution.py:39
  210.2 7.8 %collective-permute-start.15 = (f32[2,32,512]{2,1,0:T(8,128)S(1)}, f32[2,32,512]{2,1,0:T(8,128)S(1)}, u32[]{:S(2)}, u32[]{:S(2)}) collective-permute-start(f32[2,32,512]{2,1,0:T(8,128)S(1)} %add_add_fusion.1), channel_id=1, source_target_pairs={{0,16},{4,20},{8,24},{12,28},{16,0},{20,4},{24,8},{28,12},{32,48},... | collective-permute-start | bytes 393224 | tf_op jit(solution)/shard_map/ppermute | solution.py:39
  212.0 6.6 %collective-permute-start.14 = (f32[2,32,512]{2,1,0:T(8,128)S(1)}, f32[2,32,512]{2,1,0:T(8,128)S(1)}, u32[]{:S(2)}, u32[]{:S(2)}) collective-permute-start(f32[2,32,512]{2,1,0:T(8,128)S(1)} %add_add_fusion.1), channel_id=1, source_target_pairs={{0,8},{4,12},{8,0},{12,4},{16,24},{20,28},{24,16},{28,20},{32,40},... | collective-permute-start | bytes 393224 | tf_op jit(solution)/shard_map/ppermute | solution.py:39
  218.7 6.3 %collective-permute-start.19 = (f32[2,32,512]{2,1,0:T(8,128)S(1)}, f32[2,32,512]{2,1,0:T(8,128)S(1)}, u32[]{:S(2)}, u32[]{:S(2)}) collective-permute-start(f32[2,32,512]{2,1,0:T(8,128)S(1)} %add_add_fusion), channel_id=1, source_target_pairs={{0,96},{4,100},{8,104},{12,108},{16,112},{20,116},{24,120},{28,124... | collective-permute-start | bytes 393224 | tf_op jit(solution)/shard_map/ppermute | solution.py:39
  219.8 6.5 %collective-permute-start.18 = (f32[2,32,512]{2,1,0:T(8,128)S(1)}, f32[2,32,512]{2,1,0:T(8,128)S(1)}, u32[]{:S(2)}, u32[]{:S(2)}) collective-permute-start(f32[2,32,512]{2,1,0:T(8,128)S(1)} %add_add_fusion), channel_id=1, source_target_pairs={{0,64},{4,68},{8,72},{12,76},{16,80},{20,84},{24,88},{28,92},{32,9... | collective-permute-start | bytes 393224 | tf_op jit(solution)/shard_map/ppermute | solution.py:39
  221.4 5.7 %collective-permute-start.17 = (f32[2,32,512]{2,1,0:T(8,128)S(1)}, f32[2,32,512]{2,1,0:T(8,128)S(1)}, u32[]{:S(2)}, u32[]{:S(2)}) collective-permute-start(f32[2,32,512]{2,1,0:T(8,128)S(1)} %add_add_fusion), channel_id=1, source_target_pairs={{0,32},{4,36},{8,40},{12,44},{16,48},{20,52},{24,56},{28,60},{32,0... | collective-permute-start | bytes 393224 | tf_op jit(solution)/shard_map/ppermute | solution.py:39
  233.9 3.4 %copy-start.3 = (f32[2,2048,512]{2,1,0:T(8,128)}, f32[2,2048,512]{2,1,0:T(8,128)S(1)}, u32[]{:S(2)}) copy-start(f32[2,2048,512]{2,1,0:T(8,128)S(1)} %fusion.21) | copy-start | bytes 25165828
  255.8 16.2 %copy-start.1 = (f32[2,512,32]{1,2,0:T(8,128)S(1)}, f32[2,512,32]{1,2,0:T(8,128)}, u32[]{:S(2)}) copy-start(f32[2,512,32]{1,2,0:T(8,128)} %param.14) | copy-start | bytes 393220
Sparse Core Ops, SparseCore 0:
  11.1 91.0 all-gather.1

commit v3 on v2

--- a/solution.py
+++ b/solution.py
@@ -6,6 +6,7 @@
 momentum_decay = 0.9
 step_rate = 0.5
 HI = lax.Precision.HIGHEST
+MID = lax.Precision.HIGH
 
 
 def radix4_rounds(dp_size, group_size):
@@ -56,11 +57,11 @@
 
 
 def left_t(merged, right_t):
-    return jnp.einsum("mdk,mrk->mrd", merged, right_t, precision=HI)
+    return jnp.einsum("mdk,mrk->mrd", merged, right_t, precision=MID)
 
 
 def right_t_of(merged, left_tr):
-    return jnp.einsum("mdk,mrd->mrk", merged, left_tr, precision=HI)
+    return jnp.einsum("mdk,mrd->mrk", merged, left_tr, precision=MID)
 
 
 def on_device(
@@ -96,7 +97,7 @@
     p2_sum = sum_all_to_all(left_t(merged, right_one).reshape(-1), replicas)
     left_two = orth_t(p2_sum.reshape(lshape))
     right_two = sum_radix4(right_t_of(merged, left_two), rounds) / replicas
-    update = jnp.einsum("mrd,mrk->mdk", left_two, right_two, precision=HI)
+    update = jnp.einsum("mrd,mrk->mdk", left_two, right_two, precision=MID)
     new_errors = (merged - update)[None]
     new_norm_moment = momentum_decay * norm_moment + norm_sum / replicas
     new_norm_weights = norm_weights - step_rate * new_norm_moment
@@ -110,12 +111,20 @@
     slot_of = jnp.sum((same_owner & earlier).astype(jnp.int32), axis=0)
     my_index = lax.axis_index(("dp", "group"))
     owned = owners == my_index
-    slot_range = jnp.arange(slot_count, dtype=jnp.int32)
-    selector = (owned[:, None] & (slot_of[:, None] == slot_range[None, :])).astype(jnp.float32)
+    pieces_per_matrix = piece_count // merged.shape[0]
+    moment_list = []
+    for s in range(slot_count):
+        hit = owned & (slot_of == s)
+        piece = jnp.sum(jnp.where(hit, positions, 0))
+        matrix = piece // pieces_per_matrix
+        row0 = (piece % pieces_per_matrix) * piece_rows
+        rows_l = lax.dynamic_slice(left_two, (matrix, 0, row0), (1, left_two.shape[1], piece_rows))[0]
+        rows_r = lax.dynamic_index_in_dim(right_two, matrix, 0, keepdims=False)
+        piece_update = jnp.einsum("rd,rk->dk", rows_l, rows_r, precision=MID)
+        fresh = momentum_decay * old_moment[s] + piece_update
+        moment_list.append(jnp.where(jnp.any(hit), fresh, old_moment[s]))
+    moment_slots = jnp.stack(moment_list)
     pieces = update.reshape(piece_count, piece_rows, features)
-    slot_update = jnp.einsum("js,jrk->srk", selector, pieces, precision=HI)
-    used = jnp.sum(selector, axis=0)[:, None, None] > 0.5
-    moment_slots = jnp.where(used, momentum_decay * old_moment + slot_update, old_moment)
     chosen = every_carried[owners, slot_of] - step_rate * pieces
     new_weights = chosen.astype(jnp.bfloat16).reshape(2, piece_count * piece_rows // 2, features)
     return (new_errors, moment_slots[None], new_weights, new_norm_weights, new_norm_moment)

time: 285 us -> 264 us (0.926); the launches traced: 279 us -> 263 us
  blocking collectives: 45.4 us -> 64 us
  waiting for transfers between devices: 63.5 us -> 46.4 us
  matrix products: 55.6 us -> 41.5 us
  starting transfers between devices: 35.8 us -> 30.5 us
  between operations: 14.6 us -> 19.6 us
  local copies, waits for them, and re-layouts: 20.1 us -> 15.2 us
    all_to_all x0 -> x1, blocking collectives: none -> 17.5 us  [sum_all_to_all(): return lax.all_to_all(spread, axes, 0, 0, tiled=False).reshape(-1)]
    dot_general x6 -> x7, matrix products: 53.1 us -> 39 us  [the longest x2 15.7 us: right_t_of(): return jnp.einsum('mdk,mrd->mrk', merged, left_tr, precision=MID)]
    all_to_all x2 -> x1, waiting for transfers between devices: 29.5 us -> 17.3 us  [sum_all_to_all(): return lax.all_to_all(spread, axes, 0, 0, tiled=False).reshape(-1)]
    ppermute x18, waiting for transfers between devices: 31.7 us -> 26.7 us  [sum_radix4(): r1, r2, r3 = [lax.ppermute(x, axis, perm) for axis, perm in parts]]
    all_to_all x2 -> x1, starting transfers between devices: 9.62 us -> 4.8 us  [sum_all_to_all(): return lax.all_to_all(spread, axes, 0, 0, tiled=False).reshape(-1)]
    unnamed x19 -> x16, local copies, waits for them, and re-layouts: 4.93 us -> 0.86 us
  transfers between devices with their start and end apart: 23 -> 22, of which waited for: 16 -> 13; matrix products, arithmetic and copies ran while one was open for 31% -> 28% of each run, Pallas kernels for 0% -> 0%
where the time goes in v3:
time: 264 us; the launch traced here: 263 us
  blocking collectives  64 us (24%)
  waiting for transfers between devices  46.4 us (18%)
  other arithmetic  46.1 us (17%)
  matrix products  41.5 us (16%)
  starting transfers between devices  30.5 us (12%)
  between operations  19.6 us (7%)
  local copies, waits for them, and re-layouts  15.2 us (6%)
    all_to_all x2, blocking collectives, sum_all_to_all(): rows = lax.all_to_all(x.reshape(count, -1), axes, 0, 0, tiled=False)  46.5 us
    ppermute x18, waiting for transfers between devices, sum_radix4(): r1, r2, r3 = [lax.ppermute(x, axis, perm) for axis, perm in parts]  26.7 us
    ppermute x18, starting transfers between devices, sum_radix4(): r1, r2, r3 = [lax.ppermute(x, axis, perm) for axis, perm in parts]  25 us
    all_to_all x1, blocking collectives, sum_all_to_all(): return lax.all_to_all(spread, axes, 0, 0, tiled=False).reshape(-1)  17.5 us
    all_to_all x1, waiting for transfers between devices, sum_all_to_all(): return lax.all_to_all(spread, axes, 0, 0, tiled=False).reshape(-1)  17.3 us
    convert_element_type x1, other arithmetic, on_device(): chosen.astype(jnp.bfloat16)  16.2 us
    dot_general x2, matrix products, right_t_of(): return jnp.einsum('mdk,mrd->mrk', merged, left_tr, precision=MID)  15.7 us
    dot_general x2, matrix products, left_t(): return jnp.einsum('mdk,mrk->mrd', merged, right_t, precision=MID)  15.6 us
  transfers between devices with their start and end apart: 22, of which 13 were waited for; matrix products, arithmetic and copies ran while one was open for 28% of the time, Pallas kernels for 0%

profile of v3, /device:TPU:0, one launch (start us, length us, event | category | flops | bytes accessed | tf_op | source)
XLA Modules:
  0.0 263.3 jit_solution(13099169567397334155)
XLA Ops:
  7.2 1.6 multiply_subtract_fusion
  9.6 8.4 %fusion.7 = f32[2,2048,32]{1,2,0:T(8,128)S(1)} fusion(f32[2,512,32]{1,2,0:T(8,128)S(1)} %copy-done, f32[1,2,2048,512]{3,2,1,0:T(8,128)} %param.13, bf16[1,2,2048,512]{3,2,1,0:T(8,128)(2,1)} %param.12), kind=kOutput, calls=%fused_computation.10 | convolution fusion | flops 406847488 | bytes 13238272 | tf_op jit(solution)/shard_map/mdk,mrk->mrd/dot_general | solution.py:60
  18.9 25.3 %all_to_all.32 = f32[128,1,1056]{2,1,0:T(1,128)S(1)} all-to-all(f32[128,1,1056]{2,1,0:T(1,128)S(1)} %all_to_all.26), channel_id=1, replica_groups=mesh['dp'=32,'group'=4] {'dp','group'}, dimensions={0} | all-to-all | bytes 1081344 | tf_op jit(solution)/shard_map/all_to_all | solution.py:47
  45.8 4.8 %all-to-all-start.1 = ((f32[128,1,1056]{2,1,0:T(1,128)}), f32[128,1,1056]{2,1,0:T(1,128)S(1)}, u32[]{:S(2)}, u32[]{:S(2)}) async-start(f32[128,1,1056]{2,1,0:T(1,128)} %broadcast_in_dim.16), calls=%async_computation.1 | async-start | bytes 1179648 | tf_op jit(solution)/shard_map/all_to_all | solution.py:50
  50.6 17.3 %all-to-all-done.1 = f32[128,1,1056]{2,1,0:T(1,128)S(1)} async-done(((f32[128,1,1056]{2,1,0:T(1,128)}), f32[128,1,1056]{2,1,0:T(1,128)S(1)}, u32[]{:S(2)}, u32[]{:S(2)}) %all-to-all-start.1) | async-done | bytes 540704 | tf_op jit(solution)/shard_map/all_to_all | solution.py:50
  70.6 5.9 %custom-call.10 = f32[2,32,32]{2,1,0:T(8,128)S(1)} custom-call(f32[2,32,32]{2,1,0:T(8,128)S(1)} %fusion.29), custom_call_target="Cholesky" | custom-call | tf_op jit(solution)/shard_map/jit(cholesky)/cholesky | solution.py:55
  76.7 4.9 %custom-call.11 = f32[2,1,32,32]{2,3,1,0:T(8,128)S(1)} custom-call(f32[2,1,32,32]{3,2,1,0:T(8,128)S(1)} %select_bitcast_fusion.1), custom_call_target="InvertDiagBlocksLowerTriangular" | custom-call | tf_op jit(solution)/shard_map/jit(_solve_triangular)/vmap()/triangular_solve | solution.py:56
  82.3 8.5 %fusion.5 = f32[2,32,512]{2,1,0:T(8,128)S(1)} fusion(f32[2,32,2048]{2,1,0:T(8,128)S(1)} %fusion.27, f32[1,2,2048,512]{3,2,1,0:T(8,128)} %param.13, bf16[1,2,2048,512]{3,2,1,0:T(8,128)(2,1)} %param.12), kind=kOutput, calls=%fused_computation.8 | convolution fusion | flops 406847488 | bytes 13238272 | tf_op jit(solution)/shard_map/mdk,mrd->mrk/dot_general | solution.py:64
  91.0 1.4 collective-permute-done
  94.8 1.8 collective-permute-start.1
  96.7 7.4 %collective-permute-done.3 = f32[2,32,512]{2,1,0:T(8,128)S(1)} collective-permute-done((f32[2,32,512]{2,1,0:T(8,128)S(1)}, f32[2,32,512]{2,1,0:T(8,128)S(1)}, u32[]{:S(2)}, u32[]{:S(2)}) %collective-permute-start.3) | collective-permute-done | bytes 131104 | tf_op jit(solution)/shard_map/ppermute | solution.py:40
  104.1 1.9 collective-permute-start.6
  106.0 1.8 collective-permute-start.5
  108.2 4.8 %collective-permute-done.6 = f32[2,32,512]{2,1,0:T(8,128)S(1)} collective-permute-done((f32[2,32,512]{2,1,0:T(8,128)S(1)}, f32[2,32,512]{2,1,0:T(8,128)S(1)}, u32[]{:S(2)}, u32[]{:S(2)}) %collective-permute-start.6) | collective-permute-done | bytes 131104 | tf_op jit(solution)/shard_map/ppermute | solution.py:40
  114.1 2.6 collective-permute-start.9
  118.3 3.1 %collective-permute-done.9 = f32[2,32,512]{2,1,0:T(8,128)S(1)} collective-permute-done((f32[2,32,512]{2,1,0:T(8,128)S(1)}, f32[2,32,512]{2,1,0:T(8,128)S(1)}, u32[]{:S(2)}, u32[]{:S(2)}) %collective-permute-start.9) | collective-permute-done | bytes 131104 | tf_op jit(solution)/shard_map/ppermute | solution.py:40
  121.4 1.8 collective-permute-done.8
  123.2 7.2 %fusion.3 = f32[2,32,2048]{2,1,0:T(8,128)S(1)} fusion(f32[2,32,512]{2,1,0:T(8,128)S(1)} %collective-permute-done.8, f32[2,32,512]{2,1,0:T(8,128)S(1)} %collective-permute-done.9, f32[2,32,512]{2,1,0:T(8,128)S(1)} %add_add_fusion.2, f32[2,32,512]{2,1,0:T(8,128)S(1)} %collective-permute-done.7, f32[1,2,2048,512]{3,2,1,0:T(8,128)} %param.13, ...), kind=kOutput, calls=%fused_computation.6 | convolution fusion | flops 406978560 | bytes 13631488 | tf_op jit(solution)/shard_map/mdk,mrk->mrd/dot_general | solution.py:60
  131.0 21.2 %all_to_all.33 = f32[128,1,1024]{2,1,0:T(1,128)S(1)} all-to-all(f32[128,1,1024]{2,1,0:T(1,128)S(1)} %all_to_all.27), channel_id=1, replica_groups=mesh['dp'=32,'group'=4] {'dp','group'}, dimensions={0} | all-to-all | bytes 1048576 | tf_op jit(solution)/shard_map/all_to_all | solution.py:47
  152.8 17.5 %all_to_all.34 = f32[128,1,1024]{2,1,0:T(1,128)S(1)} all-to-all(f32[128,1,1024]{2,1,0:T(1,128)S(1)} %broadcast_in_dim.17), channel_id=1, replica_groups=mesh['dp'=32,'group'=4] {'dp','group'}, dimensions={0} | all-to-all | bytes 1048576 | tf_op jit(solution)/shard_map/all_to_all | solution.py:50
  172.5 5.9 %custom-call.12 = f32[2,32,32]{2,1,0:T(8,128)S(1)} custom-call(f32[2,32,32]{2,1,0:T(8,128)S(1)} %fusion.26), custom_call_target="Cholesky" | custom-call | tf_op jit(solution)/shard_map/jit(cholesky)/cholesky | solution.py:55
  178.6 4.9 %custom-call.13 = f32[2,1,32,32]{2,3,1,0:T(8,128)S(1)} custom-call(f32[2,1,32,32]{3,2,1,0:T(8,128)S(1)} %select_bitcast_fusion), custom_call_target="InvertDiagBlocksLowerTriangular" | custom-call | tf_op jit(solution)/shard_map/jit(_solve_triangular)/vmap()/triangular_solve | solution.py:56
  184.2 7.2 %fusion.1 = f32[2,32,512]{2,1,0:T(8,128)S(1)} fusion(f32[2,32,2048]{2,1,0:T(8,128)S(1)} %fusion.24, f32[1,2,2048,512]{3,2,1,0:T(8,128)} %param.13, bf16[1,2,2048,512]{3,2,1,0:T(8,128)(2,1)} %param.12), kind=kOutput, calls=%fused_computation.4 | convolution fusion | flops 406847488 | bytes 13238272 | tf_op jit(solution)/shard_map/mdk,mrd->mrk/dot_general | solution.py:64
  192.9 1.8 collective-permute-start.13
  195.6 1.4 collective-permute-start.11
  204.7 1.9 collective-permute-start.15
  208.3 4.3 %collective-permute-done.16 = f32[2,32,512]{2,1,0:T(8,128)S(1)} collective-permute-done((f32[2,32,512]{2,1,0:T(8,128)S(1)}, f32[2,32,512]{2,1,0:T(8,128)S(1)}, u32[]{:S(2)}, u32[]{:S(2)}) %collective-permute-start.16) | collective-permute-done | bytes 131104 | tf_op jit(solution)/shard_map/ppermute | solution.py:40
  214.5 1.6 collective-permute-start.18
  218.1 3.1 %collective-permute-done.19 = f32[2,32,512]{2,1,0:T(8,128)S(1)} collective-permute-done((f32[2,32,512]{2,1,0:T(8,128)S(1)}, f32[2,32,512]{2,1,0:T(8,128)S(1)}, u32[]{:S(2)}, u32[]{:S(2)}) %collective-permute-start.19) | collective-permute-done | bytes 131104 | tf_op jit(solution)/shard_map/ppermute | solution.py:40
  224.4 5.7 %fusion.50 = f32[2,2048,512]{2,1,0:T(8,128)} fusion(f32[2,32,2048]{2,1,0:T(8,128)S(1)} %fusion.24, f32[2,32,512]{2,1,0:T(8,128)S(1)} %add_multiply_fusion), kind=kOutput, calls=%fused_computation.85 | convolution fusion | flops 402653184 | bytes 9043968 | tf_op jit(solution)/shard_map/mrd,mrk->mdk/dot_general | solution.py:100
  230.2 10.1 %gather_fusion = f32[128,32,512]{2,1,0:T(8,128)} fusion(f32[128,2,32,512]{3,2,1,0:T(8,128)} %all-gather.2.cloned.1.call-done, s32[128]{0:T(128)S(1)} %fusion.43), kind=kCustom, calls=%fused_computation | custom fusion | bytes 16778240 | tf_op jit(solution)/shard_map/gather | solution.py:128
  240.3 16.2 %fusion = (bf16[2,2048,512]{2,1,0:T(8,128)(2,1)}, f32[1,2,2048,512]{3,2,1,0:T(8,128)}) fusion(f32[2,2048,512]{2,1,0:T(8,128)} %fusion.50, f32[1,2,2048,512]{3,2,1,0:T(8,128)} %param.13, bf16[1,2,2048,512]{3,2,1,0:T(8,128)(2,1)} %param.12, f32[2,2048,512]{2,1,0:T(8,128)} %bitcast.93), kind=kLoop, calls=%fused_computation.2 | loop fusion | flops 12582912 | bytes 41943040 | tf_op jit(solution)/shard_map/convert_element_type | solution.py:129
  (89 shorter events, 30.4 us)
Async XLA Ops:
  7.2 2.4 copy-start
  7.2 223.0 %all-gather.2.cloned.1.call-start = ((), (), s32[]{:S(2)}) async-start(), calls=%async_computation.4 | async-start | bytes 16908288 | tf_op jit(solution)/shard_map/all_gather | solution.py:85
  45.8 22.1 %all-to-all-start.1 = ((f32[128,1,1056]{2,1,0:T(1,128)}), f32[128,1,1056]{2,1,0:T(1,128)S(1)}, u32[]{:S(2)}, u32[]{:S(2)}) async-start(f32[128,1,1056]{2,1,0:T(1,128)} %broadcast_in_dim.16), calls=%async_computation.1 | async-start | bytes 1179648 | tf_op jit(solution)/shard_map/all_to_all | solution.py:50
  81.6 41.5 %copy-start.2 = (bf16[1,2,2048,512]{3,2,1,0:T(8,128)(2,1)S(1)}, bf16[1,2,2048,512]{3,2,1,0:T(8,128)(2,1)}, u32[]{:S(2)}) copy-start(bf16[1,2,2048,512]{3,2,1,0:T(8,128)(2,1)} %param.12) | copy-start | bytes 12582916
  90.8 1.6 collective-permute-start
  92.5 11.5 %collective-permute-start.3 = (f32[2,32,512]{2,1,0:T(8,128)S(1)}, f32[2,32,512]{2,1,0:T(8,128)S(1)}, u32[]{:S(2)}, u32[]{:S(2)}) collective-permute-start(f32[2,32,512]{2,1,0:T(8,128)S(1)} %add.132), channel_id=1, source_target_pairs={{0,3},{1,2},{2,1},{3,0},{4,7},{5,6},{6,5},{7,4},{8,11},{9,10},{10,... | collective-permute-start | bytes 393224 | tf_op jit(solution)/shard_map/ppermute | solution.py:40
  93.9 10.1 %collective-permute-start.2 = (f32[2,32,512]{2,1,0:T(8,128)S(1)}, f32[2,32,512]{2,1,0:T(8,128)S(1)}, u32[]{:S(2)}, u32[]{:S(2)}) collective-permute-start(f32[2,32,512]{2,1,0:T(8,128)S(1)} %add.132), channel_id=1, source_target_pairs={{0,2},{1,3},{2,0},{3,1},{4,6},{5,7},{6,4},{7,5},{8,10},{9,11},{10,... | collective-permute-start | bytes 393224 | tf_op jit(solution)/shard_map/ppermute | solution.py:40
  94.8 9.2 %collective-permute-start.1 = (f32[2,32,512]{2,1,0:T(8,128)S(1)}, f32[2,32,512]{2,1,0:T(8,128)S(1)}, u32[]{:S(2)}, u32[]{:S(2)}) collective-permute-start(f32[2,32,512]{2,1,0:T(8,128)S(1)} %add.132), channel_id=1, source_target_pairs={{0,1},{1,0},{2,3},{3,2},{4,5},{5,4},{6,7},{7,6},{8,9},{9,8},{10,11... | collective-permute-start | bytes 393224 | tf_op jit(solution)/shard_map/ppermute | solution.py:40
  104.1 9.0 %collective-permute-start.6 = (f32[2,32,512]{2,1,0:T(8,128)S(1)}, f32[2,32,512]{2,1,0:T(8,128)S(1)}, u32[]{:S(2)}, u32[]{:S(2)}) collective-permute-start(f32[2,32,512]{2,1,0:T(8,128)S(1)} %add_add_fusion.3), channel_id=1, source_target_pairs={{0,24},{4,28},{8,16},{12,20},{16,8},{20,12},{24,0},{28,4},{32,56},... | collective-permute-start | bytes 393224 | tf_op jit(solution)/shard_map/ppermute | solution.py:40
  106.0 7.8 %collective-permute-start.5 = (f32[2,32,512]{2,1,0:T(8,128)S(1)}, f32[2,32,512]{2,1,0:T(8,128)S(1)}, u32[]{:S(2)}, u32[]{:S(2)}) collective-permute-start(f32[2,32,512]{2,1,0:T(8,128)S(1)} %add_add_fusion.3), channel_id=1, source_target_pairs={{0,16},{4,20},{8,24},{12,28},{16,0},{20,4},{24,8},{28,12},{32,48},... | collective-permute-start | bytes 393224 | tf_op jit(solution)/shard_map/ppermute | solution.py:40
  107.8 6.3 %collective-permute-start.4 = (f32[2,32,512]{2,1,0:T(8,128)S(1)}, f32[2,32,512]{2,1,0:T(8,128)S(1)}, u32[]{:S(2)}, u32[]{:S(2)}) collective-permute-start(f32[2,32,512]{2,1,0:T(8,128)S(1)} %add_add_fusion.3), channel_id=1, source_target_pairs={{0,8},{4,12},{8,0},{12,4},{16,24},{20,28},{24,16},{28,20},{32,40},... | collective-permute-start | bytes 393224 | tf_op jit(solution)/shard_map/ppermute | solution.py:40
  114.1 7.2 %collective-permute-start.9 = (f32[2,32,512]{2,1,0:T(8,128)S(1)}, f32[2,32,512]{2,1,0:T(8,128)S(1)}, u32[]{:S(2)}, u32[]{:S(2)}) collective-permute-start(f32[2,32,512]{2,1,0:T(8,128)S(1)} %add_add_fusion.2), channel_id=1, source_target_pairs={{0,96},{4,100},{8,104},{12,108},{16,112},{20,116},{24,120},{28,124... | collective-permute-start | bytes 393224 | tf_op jit(solution)/shard_map/ppermute | solution.py:40
  116.7 6.5 %collective-permute-start.8 = (f32[2,32,512]{2,1,0:T(8,128)S(1)}, f32[2,32,512]{2,1,0:T(8,128)S(1)}, u32[]{:S(2)}, u32[]{:S(2)}) collective-permute-start(f32[2,32,512]{2,1,0:T(8,128)S(1)} %add_add_fusion.2), channel_id=1, source_target_pairs={{0,64},{4,68},{8,72},{12,76},{16,80},{20,84},{24,88},{28,92},{32,9... | collective-permute-start | bytes 393224 | tf_op jit(solution)/shard_map/ppermute | solution.py:40
  117.6 5.6 %collective-permute-start.7 = (f32[2,32,512]{2,1,0:T(8,128)S(1)}, f32[2,32,512]{2,1,0:T(8,128)S(1)}, u32[]{:S(2)}, u32[]{:S(2)}) collective-permute-start(f32[2,32,512]{2,1,0:T(8,128)S(1)} %add_add_fusion.2), channel_id=1, source_target_pairs={{0,32},{4,36},{8,40},{12,44},{16,48},{20,52},{24,56},{28,60},{32,0... | collective-permute-start | bytes 393224 | tf_op jit(solution)/shard_map/ppermute | solution.py:40
  171.6 20.3 %copy-start.6 = (s32[128]{0:T(128)S(1)}, s32[128]{0:T(128)}, u32[]{:S(2)}) copy-start(s32[128]{0:T(128)} %param.18) | copy-start | bytes 1540
  184.2 33.3 %copy-start.4 = (f32[2,2048]{1,0:T(2,128)S(1)}, f32[2,2048]{1,0:T(2,128)}, u32[]{:S(2)}) copy-start(f32[2,2048]{1,0:T(2,128)} %param.16) | copy-start | bytes 49156
  184.2 33.3 %copy-start.5 = (f32[2,2048]{1,0:T(2,128)S(1)}, f32[2,2048]{1,0:T(2,128)}, u32[]{:S(2)}) copy-start(f32[2,2048]{1,0:T(2,128)} %param.17) | copy-start | bytes 49156
  184.2 37.7 %copy-start.3 = (f32[1,2,32,512]{3,2,1,0:T(8,128)S(1)}, f32[1,2,32,512]{3,2,1,0:T(8,128)}, u32[]{:S(2)}) copy-start(f32[1,2,32,512]{3,2,1,0:T(8,128)} %param.20) | copy-start | bytes 393220
  191.4 1.4 collective-permute-start.10
  192.9 10.7 %collective-permute-start.13 = (f32[2,32,512]{2,1,0:T(8,128)S(1)}, f32[2,32,512]{2,1,0:T(8,128)S(1)}, u32[]{:S(2)}, u32[]{:S(2)}) collective-permute-start(f32[2,32,512]{2,1,0:T(8,128)S(1)} %add.142), channel_id=1, source_target_pairs={{0,3},{1,2},{2,1},{3,0},{4,7},{5,6},{6,5},{7,4},{8,11},{9,10},{10,... | collective-permute-start | bytes 393224 | tf_op jit(solution)/shard_map/ppermute | solution.py:40
  194.6 8.9 %collective-permute-start.12 = (f32[2,32,512]{2,1,0:T(8,128)S(1)}, f32[2,32,512]{2,1,0:T(8,128)S(1)}, u32[]{:S(2)}, u32[]{:S(2)}) collective-permute-start(f32[2,32,512]{2,1,0:T(8,128)S(1)} %add.142), channel_id=1, source_target_pairs={{0,2},{1,3},{2,0},{3,1},{4,6},{5,7},{6,4},{7,5},{8,10},{9,11},{10,... | collective-permute-start | bytes 393224 | tf_op jit(solution)/shard_map/ppermute | solution.py:40
  195.6 8.0 %collective-permute-start.11 = (f32[2,32,512]{2,1,0:T(8,128)S(1)}, f32[2,32,512]{2,1,0:T(8,128)S(1)}, u32[]{:S(2)}, u32[]{:S(2)}) collective-permute-start(f32[2,32,512]{2,1,0:T(8,128)S(1)} %add.142), channel_id=1, source_target_pairs={{0,1},{1,0},{2,3},{3,2},{4,5},{5,4},{6,7},{7,6},{8,9},{9,8},{10,11... | collective-permute-start | bytes 393224 | tf_op jit(solution)/shard_map/ppermute | solution.py:40
  203.6 9.0 %collective-permute-start.16 = (f32[2,32,512]{2,1,0:T(8,128)S(1)}, f32[2,32,512]{2,1,0:T(8,128)S(1)}, u32[]{:S(2)}, u32[]{:S(2)}) collective-permute-start(f32[2,32,512]{2,1,0:T(8,128)S(1)} %add_add_fusion.1), channel_id=1, source_target_pairs={{0,24},{4,28},{8,16},{12,20},{16,8},{20,12},{24,0},{28,4},{32,56},... | collective-permute-start | bytes 393224 | tf_op jit(solution)/shard_map/ppermute | solution.py:40
  204.7 7.9 %collective-permute-start.15 = (f32[2,32,512]{2,1,0:T(8,128)S(1)}, f32[2,32,512]{2,1,0:T(8,128)S(1)}, u32[]{:S(2)}, u32[]{:S(2)}) collective-permute-start(f32[2,32,512]{2,1,0:T(8,128)S(1)} %add_add_fusion.1), channel_id=1, source_target_pairs={{0,16},{4,20},{8,24},{12,28},{16,0},{20,4},{24,8},{28,12},{32,48},... | collective-permute-start | bytes 393224 | tf_op jit(solution)/shard_map/ppermute | solution.py:40
  206.6 6.7 %collective-permute-start.14 = (f32[2,32,512]{2,1,0:T(8,128)S(1)}, f32[2,32,512]{2,1,0:T(8,128)S(1)}, u32[]{:S(2)}, u32[]{:S(2)}) collective-permute-start(f32[2,32,512]{2,1,0:T(8,128)S(1)} %add_add_fusion.1), channel_id=1, source_target_pairs={{0,8},{4,12},{8,0},{12,4},{16,24},{20,28},{24,16},{28,20},{32,40},... | collective-permute-start | bytes 393224 | tf_op jit(solution)/shard_map/ppermute | solution.py:40
  213.3 7.9 %collective-permute-start.19 = (f32[2,32,512]{2,1,0:T(8,128)S(1)}, f32[2,32,512]{2,1,0:T(8,128)S(1)}, u32[]{:S(2)}, u32[]{:S(2)}) collective-permute-start(f32[2,32,512]{2,1,0:T(8,128)S(1)} %add_add_fusion), channel_id=1, source_target_pairs={{0,96},{4,100},{8,104},{12,108},{16,112},{20,116},{24,120},{28,124... | collective-permute-start | bytes 393224 | tf_op jit(solution)/shard_map/ppermute | solution.py:40
  214.5 6.8 %collective-permute-start.18 = (f32[2,32,512]{2,1,0:T(8,128)S(1)}, f32[2,32,512]{2,1,0:T(8,128)S(1)}, u32[]{:S(2)}, u32[]{:S(2)}) collective-permute-start(f32[2,32,512]{2,1,0:T(8,128)S(1)} %add_add_fusion), channel_id=1, source_target_pairs={{0,64},{4,68},{8,72},{12,76},{16,80},{20,84},{24,88},{28,92},{32,9... | collective-permute-start | bytes 393224 | tf_op jit(solution)/shard_map/ppermute | solution.py:40
  216.1 5.7 %collective-permute-start.17 = (f32[2,32,512]{2,1,0:T(8,128)S(1)}, f32[2,32,512]{2,1,0:T(8,128)S(1)}, u32[]{:S(2)}, u32[]{:S(2)}) collective-permute-start(f32[2,32,512]{2,1,0:T(8,128)S(1)} %add_add_fusion), channel_id=1, source_target_pairs={{0,32},{4,36},{8,40},{12,44},{16,48},{20,52},{24,56},{28,60},{32,0... | collective-permute-start | bytes 393224 | tf_op jit(solution)/shard_map/ppermute | solution.py:40
  240.3 16.2 %copy-start.1 = (f32[2,512,32]{1,2,0:T(8,128)S(1)}, f32[2,512,32]{1,2,0:T(8,128)}, u32[]{:S(2)}) copy-start(f32[2,512,32]{1,2,0:T(8,128)} %param.14) | copy-start | bytes 393220
Sparse Core Ops, SparseCore 0:
  11.1 93.8 all-gather.1

commit v4 on v3

--- a/solution.py
+++ b/solution.py
@@ -50,10 +50,13 @@
     return lax.all_to_all(spread, axes, 0, 0, tiled=False).reshape(-1)
 
 
-def orth_t(ft):
+def gram_factor(ft):
     gram = jnp.einsum("mrd,msd->mrs", ft, ft, precision=HI)
-    lower_factor = jnp.linalg.cholesky(gram)
-    return jax.scipy.linalg.solve_triangular(lower_factor, ft, lower=True)
+    return jnp.linalg.cholesky(gram)
+
+
+def solve_lower(lower_factor, rows):
+    return jax.scipy.linalg.solve_triangular(lower_factor, rows, lower=True)
 
 
 def left_t(merged, right_t):
@@ -92,11 +95,14 @@
     joined_sum = sum_all_to_all(joined, replicas)
     p1_sum = joined_sum[: p1.size].reshape(lshape)
     norm_sum = joined_sum[p1.size :].reshape(norm_local.shape)
-    left_one = orth_t(p1_sum)
-    right_one = sum_radix4(right_t_of(merged, left_one), rounds) / replicas
-    p2_sum = sum_all_to_all(left_t(merged, right_one).reshape(-1), replicas)
-    left_two = orth_t(p2_sum.reshape(lshape))
-    right_two = sum_radix4(right_t_of(merged, left_two), rounds) / replicas
+    lower_one = gram_factor(p1_sum)
+    q1_sum = sum_radix4(right_t_of(merged, p1_sum), rounds)
+    right_one = solve_lower(lower_one, q1_sum) / replicas
+    p2_sum = sum_all_to_all(left_t(merged, right_one).reshape(-1), replicas).reshape(lshape)
+    lower_two = gram_factor(p2_sum)
+    left_two = solve_lower(lower_two, p2_sum)
+    q2_sum = sum_radix4(right_t_of(merged, p2_sum), rounds)
+    right_two = solve_lower(lower_two, q2_sum) / replicas
     update = jnp.einsum("mrd,mrk->mdk", left_two, right_two, precision=MID)
     new_errors = (merged - update)[None]
     new_norm_moment = momentum_decay * norm_moment + norm_sum / replicas

time: 264 us -> 251 us (0.951)
  blocking collectives: 64 us -> 25.4 us
  starting transfers between devices: 30.5 us -> 42.4 us
  waiting for transfers between devices: 46.4 us -> 58.2 us
    all_to_all x2 -> x1, blocking collectives: 46.5 us -> 25.4 us  [sum_all_to_all(): rows = lax.all_to_all(x.reshape(count, -1), axes, 0, 0, tiled=False)]
    all_to_all x1 -> x0, blocking collectives: 17.5 us -> none  [sum_all_to_all(): return lax.all_to_all(spread, axes, 0, 0, tiled=False).reshape(-1)]
    all_to_all x0 -> x1, waiting for transfers between devices: none -> 12.4 us  [sum_all_to_all(): rows = lax.all_to_all(x.reshape(count, -1), axes, 0, 0, tiled=False)]
    all_to_all x0 -> x1, starting transfers between devices: none -> 6.7 us  [sum_all_to_all(): rows = lax.all_to_all(x.reshape(count, -1), axes, 0, 0, tiled=False)]
    all_to_all x1 -> x2, waiting for transfers between devices: 17.3 us -> 23 us  [sum_all_to_all(): return lax.all_to_all(spread, axes, 0, 0, tiled=False).reshape(-1)]
    all_to_all x1 -> x2, starting transfers between devices: 4.8 us -> 9.46 us  [sum_all_to_all(): return lax.all_to_all(spread, axes, 0, 0, tiled=False).reshape(-1)]
    ppermute x18, waiting for transfers between devices: 26.7 us -> 22.3 us  [sum_radix4(): r1, r2, r3 = [lax.ppermute(x, axis, perm) for axis, perm in parts]]
  transfers between devices with their start and end apart: 22 -> 24, of which waited for: 13 -> 14; matrix products, arithmetic and copies ran while one was open for 28% -> 30% of each run, Pallas kernels for 0% -> 0%
where the time goes in v4:
time: 251 us
  waiting for transfers between devices  58.2 us (23%)
  other arithmetic  46.1 us (18%)
  starting transfers between devices  42.4 us (17%)
  matrix products  42.4 us (17%)
  blocking collectives  25.4 us (10%)
  between operations  19.6 us (8%)
  local copies, waits for them, and re-layouts  16.8 us (7%)
    all_to_all x1, blocking collectives, sum_all_to_all(): rows = lax.all_to_all(x.reshape(count, -1), axes, 0, 0, tiled=False)  25.4 us
    ppermute x18, starting transfers between devices, sum_radix4(): r1, r2, r3 = [lax.ppermute(x, axis, perm) for axis, perm in parts]  25 us
    all_to_all x2, waiting for transfers between devices, sum_all_to_all(): return lax.all_to_all(spread, axes, 0, 0, tiled=False).reshape(-1)  23 us
    ppermute x18, waiting for transfers between devices, sum_radix4(): r1, r2, r3 = [lax.ppermute(x, axis, perm) for axis, perm in parts]  22.3 us
    dot_general x2, matrix products, left_t(): return jnp.einsum('mdk,mrk->mrd', merged, right_t, precision=MID)  16.7 us
    convert_element_type x1, other arithmetic, on_device(): chosen.astype(jnp.bfloat16)  16.2 us
    dot_general x2, matrix products, right_t_of(): return jnp.einsum('mdk,mrd->mrk', merged, left_tr, precision=MID)  15.7 us
    all_to_all x1, waiting for transfers between devices, sum_all_to_all(): rows = lax.all_to_all(x.reshape(count, -1), axes, 0, 0, tiled=False)  12.4 us
  transfers between devices with their start and end apart: 24, of which 14 were waited for; matrix products, arithmetic and copies ran while one was open for 30% of the time, Pallas kernels for 0%

profile of v4, /device:TPU:0, one launch (start us, length us, event | category | flops | bytes accessed | tf_op | source)
XLA Modules:
  0.0 250.8 jit_solution(12016356980433842166)
XLA Ops:
  7.2 1.6 multiply_subtract_fusion
  9.6 8.4 %fusion.7 = f32[2,2048,32]{1,2,0:T(8,128)S(1)} fusion(f32[2,512,32]{1,2,0:T(8,128)S(1)} %copy-done, f32[1,2,2048,512]{3,2,1,0:T(8,128)} %param.13, bf16[1,2,2048,512]{3,2,1,0:T(8,128)(2,1)} %param.12), kind=kOutput, calls=%fused_computation.10 | convolution fusion | flops 406847488 | bytes 13238272 | tf_op jit(solution)/shard_map/mdk,mrk->mrd/dot_general | solution.py:63
  18.9 25.4 %all_to_all.32 = f32[128,1,1056]{2,1,0:T(1,128)S(1)} all-to-all(f32[128,1,1056]{2,1,0:T(1,128)S(1)} %all_to_all.26), channel_id=1, replica_groups=mesh['dp'=32,'group'=4] {'dp','group'}, dimensions={0} | all-to-all | bytes 1081344 | tf_op jit(solution)/shard_map/all_to_all | solution.py:47
  45.8 4.6 %all-to-all-start.1 = ((f32[128,1,1056]{2,1,0:T(1,128)}), f32[128,1,1056]{2,1,0:T(1,128)S(1)}, u32[]{:S(2)}, u32[]{:S(2)}) async-start(f32[128,1,1056]{2,1,0:T(1,128)} %broadcast_in_dim.16), calls=%async_computation.1 | async-start | bytes 1179648 | tf_op jit(solution)/shard_map/all_to_all | solution.py:50
  50.4 17.1 %all-to-all-done.1 = f32[128,1,1056]{2,1,0:T(1,128)S(1)} async-done(((f32[128,1,1056]{2,1,0:T(1,128)}), f32[128,1,1056]{2,1,0:T(1,128)S(1)}, u32[]{:S(2)}, u32[]{:S(2)}) %all-to-all-start.1) | async-done | bytes 540704 | tf_op jit(solution)/shard_map/all_to_all | solution.py:50
  69.6 8.4 %fusion.5 = f32[2,32,512]{2,1,0:T(8,128)S(1)} fusion(f32[2,32,2048]{2,1,0:T(8,128)S(1)} %reshape.84, f32[1,2,2048,512]{3,2,1,0:T(8,128)} %param.13, bf16[1,2,2048,512]{3,2,1,0:T(8,128)(2,1)} %param.12), kind=kOutput, calls=%fused_computation.8 | convolution fusion | flops 406847488 | bytes 13238272 | tf_op jit(solution)/shard_map/mdk,mrd->mrk/dot_general | solution.py:67
  81.6 2.4 collective-permute-start.1
  84.0 5.9 %custom-call.15 = f32[2,32,32]{2,1,0:T(8,128)S(1)} custom-call(f32[2,32,32]{2,1,0:T(8,128)S(1)} %fusion.30), custom_call_target="Cholesky" | custom-call | tf_op jit(solution)/shard_map/jit(cholesky)/cholesky | solution.py:55
  89.9 3.1 %collective-permute-done.3 = f32[2,32,512]{2,1,0:T(8,128)S(1)} collective-permute-done((f32[2,32,512]{2,1,0:T(8,128)S(1)}, f32[2,32,512]{2,1,0:T(8,128)S(1)}, u32[]{:S(2)}, u32[]{:S(2)}) %collective-permute-start.3) | collective-permute-done | bytes 131104 | tf_op jit(solution)/shard_map/ppermute | solution.py:40
  93.0 3.6 %collective-permute-done.1 = f32[2,32,512]{2,1,0:T(8,128)S(1)} collective-permute-done((f32[2,32,512]{2,1,0:T(8,128)S(1)}, f32[2,32,512]{2,1,0:T(8,128)S(1)}, u32[]{:S(2)}, u32[]{:S(2)}) %collective-permute-start.1) | collective-permute-done | bytes 131104 | tf_op jit(solution)/shard_map/ppermute | solution.py:40
  96.7 1.9 collective-permute-start.5
  98.6 2.1 collective-permute-start.4
  100.9 5.4 %collective-permute-done.6 = f32[2,32,512]{2,1,0:T(8,128)S(1)} collective-permute-done((f32[2,32,512]{2,1,0:T(8,128)S(1)}, f32[2,32,512]{2,1,0:T(8,128)S(1)}, u32[]{:S(2)}, u32[]{:S(2)}) %collective-permute-start.6) | collective-permute-done | bytes 131104 | tf_op jit(solution)/shard_map/ppermute | solution.py:40
  106.4 2.3 collective-permute-start.9
  110.7 4.9 %custom-call.16 = f32[2,1,32,32]{2,3,1,0:T(8,128)S(1)} custom-call(f32[2,1,32,32]{3,2,1,0:T(8,128)S(1)} %select_bitcast_fusion), custom_call_target="InvertDiagBlocksLowerTriangular" | custom-call | tf_op jit(solution)/shard_map/jit(_solve_triangular)/vmap()/triangular_solve | solution.py:59
  116.5 8.3 %fusion.3 = f32[2,32,2048]{2,1,0:T(8,128)S(1)} fusion(f32[2,32,512]{2,1,0:T(8,128)S(1)} %convolution_multiply_fusion.1, f32[1,2,2048,512]{3,2,1,0:T(8,128)} %param.13, bf16[1,2,2048,512]{3,2,1,0:T(8,128)(2,1)} %param.12), kind=kOutput, calls=%fused_computation.6 | convolution fusion | flops 406847488 | bytes 13238272 | tf_op jit(solution)/shard_map/mdk,mrk->mrd/dot_general | solution.py:63
  126.2 6.7 %all-to-all-start.2 = ((f32[128,1,1024]{2,1,0:T(1,128)}), f32[128,1,1024]{2,1,0:T(1,128)S(1)}, u32[]{:S(2)}, u32[]{:S(2)}) async-start(f32[128,1,1024]{2,1,0:T(1,128)} %all_to_all.27), calls=%async_computation.2 | async-start | bytes 1048576 | tf_op jit(solution)/shard_map/all_to_all | solution.py:47
  133.7 12.4 %all-to-all-done.2 = f32[128,1,1024]{2,1,0:T(1,128)S(1)} async-done(((f32[128,1,1024]{2,1,0:T(1,128)}), f32[128,1,1024]{2,1,0:T(1,128)S(1)}, u32[]{:S(2)}, u32[]{:S(2)}) %all-to-all-start.2) | async-done | bytes 524320 | tf_op jit(solution)/shard_map/all_to_all | solution.py:47
  147.5 4.8 %all-to-all-start.3 = ((f32[128,1,1024]{2,1,0:T(1,128)}), f32[128,1,1024]{2,1,0:T(1,128)S(1)}, u32[]{:S(2)}, u32[]{:S(2)}) async-start(f32[128,1,1024]{2,1,0:T(1,128)} %broadcast_in_dim.17), calls=%async_computation.3 | async-start | bytes 1048576 | tf_op jit(solution)/shard_map/all_to_all | solution.py:50
  159.4 5.9 %all-to-all-done.3 = f32[128,1,1024]{2,1,0:T(1,128)S(1)} async-done(((f32[128,1,1024]{2,1,0:T(1,128)}), f32[128,1,1024]{2,1,0:T(1,128)S(1)}, u32[]{:S(2)}, u32[]{:S(2)}) %all-to-all-start.3) | async-done | bytes 524320 | tf_op jit(solution)/shard_map/all_to_all | solution.py:50
  167.4 7.2 %fusion.1 = f32[2,32,512]{2,1,0:T(8,128)S(1)} fusion(f32[2,32,2048]{2,1,0:T(8,128)S(1)} %reshape_reshape.4, f32[1,2,2048,512]{3,2,1,0:T(8,128)} %param.13, bf16[1,2,2048,512]{3,2,1,0:T(8,128)(2,1)} %param.12), kind=kOutput, calls=%fused_computation.4 | convolution fusion | flops 406847488 | bytes 13238272 | tf_op jit(solution)/shard_map/mdk,mrd->mrk/dot_general | solution.py:67
  175.1 5.9 %custom-call.17 = f32[2,32,32]{2,1,0:T(8,128)S(1)} custom-call(f32[2,32,32]{2,1,0:T(8,128)S(1)} %fusion.28), custom_call_target="Cholesky" | custom-call | tf_op jit(solution)/shard_map/jit(cholesky)/cholesky | solution.py:55
  181.0 1.4 collective-permute-start.13
  183.7 1.4 collective-permute-start.11
  185.3 5.3 %collective-permute-done.13 = f32[2,32,512]{2,1,0:T(8,128)S(1)} collective-permute-done((f32[2,32,512]{2,1,0:T(8,128)S(1)}, f32[2,32,512]{2,1,0:T(8,128)S(1)}, u32[]{:S(2)}, u32[]{:S(2)}) %collective-permute-start.13) | collective-permute-done | bytes 131104 | tf_op jit(solution)/shard_map/ppermute | solution.py:40
  192.4 1.9 collective-permute-start.15
  195.6 4.9 %custom-call.10 = f32[2,1,32,32]{2,3,1,0:T(8,128)S(1)} custom-call(f32[2,1,32,32]{3,2,1,0:T(8,128)S(1)} %fusion.31), custom_call_target="InvertDiagBlocksLowerTriangular" | custom-call | tf_op jit(solution)/shard_map/jit(_solve_triangular)/vmap()/triangular_solve | solution.py:59
  201.8 1.6 collective-permute-start.18
  205.4 1.5 collective-permute-done.19
  212.0 5.7 %fusion.51 = f32[2,2048,512]{2,1,0:T(8,128)} fusion(f32[2,32,2048]{2,1,0:T(8,128)S(1)} %fusion.26, f32[2,32,512]{2,1,0:T(8,128)S(1)} %convolution_multiply_fusion), kind=kOutput, calls=%fused_computation.87 | convolution fusion | flops 402653184 | bytes 9043968 | tf_op jit(solution)/shard_map/mrd,mrk->mdk/dot_general | solution.py:106
  217.7 10.1 %gather_fusion = f32[128,32,512]{2,1,0:T(8,128)} fusion(f32[128,2,32,512]{3,2,1,0:T(8,128)} %all-gather.2.cloned.1.call-done, s32[128]{0:T(128)S(1)} %fusion.45), kind=kCustom, calls=%fused_computation | custom fusion | bytes 16778240 | tf_op jit(solution)/shard_map/gather | solution.py:134
  227.8 16.2 %fusion = (bf16[2,2048,512]{2,1,0:T(8,128)(2,1)}, f32[1,2,2048,512]{3,2,1,0:T(8,128)}) fusion(f32[2,2048,512]{2,1,0:T(8,128)} %fusion.51, f32[1,2,2048,512]{3,2,1,0:T(8,128)} %param.13, bf16[1,2,2048,512]{3,2,1,0:T(8,128)(2,1)} %param.12, f32[2,2048,512]{2,1,0:T(8,128)} %bitcast.99), kind=kLoop, calls=%fused_computation.2 | loop fusion | flops 12582912 | bytes 41943040 | tf_op jit(solution)/shard_map/convert_element_type | solution.py:135
  (89 shorter events, 32.7 us)
Async XLA Ops:
  7.2 2.4 copy-start
  7.2 210.5 %all-gather.2.cloned.1.call-start = ((), (), s32[]{:S(2)}) async-start(), calls=%async_computation.4 | async-start | bytes 16908288 | tf_op jit(solution)/shard_map/all_gather | solution.py:88
  45.8 21.7 %all-to-all-start.1 = ((f32[128,1,1056]{2,1,0:T(1,128)}), f32[128,1,1056]{2,1,0:T(1,128)S(1)}, u32[]{:S(2)}, u32[]{:S(2)}) async-start(f32[128,1,1056]{2,1,0:T(1,128)} %broadcast_in_dim.16), calls=%async_computation.1 | async-start | bytes 1179648 | tf_op jit(solution)/shard_map/all_to_all | solution.py:50
  78.0 1.8 collective-permute-start
  79.9 13.1 %collective-permute-start.3 = (f32[2,32,512]{2,1,0:T(8,128)S(1)}, f32[2,32,512]{2,1,0:T(8,128)S(1)}, u32[]{:S(2)}, u32[]{:S(2)}) collective-permute-start(f32[2,32,512]{2,1,0:T(8,128)S(1)} %add.135), channel_id=1, source_target_pairs={{0,3},{1,2},{2,1},{3,0},{4,7},{5,6},{6,5},{7,4},{8,11},{9,10},{10,... | collective-permute-start | bytes 393224 | tf_op jit(solution)/shard_map/ppermute | solution.py:40
  80.5 12.4 %collective-permute-start.2 = (f32[2,32,512]{2,1,0:T(8,128)S(1)}, f32[2,32,512]{2,1,0:T(8,128)S(1)}, u32[]{:S(2)}, u32[]{:S(2)}) collective-permute-start(f32[2,32,512]{2,1,0:T(8,128)S(1)} %add.135), channel_id=1, source_target_pairs={{0,2},{1,3},{2,0},{3,1},{4,6},{5,7},{6,4},{7,5},{8,10},{9,11},{10,... | collective-permute-start | bytes 393224 | tf_op jit(solution)/shard_map/ppermute | solution.py:40
  81.6 15.0 %collective-permute-start.1 = (f32[2,32,512]{2,1,0:T(8,128)S(1)}, f32[2,32,512]{2,1,0:T(8,128)S(1)}, u32[]{:S(2)}, u32[]{:S(2)}) collective-permute-start(f32[2,32,512]{2,1,0:T(8,128)S(1)} %add.135), channel_id=1, source_target_pairs={{0,1},{1,0},{2,3},{3,2},{4,5},{5,4},{6,7},{7,6},{8,9},{9,8},{10,11... | collective-permute-start | bytes 393224 | tf_op jit(solution)/shard_map/ppermute | solution.py:40
  96.6 36.3 %copy-start.5 = (s32[128]{0:T(128)S(1)}, s32[128]{0:T(128)}, u32[]{:S(2)}) copy-start(s32[128]{0:T(128)} %param.18) | copy-start | bytes 1540
  96.6 9.8 %collective-permute-start.6 = (f32[2,32,512]{2,1,0:T(8,128)S(1)}, f32[2,32,512]{2,1,0:T(8,128)S(1)}, u32[]{:S(2)}, u32[]{:S(2)}) collective-permute-start(f32[2,32,512]{2,1,0:T(8,128)S(1)} %add_add_fusion.3), channel_id=1, source_target_pairs={{0,24},{4,28},{8,16},{12,20},{16,8},{20,12},{24,0},{28,4},{32,56},... | collective-permute-start | bytes 393224 | tf_op jit(solution)/shard_map/ppermute | solution.py:40
  96.7 9.7 %collective-permute-start.5 = (f32[2,32,512]{2,1,0:T(8,128)S(1)}, f32[2,32,512]{2,1,0:T(8,128)S(1)}, u32[]{:S(2)}, u32[]{:S(2)}) collective-permute-start(f32[2,32,512]{2,1,0:T(8,128)S(1)} %add_add_fusion.3), channel_id=1, source_target_pairs={{0,16},{4,20},{8,24},{12,28},{16,0},{20,4},{24,8},{28,12},{32,48},... | collective-permute-start | bytes 393224 | tf_op jit(solution)/shard_map/ppermute | solution.py:40
  98.6 7.7 %collective-permute-start.4 = (f32[2,32,512]{2,1,0:T(8,128)S(1)}, f32[2,32,512]{2,1,0:T(8,128)S(1)}, u32[]{:S(2)}, u32[]{:S(2)}) collective-permute-start(f32[2,32,512]{2,1,0:T(8,128)S(1)} %add_add_fusion.3), channel_id=1, source_target_pairs={{0,8},{4,12},{8,0},{12,4},{16,24},{20,28},{24,16},{28,20},{32,40},... | collective-permute-start | bytes 393224 | tf_op jit(solution)/shard_map/ppermute | solution.py:40
  106.4 9.2 %collective-permute-start.9 = (f32[2,32,512]{2,1,0:T(8,128)S(1)}, f32[2,32,512]{2,1,0:T(8,128)S(1)}, u32[]{:S(2)}, u32[]{:S(2)}) collective-permute-start(f32[2,32,512]{2,1,0:T(8,128)S(1)} %add_add_fusion.2), channel_id=1, source_target_pairs={{0,96},{4,100},{8,104},{12,108},{16,112},{20,116},{24,120},{28,124... | collective-permute-start | bytes 393224 | tf_op jit(solution)/shard_map/ppermute | solution.py:40
  108.7 7.2 %collective-permute-start.8 = (f32[2,32,512]{2,1,0:T(8,128)S(1)}, f32[2,32,512]{2,1,0:T(8,128)S(1)}, u32[]{:S(2)}, u32[]{:S(2)}) collective-permute-start(f32[2,32,512]{2,1,0:T(8,128)S(1)} %add_add_fusion.2), channel_id=1, source_target_pairs={{0,64},{4,68},{8,72},{12,76},{16,80},{20,84},{24,88},{28,92},{32,9... | collective-permute-start | bytes 393224 | tf_op jit(solution)/shard_map/ppermute | solution.py:40
  110.0 6.2 %collective-permute-start.7 = (f32[2,32,512]{2,1,0:T(8,128)S(1)}, f32[2,32,512]{2,1,0:T(8,128)S(1)}, u32[]{:S(2)}, u32[]{:S(2)}) collective-permute-start(f32[2,32,512]{2,1,0:T(8,128)S(1)} %add_add_fusion.2), channel_id=1, source_target_pairs={{0,32},{4,36},{8,40},{12,44},{16,48},{20,52},{24,56},{28,60},{32,0... | collective-permute-start | bytes 393224 | tf_op jit(solution)/shard_map/ppermute | solution.py:40
  116.5 42.3 %copy-start.3 = (f32[2,2048]{1,0:T(2,128)S(1)}, f32[2,2048]{1,0:T(2,128)}, u32[]{:S(2)}) copy-start(f32[2,2048]{1,0:T(2,128)} %param.16) | copy-start | bytes 49156
  116.5 42.3 %copy-start.4 = (f32[2,2048]{1,0:T(2,128)S(1)}, f32[2,2048]{1,0:T(2,128)}, u32[]{:S(2)}) copy-start(f32[2,2048]{1,0:T(2,128)} %param.17) | copy-start | bytes 49156
  126.2 19.9 %all-to-all-start.2 = ((f32[128,1,1024]{2,1,0:T(1,128)}), f32[128,1,1024]{2,1,0:T(1,128)S(1)}, u32[]{:S(2)}, u32[]{:S(2)}) async-start(f32[128,1,1024]{2,1,0:T(1,128)} %all_to_all.27), calls=%async_computation.2 | async-start | bytes 1048576 | tf_op jit(solution)/shard_map/all_to_all | solution.py:47
  147.5 17.8 %all-to-all-start.3 = ((f32[128,1,1024]{2,1,0:T(1,128)}), f32[128,1,1024]{2,1,0:T(1,128)S(1)}, u32[]{:S(2)}, u32[]{:S(2)}) async-start(f32[128,1,1024]{2,1,0:T(1,128)} %broadcast_in_dim.17), calls=%async_computation.3 | async-start | bytes 1048576 | tf_op jit(solution)/shard_map/all_to_all | solution.py:50
  167.4 42.0 %copy-start.2 = (f32[1,2,32,512]{3,2,1,0:T(8,128)S(1)}, f32[1,2,32,512]{3,2,1,0:T(8,128)}, u32[]{:S(2)}) copy-start(f32[1,2,32,512]{3,2,1,0:T(8,128)} %param.20) | copy-start | bytes 393220
  174.7 6.3 %collective-permute-start.10 = (f32[2,32,512]{2,1,0:T(8,128)S(1)}, f32[2,32,512]{2,1,0:T(8,128)S(1)}, u32[]{:S(2)}, u32[]{:S(2)}) collective-permute-start(f32[2,32,512]{2,1,0:T(8,128)S(1)} %fusion.1), channel_id=1, source_target_pairs={{0,4},{4,0},{8,12},{12,8},{16,20},{20,16},{24,28},{28,24},{32,36},... | collective-permute-start | bytes 393224 | tf_op jit(solution)/shard_map/ppermute | solution.py:38
  181.0 9.6 %collective-permute-start.13 = (f32[2,32,512]{2,1,0:T(8,128)S(1)}, f32[2,32,512]{2,1,0:T(8,128)S(1)}, u32[]{:S(2)}, u32[]{:S(2)}) collective-permute-start(f32[2,32,512]{2,1,0:T(8,128)S(1)} %add.145), channel_id=1, source_target_pairs={{0,3},{1,2},{2,1},{3,0},{4,7},{5,6},{6,5},{7,4},{8,11},{9,10},{10,... | collective-permute-start | bytes 393224 | tf_op jit(solution)/shard_map/ppermute | solution.py:40
  182.5 8.2 %collective-permute-start.12 = (f32[2,32,512]{2,1,0:T(8,128)S(1)}, f32[2,32,512]{2,1,0:T(8,128)S(1)}, u32[]{:S(2)}, u32[]{:S(2)}) collective-permute-start(f32[2,32,512]{2,1,0:T(8,128)S(1)} %add.145), channel_id=1, source_target_pairs={{0,2},{1,3},{2,0},{3,1},{4,6},{5,7},{6,4},{7,5},{8,10},{9,11},{10,... | collective-permute-start | bytes 393224 | tf_op jit(solution)/shard_map/ppermute | solution.py:40
  183.7 7.5 %collective-permute-start.11 = (f32[2,32,512]{2,1,0:T(8,128)S(1)}, f32[2,32,512]{2,1,0:T(8,128)S(1)}, u32[]{:S(2)}, u32[]{:S(2)}) collective-permute-start(f32[2,32,512]{2,1,0:T(8,128)S(1)} %add.145), channel_id=1, source_target_pairs={{0,1},{1,0},{2,3},{3,2},{4,5},{5,4},{6,7},{7,6},{8,9},{9,8},{10,11... | collective-permute-start | bytes 393224 | tf_op jit(solution)/shard_map/ppermute | solution.py:40
  191.3 9.2 %collective-permute-start.16 = (f32[2,32,512]{2,1,0:T(8,128)S(1)}, f32[2,32,512]{2,1,0:T(8,128)S(1)}, u32[]{:S(2)}, u32[]{:S(2)}) collective-permute-start(f32[2,32,512]{2,1,0:T(8,128)S(1)} %add_add_fusion.1), channel_id=1, source_target_pairs={{0,24},{4,28},{8,16},{12,20},{16,8},{20,12},{24,0},{28,4},{32,56},... | collective-permute-start | bytes 393224 | tf_op jit(solution)/shard_map/ppermute | solution.py:40
  192.4 8.1 %collective-permute-start.15 = (f32[2,32,512]{2,1,0:T(8,128)S(1)}, f32[2,32,512]{2,1,0:T(8,128)S(1)}, u32[]{:S(2)}, u32[]{:S(2)}) collective-permute-start(f32[2,32,512]{2,1,0:T(8,128)S(1)} %add_add_fusion.1), channel_id=1, source_target_pairs={{0,16},{4,20},{8,24},{12,28},{16,0},{20,4},{24,8},{28,12},{32,48},... | collective-permute-start | bytes 393224 | tf_op jit(solution)/shard_map/ppermute | solution.py:40
  194.3 6.2 %collective-permute-start.14 = (f32[2,32,512]{2,1,0:T(8,128)S(1)}, f32[2,32,512]{2,1,0:T(8,128)S(1)}, u32[]{:S(2)}, u32[]{:S(2)}) collective-permute-start(f32[2,32,512]{2,1,0:T(8,128)S(1)} %add_add_fusion.1), channel_id=1, source_target_pairs={{0,8},{4,12},{8,0},{12,4},{16,24},{20,28},{24,16},{28,20},{32,40},... | collective-permute-start | bytes 393224 | tf_op jit(solution)/shard_map/ppermute | solution.py:40
  200.6 6.3 %collective-permute-start.19 = (f32[2,32,512]{2,1,0:T(8,128)S(1)}, f32[2,32,512]{2,1,0:T(8,128)S(1)}, u32[]{:S(2)}, u32[]{:S(2)}) collective-permute-start(f32[2,32,512]{2,1,0:T(8,128)S(1)} %add_add_fusion), channel_id=1, source_target_pairs={{0,96},{4,100},{8,104},{12,108},{16,112},{20,116},{24,120},{28,124... | collective-permute-start | bytes 393224 | tf_op jit(solution)/shard_map/ppermute | solution.py:40
  201.8 6.5 %collective-permute-start.18 = (f32[2,32,512]{2,1,0:T(8,128)S(1)}, f32[2,32,512]{2,1,0:T(8,128)S(1)}, u32[]{:S(2)}, u32[]{:S(2)}) collective-permute-start(f32[2,32,512]{2,1,0:T(8,128)S(1)} %add_add_fusion), channel_id=1, source_target_pairs={{0,64},{4,68},{8,72},{12,76},{16,80},{20,84},{24,88},{28,92},{32,9... | collective-permute-start | bytes 393224 | tf_op jit(solution)/shard_map/ppermute | solution.py:40
  203.4 5.7 %collective-permute-start.17 = (f32[2,32,512]{2,1,0:T(8,128)S(1)}, f32[2,32,512]{2,1,0:T(8,128)S(1)}, u32[]{:S(2)}, u32[]{:S(2)}) collective-permute-start(f32[2,32,512]{2,1,0:T(8,128)S(1)} %add_add_fusion), channel_id=1, source_target_pairs={{0,32},{4,36},{8,40},{12,44},{16,48},{20,52},{24,56},{28,60},{32,0... | collective-permute-start | bytes 393224 | tf_op jit(solution)/shard_map/ppermute | solution.py:40
  227.8 16.2 %copy-start.1 = (f32[2,512,32]{1,2,0:T(8,128)S(1)}, f32[2,512,32]{1,2,0:T(8,128)}, u32[]{:S(2)}) copy-start(f32[2,512,32]{1,2,0:T(8,128)} %param.14) | copy-start | bytes 393220
Sparse Core Ops, SparseCore 0:
  11.1 95.8 all-gather.1

commit v5 on v4

--- a/solution.py
+++ b/solution.py
@@ -1,6 +1,8 @@
 import jax
 import jax.numpy as jnp
 from jax import lax
+from jax.experimental import pallas as pl
+from jax.experimental.pallas import tpu as pltpu
 from jax.sharding import PartitionSpec as P
 
 momentum_decay = 0.9
@@ -65,6 +67,66 @@
 
 def right_t_of(merged, left_tr):
     return jnp.einsum("mdk,mrd->mrk", merged, left_tr, precision=MID)
+
+
+TAIL_ROWS = 256
+
+
+def tail_kernel(table, grads, errs, left_rows, right_t, carried, out_err, out_w, cbuf, sems):
+    m = pl.program_id(0)
+    i = pl.program_id(1)
+    per_block = cbuf.shape[0]
+    piece_rows = cbuf.shape[1]
+    blocks = pl.num_programs(1)
+    base = (m * blocks + i) * per_block
+    copies = []
+    for p in range(per_block):
+        cp = pltpu.make_async_copy(carried.at[table[base + p]], cbuf.at[p], sems.at[p])
+        cp.start()
+        copies.append(cp)
+    upd = jnp.dot(left_rows[0], right_t[0], precision=HI, preferred_element_type=jnp.float32)
+    merged = grads[0].astype(jnp.float32) + errs[0]
+    out_err[0] = merged - upd
+    for p in range(per_block):
+        copies[p].wait()
+        rows = slice(p * piece_rows, (p + 1) * piece_rows)
+        out_w[0, rows, :] = (cbuf[p] - step_rate * upd[rows, :]).astype(out_w.dtype)
+
+
+def tail(table, grads, errs, left_rows, right_t, carried):
+    mats, dw, kv = grads.shape
+    rank = left_rows.shape[2]
+    piece_rows = carried.shape[1]
+    per_block = TAIL_ROWS // piece_rows
+    grid = (mats, dw // TAIL_ROWS)
+    row_spec = pl.BlockSpec((1, TAIL_ROWS, kv), lambda m, i, t: (m, i, 0))
+    spec = pltpu.PrefetchScalarGridSpec(
+        num_scalar_prefetch=1,
+        grid=grid,
+        in_specs=[
+            row_spec,
+            row_spec,
+            pl.BlockSpec((1, TAIL_ROWS, rank), lambda m, i, t: (m, i, 0)),
+            pl.BlockSpec((1, rank, kv), lambda m, i, t: (m, 0, 0)),
+            pl.BlockSpec(memory_space=pl.ANY),
+        ],
+        out_specs=[row_spec, row_spec],
+        scratch_shapes=[
+            pltpu.VMEM((per_block, piece_rows, kv), jnp.float32),
+            pltpu.SemaphoreType.DMA((per_block,)),
+        ],
+    )
+    elems = mats * dw * kv
+    cost = pl.CostEstimate(flops=2 * elems * rank, transcendentals=0, bytes_accessed=elems * (2 + 4 + 4 + 4 + 2))
+    return pl.pallas_call(
+        tail_kernel,
+        grid_spec=spec,
+        out_shape=[
+            jax.ShapeDtypeStruct((mats, dw, kv), jnp.float32),
+            jax.ShapeDtypeStruct((mats, dw, kv), jnp.bfloat16),
+        ],
+        cost_estimate=cost,
+    )(table, grads, errs, left_rows, right_t, carried)
 
 
 def on_device(
@@ -103,8 +165,6 @@
     left_two = solve_lower(lower_two, p2_sum)
     q2_sum = sum_radix4(right_t_of(merged, p2_sum), rounds)
     right_two = solve_lower(lower_two, q2_sum) / replicas
-    update = jnp.einsum("mrd,mrk->mdk", left_two, right_two, precision=MID)
-    new_errors = (merged - update)[None]
     new_norm_moment = momentum_decay * norm_moment + norm_sum / replicas
     new_norm_weights = norm_weights - step_rate * new_norm_moment
     piece_count = owners.shape[0]
@@ -130,9 +190,12 @@
         fresh = momentum_decay * old_moment[s] + piece_update
         moment_list.append(jnp.where(jnp.any(hit), fresh, old_moment[s]))
     moment_slots = jnp.stack(moment_list)
-    pieces = update.reshape(piece_count, piece_rows, features)
-    chosen = every_carried[owners, slot_of] - step_rate * pieces
-    new_weights = chosen.astype(jnp.bfloat16).reshape(2, piece_count * piece_rows // 2, features)
+    table = jnp.clip(owners * slot_count + slot_of, 0, every_carried.shape[0] * slot_count - 1)
+    carried_rows = every_carried.reshape(-1, piece_rows, features)
+    new_errors, new_weights = tail(
+        table, gradients[0], errors[0], jnp.swapaxes(left_two, 1, 2), right_two, carried_rows
+    )
+    new_errors = new_errors[None]
     return (new_errors, moment_slots[None], new_weights, new_norm_weights, new_norm_moment)
 
 

time: 251 us -> 247 us (0.984)
  Pallas kernels: 0 us -> 27 us
  other arithmetic: 46.1 us -> 30.5 us
  local copies, waits for them, and re-layouts: 16.8 us -> 8.65 us
  matrix products: 42.4 us -> 35.7 us
    pallas_call x0 -> x1, Pallas kernels: none -> 27 us  [tail(): pl.pallas_call(tail_kernel, grid_spec=spec, out_shape=[jax.ShapeDtypeStru...]
    convert_element_type x1 -> x0, other arithmetic: 16.2 us -> none  [on_device(): chosen.astype(jnp.bfloat16)]
    gather x1 -> x0, local copies, waits for them, and re-layouts: 10.1 us -> none  [on_device(): chosen = every_carried[owners, slot_of] - step_rate * pieces]
    dot_general x1 -> x0, matrix products: 5.72 us -> none  [on_device(): update = jnp.einsum('mrd,mrk->mdk', left_two, right_two, precision=MID)]
  transfers between devices with their start and end apart: 24 -> 24, of which waited for: 14 -> 13; matrix products, arithmetic and copies ran while one was open for 30% -> 29% of each run, Pallas kernels for 0% -> 0%
where the time goes in v5:
time: 247 us; the launch traced here: 246 us
  waiting for transfers between devices  56 us (23%)
  starting transfers between devices  43.4 us (18%)
  matrix products  35.7 us (14%)
  other arithmetic  30.5 us (12%)
  Pallas kernels  27 us (11%)
  blocking collectives  25.3 us (10%)
  between operations  19.6 us (8%)
  local copies, waits for them, and re-layouts  8.65 us (4%)
    pallas_call x1, Pallas kernels, tail(): pl.pallas_call(tail_kernel, grid_spec=spec, out_shape=[jax.ShapeDtypeStru...  27 us
    all_to_all x1, blocking collectives, sum_all_to_all(): rows = lax.all_to_all(x.reshape(count, -1), axes, 0, 0, tiled=False)  25.3 us
    ppermute x18, starting transfers between devices, sum_radix4(): r1, r2, r3 = [lax.ppermute(x, axis, perm) for axis, perm in parts]  25 us
    all_to_all x2, waiting for transfers between devices, sum_all_to_all(): return lax.all_to_all(spread, axes, 0, 0, tiled=False).reshape(-1)  22.3 us
    ppermute x18, waiting for transfers between devices, sum_radix4(): r1, r2, r3 = [lax.ppermute(x, axis, perm) for axis, perm in parts]  21.6 us
    dot_general x2, matrix products, left_t(): return jnp.einsum('mdk,mrk->mrd', merged, right_t, precision=MID)  16.7 us
    dot_general x2, matrix products, right_t_of(): return jnp.einsum('mdk,mrd->mrk', merged, left_tr, precision=MID)  14.6 us
    another operation x7, other arithmetic, gram_factor(): return jnp.linalg.cholesky(gram)  12 us
  transfers between devices with their start and end apart: 24, of which 13 were waited for; matrix products, arithmetic and copies ran while one was open for 29% of the time, Pallas kernels for 0%

profile of v5, /device:TPU:0, one launch (start us, length us, event | category | flops | bytes accessed | tf_op | source)
XLA Modules:
  0.0 246.1 jit_solution(6268168570780240302)
XLA Ops:
  7.2 1.6 multiply_subtract_fusion
  9.6 8.4 %fusion.7 = f32[2,2048,32]{1,2,0:T(8,128)S(1)} fusion(f32[2,512,32]{1,2,0:T(8,128)S(1)} %copy-done, f32[1,2,2048,512]{3,2,1,0:T(8,128)} %param.13, bf16[1,2,2048,512]{3,2,1,0:T(8,128)(2,1)} %param.12), kind=kOutput, calls=%fused_computation.12 | convolution fusion | flops 406847488 | bytes 13238272 | tf_op jit(solution)/shard_map/mdk,mrk->mrd/dot_general | solution.py:65
  18.9 25.3 %all_to_all.32 = f32[128,1,1056]{2,1,0:T(1,128)S(1)} all-to-all(f32[128,1,1056]{2,1,0:T(1,128)S(1)} %all_to_all.26), channel_id=1, replica_groups=mesh['dp'=32,'group'=4] {'dp','group'}, dimensions={0} | all-to-all | bytes 1081344 | tf_op jit(solution)/shard_map/all_to_all | solution.py:49
  45.7 4.6 %all-to-all-start.1 = ((f32[128,1,1056]{2,1,0:T(1,128)}), f32[128,1,1056]{2,1,0:T(1,128)S(1)}, u32[]{:S(2)}, u32[]{:S(2)}) async-start(f32[128,1,1056]{2,1,0:T(1,128)} %broadcast_in_dim.14), calls=%async_computation.1 | async-start | bytes 1179648 | tf_op jit(solution)/shard_map/all_to_all | solution.py:52
  50.4 16.4 %all-to-all-done.1 = f32[128,1,1056]{2,1,0:T(1,128)S(1)} async-done(((f32[128,1,1056]{2,1,0:T(1,128)}), f32[128,1,1056]{2,1,0:T(1,128)S(1)}, u32[]{:S(2)}, u32[]{:S(2)}) %all-to-all-start.1) | async-done | bytes 540704 | tf_op jit(solution)/shard_map/all_to_all | solution.py:52
  68.8 7.4 %fusion.6 = f32[2,32,512]{2,1,0:T(8,128)S(1)} fusion(f32[2,32,2048]{2,1,0:T(8,128)S(1)} %reshape.69, f32[1,2,2048,512]{3,2,1,0:T(8,128)} %param.13, bf16[1,2,2048,512]{3,2,1,0:T(8,128)(2,1)} %param.12), kind=kOutput, calls=%fused_computation.11 | convolution fusion | flops 406847488 | bytes 13238272 | tf_op jit(solution)/shard_map/mdk,mrd->mrk/dot_general | solution.py:69
  76.1 1.9 collective-permute-start
  80.7 2.6 %collective-permute-start.1 = (f32[2,32,512]{2,1,0:T(8,128)S(1)}, f32[2,32,512]{2,1,0:T(8,128)S(1)}, u32[]{:S(2)}, u32[]{:S(2)}) collective-permute-start(f32[2,32,512]{2,1,0:T(8,128)S(1)} %add.116), channel_id=1, source_target_pairs={{0,1},{1,0},{2,3},{3,2},{4,5},{5,4},{6,7},{7,6},{8,9},{9,8},{10,11... | collective-permute-start | bytes 393224 | tf_op jit(solution)/shard_map/ppermute | solution.py:42
  83.2 5.9 %custom-call.13 = f32[2,32,32]{2,1,0:T(8,128)S(1)} custom-call(f32[2,32,32]{2,1,0:T(8,128)S(1)} %fusion.24), custom_call_target="Cholesky" | custom-call | tf_op jit(solution)/shard_map/jit(cholesky)/cholesky | solution.py:57
  89.1 3.1 %collective-permute-done.3 = f32[2,32,512]{2,1,0:T(8,128)S(1)} collective-permute-done((f32[2,32,512]{2,1,0:T(8,128)S(1)}, f32[2,32,512]{2,1,0:T(8,128)S(1)}, u32[]{:S(2)}, u32[]{:S(2)}) %collective-permute-start.3) | collective-permute-done | bytes 131104 | tf_op jit(solution)/shard_map/ppermute | solution.py:42
  92.2 3.6 %collective-permute-done.1 = f32[2,32,512]{2,1,0:T(8,128)S(1)} collective-permute-done((f32[2,32,512]{2,1,0:T(8,128)S(1)}, f32[2,32,512]{2,1,0:T(8,128)S(1)}, u32[]{:S(2)}, u32[]{:S(2)}) %collective-permute-start.1) | collective-permute-done | bytes 131104 | tf_op jit(solution)/shard_map/ppermute | solution.py:42
  96.9 3.0 %collective-permute-start.4 = (f32[2,32,512]{2,1,0:T(8,128)S(1)}, f32[2,32,512]{2,1,0:T(8,128)S(1)}, u32[]{:S(2)}, u32[]{:S(2)}) collective-permute-start(f32[2,32,512]{2,1,0:T(8,128)S(1)} %add_add_fusion.3), channel_id=1, source_target_pairs={{0,8},{4,12},{8,0},{12,4},{16,24},{20,28},{24,16},{28,20},{32,40},... | collective-permute-start | bytes 393224 | tf_op jit(solution)/shard_map/ppermute | solution.py:42
  100.1 6.5 %collective-permute-done.6 = f32[2,32,512]{2,1,0:T(8,128)S(1)} collective-permute-done((f32[2,32,512]{2,1,0:T(8,128)S(1)}, f32[2,32,512]{2,1,0:T(8,128)S(1)}, u32[]{:S(2)}, u32[]{:S(2)}) %collective-permute-start.6) | collective-permute-done | bytes 131104 | tf_op jit(solution)/shard_map/ppermute | solution.py:42
  106.6 1.7 collective-permute-start.9
  108.3 1.8 collective-permute-start.8
  110.9 4.9 %custom-call.14 = f32[2,1,32,32]{2,3,1,0:T(8,128)S(1)} custom-call(f32[2,1,32,32]{3,2,1,0:T(8,128)S(1)} %select_bitcast_fusion), custom_call_target="InvertDiagBlocksLowerTriangular" | custom-call | tf_op jit(solution)/shard_map/jit(_solve_triangular)/vmap()/triangular_solve | solution.py:61
  116.9 8.3 %fusion.5 = f32[2,32,2048]{2,1,0:T(8,128)S(1)} fusion(f32[2,32,512]{2,1,0:T(8,128)S(1)} %convolution_multiply_fusion.1, f32[1,2,2048,512]{3,2,1,0:T(8,128)} %param.13, bf16[1,2,2048,512]{3,2,1,0:T(8,128)(2,1)} %param.12), kind=kOutput, calls=%fused_computation.10 | convolution fusion | flops 406847488 | bytes 13238272 | tf_op jit(solution)/shard_map/mdk,mrk->mrd/dot_general | solution.py:65
  125.2 1.4 all_to_all.27
  126.6 6.5 %all-to-all-start.2 = ((f32[128,1,1024]{2,1,0:T(1,128)}), f32[128,1,1024]{2,1,0:T(1,128)S(1)}, u32[]{:S(2)}, u32[]{:S(2)}) async-start(f32[128,1,1024]{2,1,0:T(1,128)} %all_to_all.27), calls=%async_computation.2 | async-start | bytes 1048576 | tf_op jit(solution)/shard_map/all_to_all | solution.py:49
  134.5 11.8 %all-to-all-done.2 = f32[128,1,1024]{2,1,0:T(1,128)S(1)} async-done(((f32[128,1,1024]{2,1,0:T(1,128)}), f32[128,1,1024]{2,1,0:T(1,128)S(1)}, u32[]{:S(2)}, u32[]{:S(2)}) %all-to-all-start.2) | async-done | bytes 524320 | tf_op jit(solution)/shard_map/all_to_all | solution.py:49
  147.7 4.8 %all-to-all-start.3 = ((f32[128,1,1024]{2,1,0:T(1,128)}), f32[128,1,1024]{2,1,0:T(1,128)S(1)}, u32[]{:S(2)}, u32[]{:S(2)}) async-start(f32[128,1,1024]{2,1,0:T(1,128)} %broadcast_in_dim.15), calls=%async_computation.3 | async-start | bytes 1048576 | tf_op jit(solution)/shard_map/all_to_all | solution.py:52
  159.6 5.9 %all-to-all-done.3 = f32[128,1,1024]{2,1,0:T(1,128)S(1)} async-done(((f32[128,1,1024]{2,1,0:T(1,128)}), f32[128,1,1024]{2,1,0:T(1,128)S(1)}, u32[]{:S(2)}, u32[]{:S(2)}) %all-to-all-start.3) | async-done | bytes 524320 | tf_op jit(solution)/shard_map/all_to_all | solution.py:52
  167.6 7.2 %fusion.4 = f32[2,32,512]{2,1,0:T(8,128)S(1)} fusion(f32[2,32,2048]{2,1,0:T(8,128)S(1)} %reshape_reshape.4, f32[1,2,2048,512]{3,2,1,0:T(8,128)} %param.13, bf16[1,2,2048,512]{3,2,1,0:T(8,128)(2,1)} %param.12), kind=kOutput, calls=%fused_computation.9 | convolution fusion | flops 406847488 | bytes 13238272 | tf_op jit(solution)/shard_map/mdk,mrd->mrk/dot_general | solution.py:69
  175.3 5.9 %custom-call.15 = f32[2,32,32]{2,1,0:T(8,128)S(1)} custom-call(f32[2,32,32]{2,1,0:T(8,128)S(1)} %fusion.22), custom_call_target="Cholesky" | custom-call | tf_op jit(solution)/shard_map/jit(cholesky)/cholesky | solution.py:57
  181.2 1.4 collective-permute-start.13
  183.9 1.4 collective-permute-start.11
  185.5 5.3 %collective-permute-done.13 = f32[2,32,512]{2,1,0:T(8,128)S(1)} collective-permute-done((f32[2,32,512]{2,1,0:T(8,128)S(1)}, f32[2,32,512]{2,1,0:T(8,128)S(1)}, u32[]{:S(2)}, u32[]{:S(2)}) %collective-permute-start.13) | collective-permute-done | bytes 131104 | tf_op jit(solution)/shard_map/ppermute | solution.py:42
  192.6 1.9 collective-permute-start.15
  195.8 4.9 %custom-call.10 = f32[2,1,32,32]{2,3,1,0:T(8,128)S(1)} custom-call(f32[2,1,32,32]{3,2,1,0:T(8,128)S(1)} %fusion.25), custom_call_target="InvertDiagBlocksLowerTriangular" | custom-call | tf_op jit(solution)/shard_map/jit(_solve_triangular)/vmap()/triangular_solve | solution.py:61
  201.9 1.6 collective-permute-start.18
  205.6 2.0 copy.42
  212.2 27.0 %shard_map.128 = (f32[2,2048,512]{2,1,0:T(8,128)}, bf16[2,2048,512]{2,1,0:T(8,128)(2,1)}) custom-call(s32[128]{0:T(128)} %add_clamp_fusion.table, bf16[2,2048,512]{2,1,0:T(8,128)(2,1)} %bitcast.104, f32[2,2048,512]{2,1,0:T(8,128)} %bitcast.103, f32[2,2048,32]{2,1,0:T(8,128)} %bitcast.106, f32[2,32,512]{2,1,0:T(8,128)} %copy-done.1, f32[256,32,512]{2,1,0:T(8,128)} %bitcast.105), custom_call_target="tpu_custom_call" | custom-call | flops 134217728 | bytes 33554432 | tf_op jit(solution)/shard_map/pallas_call | solution.py:121
  (88 shorter events, 30.6 us)
Async XLA Ops:
  7.2 2.4 copy-start
  7.2 205.0 %all-gather.2.cloned.1.call-start = ((), (), s32[]{:S(2)}) async-start(), calls=%async_computation.4 | async-start | bytes 16908288 | tf_op jit(solution)/shard_map/all_gather | solution.py:150
  45.7 21.0 %all-to-all-start.1 = ((f32[128,1,1056]{2,1,0:T(1,128)}), f32[128,1,1056]{2,1,0:T(1,128)S(1)}, u32[]{:S(2)}, u32[]{:S(2)}) async-start(f32[128,1,1056]{2,1,0:T(1,128)} %broadcast_in_dim.14), calls=%async_computation.1 | async-start | bytes 1179648 | tf_op jit(solution)/shard_map/all_to_all | solution.py:52
  76.1 2.9 %collective-permute-start = (f32[2,32,512]{2,1,0:T(8,128)S(1)}, f32[2,32,512]{2,1,0:T(8,128)S(1)}, u32[]{:S(2)}, u32[]{:S(2)}) collective-permute-start(f32[2,32,512]{2,1,0:T(8,128)S(1)} %fusion.6), channel_id=1, source_target_pairs={{0,4},{4,0},{8,12},{12,8},{16,20},{20,16},{24,28},{28,24},{32,36},... | collective-permute-start | bytes 393224 | tf_op jit(solution)/shard_map/ppermute | solution.py:40
  79.1 13.1 %collective-permute-start.3 = (f32[2,32,512]{2,1,0:T(8,128)S(1)}, f32[2,32,512]{2,1,0:T(8,128)S(1)}, u32[]{:S(2)}, u32[]{:S(2)}) collective-permute-start(f32[2,32,512]{2,1,0:T(8,128)S(1)} %add.116), channel_id=1, source_target_pairs={{0,3},{1,2},{2,1},{3,0},{4,7},{5,6},{6,5},{7,4},{8,11},{9,10},{10,... | collective-permute-start | bytes 393224 | tf_op jit(solution)/shard_map/ppermute | solution.py:42
  79.9 12.2 %collective-permute-start.2 = (f32[2,32,512]{2,1,0:T(8,128)S(1)}, f32[2,32,512]{2,1,0:T(8,128)S(1)}, u32[]{:S(2)}, u32[]{:S(2)}) collective-permute-start(f32[2,32,512]{2,1,0:T(8,128)S(1)} %add.116), channel_id=1, source_target_pairs={{0,2},{1,3},{2,0},{3,1},{4,6},{5,7},{6,4},{7,5},{8,10},{9,11},{10,... | collective-permute-start | bytes 393224 | tf_op jit(solution)/shard_map/ppermute | solution.py:42
  80.7 15.1 %collective-permute-start.1 = (f32[2,32,512]{2,1,0:T(8,128)S(1)}, f32[2,32,512]{2,1,0:T(8,128)S(1)}, u32[]{:S(2)}, u32[]{:S(2)}) collective-permute-start(f32[2,32,512]{2,1,0:T(8,128)S(1)} %add.116), channel_id=1, source_target_pairs={{0,1},{1,0},{2,3},{3,2},{4,5},{5,4},{6,7},{7,6},{8,9},{9,8},{10,11... | collective-permute-start | bytes 393224 | tf_op jit(solution)/shard_map/ppermute | solution.py:42
  95.8 37.3 %copy-start.5 = (s32[128]{0:T(128)S(1)}, s32[128]{0:T(128)}, u32[]{:S(2)}) copy-start(s32[128]{0:T(128)} %param.18) | copy-start | bytes 1540
  95.8 10.8 %collective-permute-start.6 = (f32[2,32,512]{2,1,0:T(8,128)S(1)}, f32[2,32,512]{2,1,0:T(8,128)S(1)}, u32[]{:S(2)}, u32[]{:S(2)}) collective-permute-start(f32[2,32,512]{2,1,0:T(8,128)S(1)} %add_add_fusion.3), channel_id=1, source_target_pairs={{0,24},{4,28},{8,16},{12,20},{16,8},{20,12},{24,0},{28,4},{32,56},... | collective-permute-start | bytes 393224 | tf_op jit(solution)/shard_map/ppermute | solution.py:42
  95.9 10.7 %collective-permute-start.5 = (f32[2,32,512]{2,1,0:T(8,128)S(1)}, f32[2,32,512]{2,1,0:T(8,128)S(1)}, u32[]{:S(2)}, u32[]{:S(2)}) collective-permute-start(f32[2,32,512]{2,1,0:T(8,128)S(1)} %add_add_fusion.3), channel_id=1, source_target_pairs={{0,16},{4,20},{8,24},{12,28},{16,0},{20,4},{24,8},{28,12},{32,48},... | collective-permute-start | bytes 393224 | tf_op jit(solution)/shard_map/ppermute | solution.py:42
  96.9 9.7 %collective-permute-start.4 = (f32[2,32,512]{2,1,0:T(8,128)S(1)}, f32[2,32,512]{2,1,0:T(8,128)S(1)}, u32[]{:S(2)}, u32[]{:S(2)}) collective-permute-start(f32[2,32,512]{2,1,0:T(8,128)S(1)} %add_add_fusion.3), channel_id=1, source_target_pairs={{0,8},{4,12},{8,0},{12,4},{16,24},{20,28},{24,16},{28,20},{32,40},... | collective-permute-start | bytes 393224 | tf_op jit(solution)/shard_map/ppermute | solution.py:42
  106.6 9.3 %collective-permute-start.9 = (f32[2,32,512]{2,1,0:T(8,128)S(1)}, f32[2,32,512]{2,1,0:T(8,128)S(1)}, u32[]{:S(2)}, u32[]{:S(2)}) collective-permute-start(f32[2,32,512]{2,1,0:T(8,128)S(1)} %add_add_fusion.2), channel_id=1, source_target_pairs={{0,96},{4,100},{8,104},{12,108},{16,112},{20,116},{24,120},{28,124... | collective-permute-start | bytes 393224 | tf_op jit(solution)/shard_map/ppermute | solution.py:42
  108.3 7.6 %collective-permute-start.8 = (f32[2,32,512]{2,1,0:T(8,128)S(1)}, f32[2,32,512]{2,1,0:T(8,128)S(1)}, u32[]{:S(2)}, u32[]{:S(2)}) collective-permute-start(f32[2,32,512]{2,1,0:T(8,128)S(1)} %add_add_fusion.2), channel_id=1, source_target_pairs={{0,64},{4,68},{8,72},{12,76},{16,80},{20,84},{24,88},{28,92},{32,9... | collective-permute-start | bytes 393224 | tf_op jit(solution)/shard_map/ppermute | solution.py:42
  110.1 6.4 %collective-permute-start.7 = (f32[2,32,512]{2,1,0:T(8,128)S(1)}, f32[2,32,512]{2,1,0:T(8,128)S(1)}, u32[]{:S(2)}, u32[]{:S(2)}) collective-permute-start(f32[2,32,512]{2,1,0:T(8,128)S(1)} %add_add_fusion.2), channel_id=1, source_target_pairs={{0,32},{4,36},{8,40},{12,44},{16,48},{20,52},{24,56},{28,60},{32,0... | collective-permute-start | bytes 393224 | tf_op jit(solution)/shard_map/ppermute | solution.py:42
  116.9 42.1 %copy-start.3 = (f32[2,2048]{1,0:T(2,128)S(1)}, f32[2,2048]{1,0:T(2,128)}, u32[]{:S(2)}) copy-start(f32[2,2048]{1,0:T(2,128)} %param.16) | copy-start | bytes 49156
  116.9 42.1 %copy-start.4 = (f32[2,2048]{1,0:T(2,128)S(1)}, f32[2,2048]{1,0:T(2,128)}, u32[]{:S(2)}) copy-start(f32[2,2048]{1,0:T(2,128)} %param.17) | copy-start | bytes 49156
  126.6 19.7 %all-to-all-start.2 = ((f32[128,1,1024]{2,1,0:T(1,128)}), f32[128,1,1024]{2,1,0:T(1,128)S(1)}, u32[]{:S(2)}, u32[]{:S(2)}) async-start(f32[128,1,1024]{2,1,0:T(1,128)} %all_to_all.27), calls=%async_computation.2 | async-start | bytes 1048576 | tf_op jit(solution)/shard_map/all_to_all | solution.py:49
  147.7 17.8 %all-to-all-start.3 = ((f32[128,1,1024]{2,1,0:T(1,128)}), f32[128,1,1024]{2,1,0:T(1,128)S(1)}, u32[]{:S(2)}, u32[]{:S(2)}) async-start(f32[128,1,1024]{2,1,0:T(1,128)} %broadcast_in_dim.15), calls=%async_computation.3 | async-start | bytes 1048576 | tf_op jit(solution)/shard_map/all_to_all | solution.py:52
  167.6 42.0 %copy-start.2 = (f32[1,2,32,512]{3,2,1,0:T(8,128)S(1)}, f32[1,2,32,512]{3,2,1,0:T(8,128)}, u32[]{:S(2)}) copy-start(f32[1,2,32,512]{3,2,1,0:T(8,128)} %param.20) | copy-start | bytes 393220
  174.8 6.3 %collective-permute-start.10 = (f32[2,32,512]{2,1,0:T(8,128)S(1)}, f32[2,32,512]{2,1,0:T(8,128)S(1)}, u32[]{:S(2)}, u32[]{:S(2)}) collective-permute-start(f32[2,32,512]{2,1,0:T(8,128)S(1)} %fusion.4), channel_id=1, source_target_pairs={{0,4},{4,0},{8,12},{12,8},{16,20},{20,16},{24,28},{28,24},{32,36},... | collective-permute-start | bytes 393224 | tf_op jit(solution)/shard_map/ppermute | solution.py:40
  181.2 9.6 %collective-permute-start.13 = (f32[2,32,512]{2,1,0:T(8,128)S(1)}, f32[2,32,512]{2,1,0:T(8,128)S(1)}, u32[]{:S(2)}, u32[]{:S(2)}) collective-permute-start(f32[2,32,512]{2,1,0:T(8,128)S(1)} %add.126), channel_id=1, source_target_pairs={{0,3},{1,2},{2,1},{3,0},{4,7},{5,6},{6,5},{7,4},{8,11},{9,10},{10,... | collective-permute-start | bytes 393224 | tf_op jit(solution)/shard_map/ppermute | solution.py:42
  182.6 8.2 %collective-permute-start.12 = (f32[2,32,512]{2,1,0:T(8,128)S(1)}, f32[2,32,512]{2,1,0:T(8,128)S(1)}, u32[]{:S(2)}, u32[]{:S(2)}) collective-permute-start(f32[2,32,512]{2,1,0:T(8,128)S(1)} %add.126), channel_id=1, source_target_pairs={{0,2},{1,3},{2,0},{3,1},{4,6},{5,7},{6,4},{7,5},{8,10},{9,11},{10,... | collective-permute-start | bytes 393224 | tf_op jit(solution)/shard_map/ppermute | solution.py:42
  183.9 7.5 %collective-permute-start.11 = (f32[2,32,512]{2,1,0:T(8,128)S(1)}, f32[2,32,512]{2,1,0:T(8,128)S(1)}, u32[]{:S(2)}, u32[]{:S(2)}) collective-permute-start(f32[2,32,512]{2,1,0:T(8,128)S(1)} %add.126), channel_id=1, source_target_pairs={{0,1},{1,0},{2,3},{3,2},{4,5},{5,4},{6,7},{7,6},{8,9},{9,8},{10,11... | collective-permute-start | bytes 393224 | tf_op jit(solution)/shard_map/ppermute | solution.py:42
  191.5 9.2 %collective-permute-start.16 = (f32[2,32,512]{2,1,0:T(8,128)S(1)}, f32[2,32,512]{2,1,0:T(8,128)S(1)}, u32[]{:S(2)}, u32[]{:S(2)}) collective-permute-start(f32[2,32,512]{2,1,0:T(8,128)S(1)} %add_add_fusion.1), channel_id=1, source_target_pairs={{0,24},{4,28},{8,16},{12,20},{16,8},{20,12},{24,0},{28,4},{32,56},... | collective-permute-start | bytes 393224 | tf_op jit(solution)/shard_map/ppermute | solution.py:42
  192.6 8.1 %collective-permute-start.15 = (f32[2,32,512]{2,1,0:T(8,128)S(1)}, f32[2,32,512]{2,1,0:T(8,128)S(1)}, u32[]{:S(2)}, u32[]{:S(2)}) collective-permute-start(f32[2,32,512]{2,1,0:T(8,128)S(1)} %add_add_fusion.1), channel_id=1, source_target_pairs={{0,16},{4,20},{8,24},{12,28},{16,0},{20,4},{24,8},{28,12},{32,48},... | collective-permute-start | bytes 393224 | tf_op jit(solution)/shard_map/ppermute | solution.py:42
  194.5 6.2 %collective-permute-start.14 = (f32[2,32,512]{2,1,0:T(8,128)S(1)}, f32[2,32,512]{2,1,0:T(8,128)S(1)}, u32[]{:S(2)}, u32[]{:S(2)}) collective-permute-start(f32[2,32,512]{2,1,0:T(8,128)S(1)} %add_add_fusion.1), channel_id=1, source_target_pairs={{0,8},{4,12},{8,0},{12,4},{16,24},{20,28},{24,16},{28,20},{32,40},... | collective-permute-start | bytes 393224 | tf_op jit(solution)/shard_map/ppermute | solution.py:42
  200.7 6.8 %collective-permute-start.19 = (f32[2,32,512]{2,1,0:T(8,128)S(1)}, f32[2,32,512]{2,1,0:T(8,128)S(1)}, u32[]{:S(2)}, u32[]{:S(2)}) collective-permute-start(f32[2,32,512]{2,1,0:T(8,128)S(1)} %add_add_fusion), channel_id=1, source_target_pairs={{0,96},{4,100},{8,104},{12,108},{16,112},{20,116},{24,120},{28,124... | collective-permute-start | bytes 393224 | tf_op jit(solution)/shard_map/ppermute | solution.py:42
  201.9 6.5 %collective-permute-start.18 = (f32[2,32,512]{2,1,0:T(8,128)S(1)}, f32[2,32,512]{2,1,0:T(8,128)S(1)}, u32[]{:S(2)}, u32[]{:S(2)}) collective-permute-start(f32[2,32,512]{2,1,0:T(8,128)S(1)} %add_add_fusion), channel_id=1, source_target_pairs={{0,64},{4,68},{8,72},{12,76},{16,80},{20,84},{24,88},{28,92},{32,9... | collective-permute-start | bytes 393224 | tf_op jit(solution)/shard_map/ppermute | solution.py:42
  203.5 5.7 %collective-permute-start.17 = (f32[2,32,512]{2,1,0:T(8,128)S(1)}, f32[2,32,512]{2,1,0:T(8,128)S(1)}, u32[]{:S(2)}, u32[]{:S(2)}) collective-permute-start(f32[2,32,512]{2,1,0:T(8,128)S(1)} %add_add_fusion), channel_id=1, source_target_pairs={{0,32},{4,36},{8,40},{12,44},{16,48},{20,52},{24,56},{28,60},{32,0... | collective-permute-start | bytes 393224 | tf_op jit(solution)/shard_map/ppermute | solution.py:42
  209.6 2.6 %copy-start.1 = (f32[2,32,512]{2,1,0:T(8,128)}, f32[2,32,512]{2,1,0:T(8,128)S(1)}, u32[]{:S(2)}) copy-start(f32[2,32,512]{2,1,0:T(8,128)S(1)} %convolution_multiply_fusion.right_t) | copy-start | bytes 393220
Sparse Core Ops, SparseCore 0:
  11.7 96.3 all-gather.1

commit v6 on v5

--- a/solution.py
+++ b/solution.py
@@ -69,35 +69,41 @@
     return jnp.einsum("mdk,mrd->mrk", merged, left_tr, precision=MID)
 
 
-TAIL_ROWS = 256
+TAIL_ROWS = 512
 
 
 def tail_kernel(table, grads, errs, left_rows, right_t, carried, out_err, out_w, cbuf, sems):
     m = pl.program_id(0)
     i = pl.program_id(1)
-    per_block = cbuf.shape[0]
+    pieces = cbuf.shape[0]
     piece_rows = cbuf.shape[1]
     blocks = pl.num_programs(1)
-    base = (m * blocks + i) * per_block
-    copies = []
-    for p in range(per_block):
-        cp = pltpu.make_async_copy(carried.at[table[base + p]], cbuf.at[p], sems.at[p])
-        cp.start()
-        copies.append(cp)
+    per_block = out_w.shape[1] // piece_rows
+
+    def piece_copy(j):
+        return pltpu.make_async_copy(carried.at[table[j]], cbuf.at[j], sems.at[j])
+
+    @pl.when((m == 0) & (i == 0))
+    def _():
+        for j in range(pieces):
+            piece_copy(j).start()
+
     upd = jnp.dot(left_rows[0], right_t[0], precision=HI, preferred_element_type=jnp.float32)
     merged = grads[0].astype(jnp.float32) + errs[0]
     out_err[0] = merged - upd
+    base = (m * blocks + i) * per_block
     for p in range(per_block):
-        copies[p].wait()
+        piece_copy(base + p).wait()
+    for p in range(per_block):
         rows = slice(p * piece_rows, (p + 1) * piece_rows)
-        out_w[0, rows, :] = (cbuf[p] - step_rate * upd[rows, :]).astype(out_w.dtype)
+        out_w[0, rows, :] = (cbuf[base + p] - step_rate * upd[rows, :]).astype(out_w.dtype)
 
 
 def tail(table, grads, errs, left_rows, right_t, carried):
     mats, dw, kv = grads.shape
     rank = left_rows.shape[2]
     piece_rows = carried.shape[1]
-    per_block = TAIL_ROWS // piece_rows
+    pieces = mats * dw // piece_rows
     grid = (mats, dw // TAIL_ROWS)
     row_spec = pl.BlockSpec((1, TAIL_ROWS, kv), lambda m, i, t: (m, i, 0))
     spec = pltpu.PrefetchScalarGridSpec(
@@ -112,8 +118,8 @@
         ],
         out_specs=[row_spec, row_spec],
         scratch_shapes=[
-            pltpu.VMEM((per_block, piece_rows, kv), jnp.float32),
-            pltpu.SemaphoreType.DMA((per_block,)),
+            pltpu.VMEM((pieces, piece_rows, kv), jnp.float32),
+            pltpu.SemaphoreType.DMA((pieces,)),
         ],
     )
     elems = mats * dw * kv
@@ -126,6 +132,9 @@
             jax.ShapeDtypeStruct((mats, dw, kv), jnp.bfloat16),
         ],
         cost_estimate=cost,
+        compiler_params=pltpu.CompilerParams(
+            dimension_semantics=("arbitrary", "arbitrary"), vmem_limit_bytes=48 * 1024 * 1024
+        ),
     )(table, grads, errs, left_rows, right_t, carried)
 
 

time: 247 us -> 238 us (0.964)
  Pallas kernels: 27 us -> 17.7 us
    pallas_call x1, Pallas kernels: 27 us -> 17.7 us  [tail(): pl.pallas_call(tail_kernel, grid_spec=spec, out_shape=[jax.ShapeDtypeStru...]
where the time goes in v6:
time: 238 us
  waiting for transfers between devices  57.7 us (24%)
  starting transfers between devices  43.5 us (18%)
  matrix products  36.4 us (15%)
  other arithmetic  30 us (13%)
  blocking collectives  25.3 us (11%)
  between operations  19.7 us (8%)
  Pallas kernels  17.7 us (7%)
  local copies, waits for them, and re-layouts  7.29 us (3%)
    all_to_all x1, blocking collectives, sum_all_to_all(): rows = lax.all_to_all(x.reshape(count, -1), axes, 0, 0, tiled=False)  25.3 us
    ppermute x18, starting transfers between devices, sum_radix4(): r1, r2, r3 = [lax.ppermute(x, axis, perm) for axis, perm in parts]  25 us
    ppermute x18, waiting for transfers between devices, sum_radix4(): r1, r2, r3 = [lax.ppermute(x, axis, perm) for axis, perm in parts]  22.7 us
    all_to_all x2, waiting for transfers between devices, sum_all_to_all(): return lax.all_to_all(spread, axes, 0, 0, tiled=False).reshape(-1)  22.3 us
    pallas_call x1, Pallas kernels, tail(): pl.pallas_call(tail_kernel, grid_spec=spec, out_shape=[jax.ShapeDtypeStru...  17.7 us
    dot_general x2, matrix products, left_t(): return jnp.einsum('mdk,mrk->mrd', merged, right_t, precision=MID)  16.7 us
    dot_general x2, matrix products, right_t_of(): return jnp.einsum('mdk,mrd->mrk', merged, left_tr, precision=MID)  14.6 us
    all_to_all x1, waiting for transfers between devices, sum_all_to_all(): rows = lax.all_to_all(x.reshape(count, -1), axes, 0, 0, tiled=False)  12.3 us
  transfers between devices with their start and end apart: 24, of which 13 were waited for; matrix products, arithmetic and copies ran while one was open for 29% of the time, Pallas kernels for 0%

profile of v6, /device:TPU:0, one launch (start us, length us, event | category | flops | bytes accessed | tf_op | source)
XLA Modules:
  0.0 237.6 jit_solution(1172022239491985759)
XLA Ops:
  7.2 1.6 multiply_subtract_fusion
  9.6 8.4 %fusion.7 = f32[2,2048,32]{1,2,0:T(8,128)S(1)} fusion(f32[2,512,32]{1,2,0:T(8,128)S(1)} %copy-done, f32[1,2,2048,512]{3,2,1,0:T(8,128)} %param.13, bf16[1,2,2048,512]{3,2,1,0:T(8,128)(2,1)} %param.12), kind=kOutput, calls=%fused_computation.12 | convolution fusion | flops 406847488 | bytes 13238272 | tf_op jit(solution)/shard_map/mdk,mrk->mrd/dot_general | solution.py:65
  18.9 25.3 %all_to_all.32 = f32[128,1,1056]{2,1,0:T(1,128)S(1)} all-to-all(f32[128,1,1056]{2,1,0:T(1,128)S(1)} %all_to_all.26), channel_id=1, replica_groups=mesh['dp'=32,'group'=4] {'dp','group'}, dimensions={0} | all-to-all | bytes 1081344 | tf_op jit(solution)/shard_map/all_to_all | solution.py:49
  45.7 4.6 %all-to-all-start.1 = ((f32[128,1,1056]{2,1,0:T(1,128)}), f32[128,1,1056]{2,1,0:T(1,128)S(1)}, u32[]{:S(2)}, u32[]{:S(2)}) async-start(f32[128,1,1056]{2,1,0:T(1,128)} %broadcast_in_dim.14), calls=%async_computation.1 | async-start | bytes 1179648 | tf_op jit(solution)/shard_map/all_to_all | solution.py:52
  50.4 16.4 %all-to-all-done.1 = f32[128,1,1056]{2,1,0:T(1,128)S(1)} async-done(((f32[128,1,1056]{2,1,0:T(1,128)}), f32[128,1,1056]{2,1,0:T(1,128)S(1)}, u32[]{:S(2)}, u32[]{:S(2)}) %all-to-all-start.1) | async-done | bytes 540704 | tf_op jit(solution)/shard_map/all_to_all | solution.py:52
  66.7 1.4 reduce.6
  68.8 7.4 %fusion.6 = f32[2,32,512]{2,1,0:T(8,128)S(1)} fusion(f32[2,32,2048]{2,1,0:T(8,128)S(1)} %reshape.69, f32[1,2,2048,512]{3,2,1,0:T(8,128)} %param.13, bf16[1,2,2048,512]{3,2,1,0:T(8,128)(2,1)} %param.12), kind=kOutput, calls=%fused_computation.11 | convolution fusion | flops 406847488 | bytes 13238272 | tf_op jit(solution)/shard_map/mdk,mrd->mrk/dot_general | solution.py:69
  76.2 1.9 collective-permute-start
  80.7 2.6 %collective-permute-start.1 = (f32[2,32,512]{2,1,0:T(8,128)S(1)}, f32[2,32,512]{2,1,0:T(8,128)S(1)}, u32[]{:S(2)}, u32[]{:S(2)}) collective-permute-start(f32[2,32,512]{2,1,0:T(8,128)S(1)} %add.116), channel_id=1, source_target_pairs={{0,1},{1,0},{2,3},{3,2},{4,5},{5,4},{6,7},{7,6},{8,9},{9,8},{10,11... | collective-permute-start | bytes 393224 | tf_op jit(solution)/shard_map/ppermute | solution.py:42
  83.4 5.9 %custom-call.13 = f32[2,32,32]{2,1,0:T(8,128)S(1)} custom-call(f32[2,32,32]{2,1,0:T(8,128)S(1)} %fusion.24), custom_call_target="Cholesky" | custom-call | tf_op jit(solution)/shard_map/jit(cholesky)/cholesky | solution.py:57
  89.2 3.1 %collective-permute-done.3 = f32[2,32,512]{2,1,0:T(8,128)S(1)} collective-permute-done((f32[2,32,512]{2,1,0:T(8,128)S(1)}, f32[2,32,512]{2,1,0:T(8,128)S(1)}, u32[]{:S(2)}, u32[]{:S(2)}) %collective-permute-start.3) | collective-permute-done | bytes 131104 | tf_op jit(solution)/shard_map/ppermute | solution.py:42
  92.3 3.6 %collective-permute-done.1 = f32[2,32,512]{2,1,0:T(8,128)S(1)} collective-permute-done((f32[2,32,512]{2,1,0:T(8,128)S(1)}, f32[2,32,512]{2,1,0:T(8,128)S(1)}, u32[]{:S(2)}, u32[]{:S(2)}) %collective-permute-start.1) | collective-permute-done | bytes 131104 | tf_op jit(solution)/shard_map/ppermute | solution.py:42
  97.0 3.1 %collective-permute-start.4 = (f32[2,32,512]{2,1,0:T(8,128)S(1)}, f32[2,32,512]{2,1,0:T(8,128)S(1)}, u32[]{:S(2)}, u32[]{:S(2)}) collective-permute-start(f32[2,32,512]{2,1,0:T(8,128)S(1)} %add_add_fusion.3), channel_id=1, source_target_pairs={{0,8},{4,12},{8,0},{12,4},{16,24},{20,28},{24,16},{28,20},{32,40},... | collective-permute-start | bytes 393224 | tf_op jit(solution)/shard_map/ppermute | solution.py:42
  100.2 6.4 %collective-permute-done.6 = f32[2,32,512]{2,1,0:T(8,128)S(1)} collective-permute-done((f32[2,32,512]{2,1,0:T(8,128)S(1)}, f32[2,32,512]{2,1,0:T(8,128)S(1)}, u32[]{:S(2)}, u32[]{:S(2)}) %collective-permute-start.6) | collective-permute-done | bytes 131104 | tf_op jit(solution)/shard_map/ppermute | solution.py:42
  106.6 1.7 collective-permute-start.9
  108.4 1.7 collective-permute-start.8
  110.9 4.9 %custom-call.14 = f32[2,1,32,32]{2,3,1,0:T(8,128)S(1)} custom-call(f32[2,1,32,32]{3,2,1,0:T(8,128)S(1)} %select_bitcast_fusion), custom_call_target="InvertDiagBlocksLowerTriangular" | custom-call | tf_op jit(solution)/shard_map/jit(_solve_triangular)/vmap()/triangular_solve | solution.py:61
  116.8 8.3 %fusion.5 = f32[2,32,2048]{2,1,0:T(8,128)S(1)} fusion(f32[2,32,512]{2,1,0:T(8,128)S(1)} %convolution_multiply_fusion.1, f32[1,2,2048,512]{3,2,1,0:T(8,128)} %param.13, bf16[1,2,2048,512]{3,2,1,0:T(8,128)(2,1)} %param.12), kind=kOutput, calls=%fused_computation.10 | convolution fusion | flops 406847488 | bytes 13238272 | tf_op jit(solution)/shard_map/mdk,mrk->mrd/dot_general | solution.py:65
  125.1 1.4 all_to_all.27
  126.5 6.6 %all-to-all-start.2 = ((f32[128,1,1024]{2,1,0:T(1,128)}), f32[128,1,1024]{2,1,0:T(1,128)S(1)}, u32[]{:S(2)}, u32[]{:S(2)}) async-start(f32[128,1,1024]{2,1,0:T(1,128)} %all_to_all.27), calls=%async_computation.2 | async-start | bytes 1048576 | tf_op jit(solution)/shard_map/all_to_all | solution.py:49
  134.0 12.3 %all-to-all-done.2 = f32[128,1,1024]{2,1,0:T(1,128)S(1)} async-done(((f32[128,1,1024]{2,1,0:T(1,128)}), f32[128,1,1024]{2,1,0:T(1,128)S(1)}, u32[]{:S(2)}, u32[]{:S(2)}) %all-to-all-start.2) | async-done | bytes 524320 | tf_op jit(solution)/shard_map/all_to_all | solution.py:49
  147.8 4.8 %all-to-all-start.3 = ((f32[128,1,1024]{2,1,0:T(1,128)}), f32[128,1,1024]{2,1,0:T(1,128)S(1)}, u32[]{:S(2)}, u32[]{:S(2)}) async-start(f32[128,1,1024]{2,1,0:T(1,128)} %broadcast_in_dim.15), calls=%async_computation.3 | async-start | bytes 1048576 | tf_op jit(solution)/shard_map/all_to_all | solution.py:52
  159.7 5.9 %all-to-all-done.3 = f32[128,1,1024]{2,1,0:T(1,128)S(1)} async-done(((f32[128,1,1024]{2,1,0:T(1,128)}), f32[128,1,1024]{2,1,0:T(1,128)S(1)}, u32[]{:S(2)}, u32[]{:S(2)}) %all-to-all-start.3) | async-done | bytes 524320 | tf_op jit(solution)/shard_map/all_to_all | solution.py:52
  167.7 7.2 %fusion.4 = f32[2,32,512]{2,1,0:T(8,128)S(1)} fusion(f32[2,32,2048]{2,1,0:T(8,128)S(1)} %reshape_reshape.4, f32[1,2,2048,512]{3,2,1,0:T(8,128)} %param.13, bf16[1,2,2048,512]{3,2,1,0:T(8,128)(2,1)} %param.12), kind=kOutput, calls=%fused_computation.9 | convolution fusion | flops 406847488 | bytes 13238272 | tf_op jit(solution)/shard_map/mdk,mrd->mrk/dot_general | solution.py:69
  175.4 5.9 %custom-call.15 = f32[2,32,32]{2,1,0:T(8,128)S(1)} custom-call(f32[2,32,32]{2,1,0:T(8,128)S(1)} %fusion.22), custom_call_target="Cholesky" | custom-call | tf_op jit(solution)/shard_map/jit(cholesky)/cholesky | solution.py:57
  181.3 1.4 collective-permute-start.13
  184.0 1.4 collective-permute-start.11
  185.6 5.3 %collective-permute-done.13 = f32[2,32,512]{2,1,0:T(8,128)S(1)} collective-permute-done((f32[2,32,512]{2,1,0:T(8,128)S(1)}, f32[2,32,512]{2,1,0:T(8,128)S(1)}, u32[]{:S(2)}, u32[]{:S(2)}) %collective-permute-start.13) | collective-permute-done | bytes 131104 | tf_op jit(solution)/shard_map/ppermute | solution.py:42
  192.7 1.9 collective-permute-start.15
  195.9 4.9 %custom-call.10 = f32[2,1,32,32]{2,3,1,0:T(8,128)S(1)} custom-call(f32[2,1,32,32]{3,2,1,0:T(8,128)S(1)} %fusion.25), custom_call_target="InvertDiagBlocksLowerTriangular" | custom-call | tf_op jit(solution)/shard_map/jit(_solve_triangular)/vmap()/triangular_solve | solution.py:61
  202.1 1.6 collective-permute-start.18
  213.0 17.7 %shard_map.128 = (f32[2,2048,512]{2,1,0:T(8,128)}, bf16[2,2048,512]{2,1,0:T(8,128)(2,1)}) custom-call(s32[128]{0:T(128)S(1)} %add_clamp_fusion.table, bf16[2,2048,512]{2,1,0:T(8,128)(2,1)} %bitcast.105, f32[2,2048,512]{2,1,0:T(8,128)} %bitcast.104, f32[2,2048,32]{2,1,0:T(8,128)S(1)} %bitcast.103, f32[2,32,512]{2,1,0:T(8,128)S(1)} %convolution_multiply_fusion.right_t, ...), custom_call_target="tpu_custom_call" | custom-call | flops 134217728 | bytes 33554432 | tf_op jit(solution)/shard_map/pallas_call | solution.py:127
  (88 shorter events, 31.2 us)
Async XLA Ops:
  7.2 2.4 %copy-start = (f32[2,512,32]{1,2,0:T(8,128)S(1)}, f32[2,512,32]{1,2,0:T(8,128)}, u32[]{:S(2)}) copy-start(f32[2,512,32]{1,2,0:T(8,128)} %param.14) | copy-start | bytes 393220
  7.2 205.9 %all-gather.2.cloned.1.call-start = ((), (), s32[]{:S(2)}) async-start(), calls=%async_computation.4 | async-start | bytes 16908288 | tf_op jit(solution)/shard_map/all_gather | solution.py:159
  45.7 21.0 %all-to-all-start.1 = ((f32[128,1,1056]{2,1,0:T(1,128)}), f32[128,1,1056]{2,1,0:T(1,128)S(1)}, u32[]{:S(2)}, u32[]{:S(2)}) async-start(f32[128,1,1056]{2,1,0:T(1,128)} %broadcast_in_dim.14), calls=%async_computation.1 | async-start | bytes 1179648 | tf_op jit(solution)/shard_map/all_to_all | solution.py:52
  76.2 2.9 %collective-permute-start = (f32[2,32,512]{2,1,0:T(8,128)S(1)}, f32[2,32,512]{2,1,0:T(8,128)S(1)}, u32[]{:S(2)}, u32[]{:S(2)}) collective-permute-start(f32[2,32,512]{2,1,0:T(8,128)S(1)} %fusion.6), channel_id=1, source_target_pairs={{0,4},{4,0},{8,12},{12,8},{16,20},{20,16},{24,28},{28,24},{32,36},... | collective-permute-start | bytes 393224 | tf_op jit(solution)/shard_map/ppermute | solution.py:40
  79.2 13.1 %collective-permute-start.3 = (f32[2,32,512]{2,1,0:T(8,128)S(1)}, f32[2,32,512]{2,1,0:T(8,128)S(1)}, u32[]{:S(2)}, u32[]{:S(2)}) collective-permute-start(f32[2,32,512]{2,1,0:T(8,128)S(1)} %add.116), channel_id=1, source_target_pairs={{0,3},{1,2},{2,1},{3,0},{4,7},{5,6},{6,5},{7,4},{8,11},{9,10},{10,... | collective-permute-start | bytes 393224 | tf_op jit(solution)/shard_map/ppermute | solution.py:42
  80.0 12.3 %collective-permute-start.2 = (f32[2,32,512]{2,1,0:T(8,128)S(1)}, f32[2,32,512]{2,1,0:T(8,128)S(1)}, u32[]{:S(2)}, u32[]{:S(2)}) collective-permute-start(f32[2,32,512]{2,1,0:T(8,128)S(1)} %add.116), channel_id=1, source_target_pairs={{0,2},{1,3},{2,0},{3,1},{4,6},{5,7},{6,4},{7,5},{8,10},{9,11},{10,... | collective-permute-start | bytes 393224 | tf_op jit(solution)/shard_map/ppermute | solution.py:42
  80.7 15.1 %collective-permute-start.1 = (f32[2,32,512]{2,1,0:T(8,128)S(1)}, f32[2,32,512]{2,1,0:T(8,128)S(1)}, u32[]{:S(2)}, u32[]{:S(2)}) collective-permute-start(f32[2,32,512]{2,1,0:T(8,128)S(1)} %add.116), channel_id=1, source_target_pairs={{0,1},{1,0},{2,3},{3,2},{4,5},{5,4},{6,7},{7,6},{8,9},{9,8},{10,11... | collective-permute-start | bytes 393224 | tf_op jit(solution)/shard_map/ppermute | solution.py:42
  95.9 37.3 %copy-start.5 = (s32[128]{0:T(128)S(1)}, s32[128]{0:T(128)}, u32[]{:S(2)}) copy-start(s32[128]{0:T(128)} %param.18) | copy-start | bytes 1540
  95.9 10.7 %collective-permute-start.6 = (f32[2,32,512]{2,1,0:T(8,128)S(1)}, f32[2,32,512]{2,1,0:T(8,128)S(1)}, u32[]{:S(2)}, u32[]{:S(2)}) collective-permute-start(f32[2,32,512]{2,1,0:T(8,128)S(1)} %add_add_fusion.3), channel_id=1, source_target_pairs={{0,24},{4,28},{8,16},{12,20},{16,8},{20,12},{24,0},{28,4},{32,56},... | collective-permute-start | bytes 393224 | tf_op jit(solution)/shard_map/ppermute | solution.py:42
  96.0 10.6 %collective-permute-start.5 = (f32[2,32,512]{2,1,0:T(8,128)S(1)}, f32[2,32,512]{2,1,0:T(8,128)S(1)}, u32[]{:S(2)}, u32[]{:S(2)}) collective-permute-start(f32[2,32,512]{2,1,0:T(8,128)S(1)} %add_add_fusion.3), channel_id=1, source_target_pairs={{0,16},{4,20},{8,24},{12,28},{16,0},{20,4},{24,8},{28,12},{32,48},... | collective-permute-start | bytes 393224 | tf_op jit(solution)/shard_map/ppermute | solution.py:42
  97.0 9.6 %collective-permute-start.4 = (f32[2,32,512]{2,1,0:T(8,128)S(1)}, f32[2,32,512]{2,1,0:T(8,128)S(1)}, u32[]{:S(2)}, u32[]{:S(2)}) collective-permute-start(f32[2,32,512]{2,1,0:T(8,128)S(1)} %add_add_fusion.3), channel_id=1, source_target_pairs={{0,8},{4,12},{8,0},{12,4},{16,24},{20,28},{24,16},{28,20},{32,40},... | collective-permute-start | bytes 393224 | tf_op jit(solution)/shard_map/ppermute | solution.py:42
  106.6 9.2 %collective-permute-start.9 = (f32[2,32,512]{2,1,0:T(8,128)S(1)}, f32[2,32,512]{2,1,0:T(8,128)S(1)}, u32[]{:S(2)}, u32[]{:S(2)}) collective-permute-start(f32[2,32,512]{2,1,0:T(8,128)S(1)} %add_add_fusion.2), channel_id=1, source_target_pairs={{0,96},{4,100},{8,104},{12,108},{16,112},{20,116},{24,120},{28,124... | collective-permute-start | bytes 393224 | tf_op jit(solution)/shard_map/ppermute | solution.py:42
  108.4 7.5 %collective-permute-start.8 = (f32[2,32,512]{2,1,0:T(8,128)S(1)}, f32[2,32,512]{2,1,0:T(8,128)S(1)}, u32[]{:S(2)}, u32[]{:S(2)}) collective-permute-start(f32[2,32,512]{2,1,0:T(8,128)S(1)} %add_add_fusion.2), channel_id=1, source_target_pairs={{0,64},{4,68},{8,72},{12,76},{16,80},{20,84},{24,88},{28,92},{32,9... | collective-permute-start | bytes 393224 | tf_op jit(solution)/shard_map/ppermute | solution.py:42
  110.1 6.4 %collective-permute-start.7 = (f32[2,32,512]{2,1,0:T(8,128)S(1)}, f32[2,32,512]{2,1,0:T(8,128)S(1)}, u32[]{:S(2)}, u32[]{:S(2)}) collective-permute-start(f32[2,32,512]{2,1,0:T(8,128)S(1)} %add_add_fusion.2), channel_id=1, source_target_pairs={{0,32},{4,36},{8,40},{12,44},{16,48},{20,52},{24,56},{28,60},{32,0... | collective-permute-start | bytes 393224 | tf_op jit(solution)/shard_map/ppermute | solution.py:42
  116.8 42.3 %copy-start.3 = (f32[2,2048]{1,0:T(2,128)S(1)}, f32[2,2048]{1,0:T(2,128)}, u32[]{:S(2)}) copy-start(f32[2,2048]{1,0:T(2,128)} %param.16) | copy-start | bytes 49156
  116.8 42.3 %copy-start.4 = (f32[2,2048]{1,0:T(2,128)S(1)}, f32[2,2048]{1,0:T(2,128)}, u32[]{:S(2)}) copy-start(f32[2,2048]{1,0:T(2,128)} %param.17) | copy-start | bytes 49156
  126.5 19.8 %all-to-all-start.2 = ((f32[128,1,1024]{2,1,0:T(1,128)}), f32[128,1,1024]{2,1,0:T(1,128)S(1)}, u32[]{:S(2)}, u32[]{:S(2)}) async-start(f32[128,1,1024]{2,1,0:T(1,128)} %all_to_all.27), calls=%async_computation.2 | async-start | bytes 1048576 | tf_op jit(solution)/shard_map/all_to_all | solution.py:49
  147.8 17.8 %all-to-all-start.3 = ((f32[128,1,1024]{2,1,0:T(1,128)}), f32[128,1,1024]{2,1,0:T(1,128)S(1)}, u32[]{:S(2)}, u32[]{:S(2)}) async-start(f32[128,1,1024]{2,1,0:T(1,128)} %broadcast_in_dim.15), calls=%async_computation.3 | async-start | bytes 1048576 | tf_op jit(solution)/shard_map/all_to_all | solution.py:52
  167.7 42.8 %copy-start.1 = (f32[1,2,32,512]{3,2,1,0:T(8,128)S(1)}, f32[1,2,32,512]{3,2,1,0:T(8,128)}, u32[]{:S(2)}) copy-start(f32[1,2,32,512]{3,2,1,0:T(8,128)} %param.20) | copy-start | bytes 393220
  175.0 6.3 %collective-permute-start.10 = (f32[2,32,512]{2,1,0:T(8,128)S(1)}, f32[2,32,512]{2,1,0:T(8,128)S(1)}, u32[]{:S(2)}, u32[]{:S(2)}) collective-permute-start(f32[2,32,512]{2,1,0:T(8,128)S(1)} %fusion.4), channel_id=1, source_target_pairs={{0,4},{4,0},{8,12},{12,8},{16,20},{20,16},{24,28},{28,24},{32,36},... | collective-permute-start | bytes 393224 | tf_op jit(solution)/shard_map/ppermute | solution.py:40
  181.3 9.6 %collective-permute-start.13 = (f32[2,32,512]{2,1,0:T(8,128)S(1)}, f32[2,32,512]{2,1,0:T(8,128)S(1)}, u32[]{:S(2)}, u32[]{:S(2)}) collective-permute-start(f32[2,32,512]{2,1,0:T(8,128)S(1)} %add.126), channel_id=1, source_target_pairs={{0,3},{1,2},{2,1},{3,0},{4,7},{5,6},{6,5},{7,4},{8,11},{9,10},{10,... | collective-permute-start | bytes 393224 | tf_op jit(solution)/shard_map/ppermute | solution.py:42
  182.8 8.2 %collective-permute-start.12 = (f32[2,32,512]{2,1,0:T(8,128)S(1)}, f32[2,32,512]{2,1,0:T(8,128)S(1)}, u32[]{:S(2)}, u32[]{:S(2)}) collective-permute-start(f32[2,32,512]{2,1,0:T(8,128)S(1)} %add.126), channel_id=1, source_target_pairs={{0,2},{1,3},{2,0},{3,1},{4,6},{5,7},{6,4},{7,5},{8,10},{9,11},{10,... | collective-permute-start | bytes 393224 | tf_op jit(solution)/shard_map/ppermute | solution.py:42
  184.0 7.5 %collective-permute-start.11 = (f32[2,32,512]{2,1,0:T(8,128)S(1)}, f32[2,32,512]{2,1,0:T(8,128)S(1)}, u32[]{:S(2)}, u32[]{:S(2)}) collective-permute-start(f32[2,32,512]{2,1,0:T(8,128)S(1)} %add.126), channel_id=1, source_target_pairs={{0,1},{1,0},{2,3},{3,2},{4,5},{5,4},{6,7},{7,6},{8,9},{9,8},{10,11... | collective-permute-start | bytes 393224 | tf_op jit(solution)/shard_map/ppermute | solution.py:42
  191.6 9.2 %collective-permute-start.16 = (f32[2,32,512]{2,1,0:T(8,128)S(1)}, f32[2,32,512]{2,1,0:T(8,128)S(1)}, u32[]{:S(2)}, u32[]{:S(2)}) collective-permute-start(f32[2,32,512]{2,1,0:T(8,128)S(1)} %add_add_fusion.1), channel_id=1, source_target_pairs={{0,24},{4,28},{8,16},{12,20},{16,8},{20,12},{24,0},{28,4},{32,56},... | collective-permute-start | bytes 393224 | tf_op jit(solution)/shard_map/ppermute | solution.py:42
  192.7 8.1 %collective-permute-start.15 = (f32[2,32,512]{2,1,0:T(8,128)S(1)}, f32[2,32,512]{2,1,0:T(8,128)S(1)}, u32[]{:S(2)}, u32[]{:S(2)}) collective-permute-start(f32[2,32,512]{2,1,0:T(8,128)S(1)} %add_add_fusion.1), channel_id=1, source_target_pairs={{0,16},{4,20},{8,24},{12,28},{16,0},{20,4},{24,8},{28,12},{32,48},... | collective-permute-start | bytes 393224 | tf_op jit(solution)/shard_map/ppermute | solution.py:42
  194.6 6.2 %collective-permute-start.14 = (f32[2,32,512]{2,1,0:T(8,128)S(1)}, f32[2,32,512]{2,1,0:T(8,128)S(1)}, u32[]{:S(2)}, u32[]{:S(2)}) collective-permute-start(f32[2,32,512]{2,1,0:T(8,128)S(1)} %add_add_fusion.1), channel_id=1, source_target_pairs={{0,8},{4,12},{8,0},{12,4},{16,24},{20,28},{24,16},{28,20},{32,40},... | collective-permute-start | bytes 393224 | tf_op jit(solution)/shard_map/ppermute | solution.py:42
  200.8 4.3 %copy-start.2 = (f32[2,1,32,32]{2,3,1,0:T(8,128)}, f32[2,1,32,32]{2,3,1,0:T(8,128)S(1)}, u32[]{:S(2)}) copy-start(f32[2,1,32,32]{2,3,1,0:T(8,128)S(1)} %custom-call.10) | copy-start | bytes 24580
  200.9 6.3 %collective-permute-start.19 = (f32[2,32,512]{2,1,0:T(8,128)S(1)}, f32[2,32,512]{2,1,0:T(8,128)S(1)}, u32[]{:S(2)}, u32[]{:S(2)}) collective-permute-start(f32[2,32,512]{2,1,0:T(8,128)S(1)} %add_add_fusion), channel_id=1, source_target_pairs={{0,96},{4,100},{8,104},{12,108},{16,112},{20,116},{24,120},{28,124... | collective-permute-start | bytes 393224 | tf_op jit(solution)/shard_map/ppermute | solution.py:42
  202.1 6.5 %collective-permute-start.18 = (f32[2,32,512]{2,1,0:T(8,128)S(1)}, f32[2,32,512]{2,1,0:T(8,128)S(1)}, u32[]{:S(2)}, u32[]{:S(2)}) collective-permute-start(f32[2,32,512]{2,1,0:T(8,128)S(1)} %add_add_fusion), channel_id=1, source_target_pairs={{0,64},{4,68},{8,72},{12,76},{16,80},{20,84},{24,88},{28,92},{32,9... | collective-permute-start | bytes 393224 | tf_op jit(solution)/shard_map/ppermute | solution.py:42
  203.7 5.7 %collective-permute-start.17 = (f32[2,32,512]{2,1,0:T(8,128)S(1)}, f32[2,32,512]{2,1,0:T(8,128)S(1)}, u32[]{:S(2)}, u32[]{:S(2)}) collective-permute-start(f32[2,32,512]{2,1,0:T(8,128)S(1)} %add_add_fusion), channel_id=1, source_target_pairs={{0,32},{4,36},{8,40},{12,44},{16,48},{20,52},{24,56},{28,60},{32,0... | collective-permute-start | bytes 393224 | tf_op jit(solution)/shard_map/ppermute | solution.py:42
Sparse Core Ops, SparseCore 0:
  11.7 96.2 all-gather.1

commit v7 on v6

--- a/solution.py
+++ b/solution.py
@@ -72,7 +72,7 @@
 TAIL_ROWS = 512
 
 
-def tail_kernel(table, grads, errs, left_rows, right_t, carried, out_err, out_w, cbuf, sems):
+def tail_kernel(table, grads, errs, left_rows, right_t, carried, out_err, out_w, cbuf, ubuf, sems):
     m = pl.program_id(0)
     i = pl.program_id(1)
     pieces = cbuf.shape[0]
@@ -85,18 +85,25 @@
 
     @pl.when((m == 0) & (i == 0))
     def _():
-        for j in range(pieces):
+        def start(j, carry):
             piece_copy(j).start()
+            return carry
+
+        lax.fori_loop(0, pieces, start, 0)
 
     upd = jnp.dot(left_rows[0], right_t[0], precision=HI, preferred_element_type=jnp.float32)
     merged = grads[0].astype(jnp.float32) + errs[0]
     out_err[0] = merged - upd
+    ubuf[...] = upd
     base = (m * blocks + i) * per_block
-    for p in range(per_block):
+
+    def finish(p, carry):
         piece_copy(base + p).wait()
-    for p in range(per_block):
-        rows = slice(p * piece_rows, (p + 1) * piece_rows)
-        out_w[0, rows, :] = (cbuf[base + p] - step_rate * upd[rows, :]).astype(out_w.dtype)
+        rows = pl.ds(pl.multiple_of(p * piece_rows, piece_rows), piece_rows)
+        out_w[0, rows, :] = (cbuf[base + p] - step_rate * ubuf[rows, :]).astype(out_w.dtype)
+        return carry
+
+    lax.fori_loop(0, per_block, finish, 0)
 
 
 def tail(table, grads, errs, left_rows, right_t, carried):
@@ -119,6 +126,7 @@
         out_specs=[row_spec, row_spec],
         scratch_shapes=[
             pltpu.VMEM((pieces, piece_rows, kv), jnp.float32),
+            pltpu.VMEM((TAIL_ROWS, kv), jnp.float32),
             pltpu.SemaphoreType.DMA((pieces,)),
         ],
     )
@@ -156,7 +164,6 @@
 
     old_moment = slot_moment[0]
     carried = slot_weights[0].astype(jnp.float32) - (step_rate * momentum_decay) * old_moment
-    every_carried = lax.all_gather(carried[None], ("dp", "group"), axis=0, tiled=True)
 
     merged = gradients[0].astype(jnp.float32) + errors[0]
     lshape = (merged.shape[0], warm_right.shape[2], merged.shape[1])
@@ -164,6 +171,8 @@
     norm_local = norm_grads[0]
     joined = jnp.concatenate([p1.reshape(-1), norm_local.reshape(-1)])
     joined_sum = sum_all_to_all(joined, replicas)
+    joined_sum, carried = lax.optimization_barrier((joined_sum, carried))
+    every_carried = lax.all_gather(carried[None], ("dp", "group"), axis=0, tiled=True)
     p1_sum = joined_sum[: p1.size].reshape(lshape)
     norm_sum = joined_sum[p1.size :].reshape(norm_local.shape)
     lower_one = gram_factor(p1_sum)

time: 238 us -> 235 us (0.987)
    ppermute x18, waiting for transfers between devices: 22.7 us -> 18.3 us  [sum_radix4(): r1, r2, r3 = [lax.ppermute(x, axis, perm) for axis, perm in parts]]
    all_to_all x2, waiting for transfers between devices: 22.3 us -> 25.4 us  [sum_all_to_all(): return lax.all_to_all(spread, axes, 0, 0, tiled=False).reshape(-1)]
  transfers between devices with their start and end apart: 24 -> 24, of which waited for: 13 -> 14; matrix products, arithmetic and copies ran while one was open for 29% -> 24% of each run, Pallas kernels for 0% -> 0%
where the time goes in v7:
time: 235 us
  waiting for transfers between devices  56.8 us (24%)
  starting transfers between devices  42.7 us (18%)
  matrix products  36.2 us (15%)
  other arithmetic  29 us (12%)
  blocking collectives  24.9 us (11%)
  between operations  19.7 us (8%)
  Pallas kernels  18.3 us (8%)
  local copies, waits for them, and re-layouts  6.98 us (3%)
    all_to_all x2, waiting for transfers between devices, sum_all_to_all(): return lax.all_to_all(spread, axes, 0, 0, tiled=False).reshape(-1)  25.4 us
    ppermute x18, starting transfers between devices, sum_radix4(): r1, r2, r3 = [lax.ppermute(x, axis, perm) for axis, perm in parts]  25.2 us
    all_to_all x1, blocking collectives, sum_all_to_all(): rows = lax.all_to_all(x.reshape(count, -1), axes, 0, 0, tiled=False)  24.9 us
    pallas_call x1, Pallas kernels, tail(): pl.pallas_call(tail_kernel, grid_spec=spec, out_shape=[jax.ShapeDtypeStru...  18.3 us
    ppermute x18, waiting for transfers between devices, sum_radix4(): r1, r2, r3 = [lax.ppermute(x, axis, perm) for axis, perm in parts]  18.3 us
    dot_general x2, matrix products, left_t(): return jnp.einsum('mdk,mrk->mrd', merged, right_t, precision=MID)  16.8 us
    dot_general x2, matrix products, right_t_of(): return jnp.einsum('mdk,mrd->mrk', merged, left_tr, precision=MID)  14.4 us
    all_to_all x1, waiting for transfers between devices, sum_all_to_all(): rows = lax.all_to_all(x.reshape(count, -1), axes, 0, 0, tiled=False)  12.8 us
  transfers between devices with their start and end apart: 24, of which 14 were waited for; matrix products, arithmetic and copies ran while one was open for 24% of the time, Pallas kernels for 0%

profile of v7, /device:TPU:0, one launch (start us, length us, event | category | flops | bytes accessed | tf_op | source)
XLA Modules:
  0.0 234.5 jit_solution(6477571249235529630)
XLA Ops:
  8.1 8.4 %fusion.7 = f32[2,2048,32]{1,2,0:T(8,128)S(1)} fusion(f32[2,512,32]{1,2,0:T(8,128)S(1)} %copy-done, f32[1,2,2048,512]{3,2,1,0:T(8,128)} %param.13, bf16[1,2,2048,512]{3,2,1,0:T(8,128)(2,1)} %param.12), kind=kOutput, calls=%fused_computation.12 | convolution fusion | flops 406847488 | bytes 13238272 | tf_op jit(solution)/shard_map/mdk,mrk->mrd/dot_general | solution.py:65
  17.5 24.9 %all_to_all.32 = f32[128,1,1056]{2,1,0:T(1,128)S(1)} all-to-all(f32[128,1,1056]{2,1,0:T(1,128)S(1)} %all_to_all.26), channel_id=1, replica_groups=mesh['dp'=32,'group'=4] {'dp','group'}, dimensions={0} | all-to-all | bytes 1081344 | tf_op jit(solution)/shard_map/all_to_all | solution.py:49
  43.9 4.6 %all-to-all-start.1 = ((f32[128,1,1056]{2,1,0:T(1,128)}), f32[128,1,1056]{2,1,0:T(1,128)S(1)}, u32[]{:S(2)}, u32[]{:S(2)}) async-start(f32[128,1,1056]{2,1,0:T(1,128)} %broadcast_in_dim.16), calls=%async_computation.1 | async-start | bytes 1179648 | tf_op jit(solution)/shard_map/all_to_all | solution.py:52
  49.2 13.1 %all-to-all-done.1 = f32[128,1,1056]{2,1,0:T(1,128)S(1)} async-done(((f32[128,1,1056]{2,1,0:T(1,128)}), f32[128,1,1056]{2,1,0:T(1,128)S(1)}, u32[]{:S(2)}, u32[]{:S(2)}) %all-to-all-start.1) | async-done | bytes 540704 | tf_op jit(solution)/shard_map/all_to_all | solution.py:52
  62.4 1.4 reduce.6
  64.6 7.2 %fusion.6 = f32[2,32,512]{2,1,0:T(8,128)S(1)} fusion(f32[2,32,2048]{2,1,0:T(8,128)S(1)} %reshape.81, f32[1,2,2048,512]{3,2,1,0:T(8,128)} %param.13, bf16[1,2,2048,512]{3,2,1,0:T(8,128)(2,1)} %param.12), kind=kOutput, calls=%fused_computation.11 | convolution fusion | flops 406847488 | bytes 13238272 | tf_op jit(solution)/shard_map/mdk,mrd->mrk/dot_general | solution.py:69
  73.2 2.0 collective-permute-start.3
  76.1 1.4 collective-permute-start.1
  77.6 5.9 %custom-call.13 = f32[2,32,32]{2,1,0:T(8,128)S(1)} custom-call(f32[2,32,32]{2,1,0:T(8,128)S(1)} %fusion.24), custom_call_target="Cholesky" | custom-call | tf_op jit(solution)/shard_map/jit(cholesky)/cholesky | solution.py:57
  85.5 1.9 collective-permute-start.5
  88.9 4.7 %collective-permute-done.6 = f32[2,32,512]{2,1,0:T(8,128)S(1)} collective-permute-done((f32[2,32,512]{2,1,0:T(8,128)S(1)}, f32[2,32,512]{2,1,0:T(8,128)S(1)}, u32[]{:S(2)}, u32[]{:S(2)}) %collective-permute-start.6) | collective-permute-done | bytes 131104 | tf_op jit(solution)/shard_map/ppermute | solution.py:42
  95.4 1.7 collective-permute-start.8
  97.1 1.3 collective-permute-start.7
  98.5 4.9 %custom-call.14 = f32[2,1,32,32]{2,3,1,0:T(8,128)S(1)} custom-call(f32[2,1,32,32]{3,2,1,0:T(8,128)S(1)} %select_bitcast_fusion), custom_call_target="InvertDiagBlocksLowerTriangular" | custom-call | tf_op jit(solution)/shard_map/jit(_solve_triangular)/vmap()/triangular_solve | solution.py:61
  103.4 2.8 %collective-permute-done.9 = f32[2,32,512]{2,1,0:T(8,128)S(1)} collective-permute-done((f32[2,32,512]{2,1,0:T(8,128)S(1)}, f32[2,32,512]{2,1,0:T(8,128)S(1)}, u32[]{:S(2)}, u32[]{:S(2)}) %collective-permute-start.9) | collective-permute-done | bytes 131104 | tf_op jit(solution)/shard_map/ppermute | solution.py:42
  106.6 8.3 %fusion.5 = f32[2,32,2048]{2,1,0:T(8,128)S(1)} fusion(f32[2,32,512]{2,1,0:T(8,128)S(1)} %convolution_multiply_fusion.1, f32[1,2,2048,512]{3,2,1,0:T(8,128)} %param.13, bf16[1,2,2048,512]{3,2,1,0:T(8,128)(2,1)} %param.12), kind=kOutput, calls=%fused_computation.10 | convolution fusion | flops 406847488 | bytes 13238272 | tf_op jit(solution)/shard_map/mdk,mrk->mrd/dot_general | solution.py:65
  114.9 1.4 all_to_all.27
  116.3 7.1 %all-to-all-start.2 = ((f32[128,1,1024]{2,1,0:T(1,128)}), f32[128,1,1024]{2,1,0:T(1,128)S(1)}, u32[]{:S(2)}, u32[]{:S(2)}) async-start(f32[128,1,1024]{2,1,0:T(1,128)} %all_to_all.27), calls=%async_computation.2 | async-start | bytes 1048576 | tf_op jit(solution)/shard_map/all_to_all | solution.py:49
  130.0 12.8 %all-to-all-done.2 = f32[128,1,1024]{2,1,0:T(1,128)S(1)} async-done(((f32[128,1,1024]{2,1,0:T(1,128)}), f32[128,1,1024]{2,1,0:T(1,128)S(1)}, u32[]{:S(2)}, u32[]{:S(2)}) %all-to-all-start.2) | async-done | bytes 524320 | tf_op jit(solution)/shard_map/all_to_all | solution.py:49
  144.2 4.8 %all-to-all-start.3 = ((f32[128,1,1024]{2,1,0:T(1,128)}), f32[128,1,1024]{2,1,0:T(1,128)S(1)}, u32[]{:S(2)}, u32[]{:S(2)}) async-start(f32[128,1,1024]{2,1,0:T(1,128)} %broadcast_in_dim.17), calls=%async_computation.3 | async-start | bytes 1048576 | tf_op jit(solution)/shard_map/all_to_all | solution.py:52
  149.8 12.3 %all-to-all-done.3 = f32[128,1,1024]{2,1,0:T(1,128)S(1)} async-done(((f32[128,1,1024]{2,1,0:T(1,128)}), f32[128,1,1024]{2,1,0:T(1,128)S(1)}, u32[]{:S(2)}, u32[]{:S(2)}) %all-to-all-start.3) | async-done | bytes 524320 | tf_op jit(solution)/shard_map/all_to_all | solution.py:52
  164.2 7.2 %fusion.4 = f32[2,32,512]{2,1,0:T(8,128)S(1)} fusion(f32[2,32,2048]{2,1,0:T(8,128)S(1)} %reshape_reshape.4, f32[1,2,2048,512]{3,2,1,0:T(8,128)} %param.13, bf16[1,2,2048,512]{3,2,1,0:T(8,128)(2,1)} %param.12), kind=kOutput, calls=%fused_computation.9 | convolution fusion | flops 406847488 | bytes 13238272 | tf_op jit(solution)/shard_map/mdk,mrd->mrk/dot_general | solution.py:69
  171.8 5.9 %custom-call.15 = f32[2,32,32]{2,1,0:T(8,128)S(1)} custom-call(f32[2,32,32]{2,1,0:T(8,128)S(1)} %fusion.22), custom_call_target="Cholesky" | custom-call | tf_op jit(solution)/shard_map/jit(cholesky)/cholesky | solution.py:57
  177.7 1.4 collective-permute-start.13
  180.5 1.4 collective-permute-start.11
  182.0 5.3 %collective-permute-done.13 = f32[2,32,512]{2,1,0:T(8,128)S(1)} collective-permute-done((f32[2,32,512]{2,1,0:T(8,128)S(1)}, f32[2,32,512]{2,1,0:T(8,128)S(1)}, u32[]{:S(2)}, u32[]{:S(2)}) %collective-permute-start.13) | collective-permute-done | bytes 131104 | tf_op jit(solution)/shard_map/ppermute | solution.py:42
  189.1 1.9 collective-permute-start.15
  192.3 4.9 %custom-call.10 = f32[2,1,32,32]{2,3,1,0:T(8,128)S(1)} custom-call(f32[2,1,32,32]{3,2,1,0:T(8,128)S(1)} %fusion.25), custom_call_target="InvertDiagBlocksLowerTriangular" | custom-call | tf_op jit(solution)/shard_map/jit(_solve_triangular)/vmap()/triangular_solve | solution.py:61
  198.5 1.6 collective-permute-start.18
  200.1 1.4 collective-permute-start.17
  203.6 1.4 collective-permute-done.18
  209.4 18.3 %shard_map.128 = (f32[2,2048,512]{2,1,0:T(8,128)}, bf16[2,2048,512]{2,1,0:T(8,128)(2,1)}) custom-call(s32[128]{0:T(128)S(1)} %add_clamp_fusion.table, bf16[2,2048,512]{2,1,0:T(8,128)(2,1)} %bitcast.106, f32[2,2048,512]{2,1,0:T(8,128)} %bitcast.105, f32[2,2048,32]{2,1,0:T(8,128)S(1)} %bitcast.104, f32[2,32,512]{2,1,0:T(8,128)S(1)} %convolution_multiply_fusion.right_t, ...), custom_call_target="tpu_custom_call" | custom-call | flops 134217728 | bytes 33554432 | tf_op jit(solution)/shard_map/pallas_call | solution.py:135
  (91 shorter events, 31.1 us)
Async XLA Ops:
  7.2 0.9 copy-start
  8.1 40.4 %copy-start.1 = (f32[1,2,32,512]{3,2,1,0:T(8,128)S(1)}, f32[1,2,32,512]{3,2,1,0:T(8,128)}, u32[]{:S(2)}) copy-start(f32[1,2,32,512]{3,2,1,0:T(8,128)} %param.20) | copy-start | bytes 393220
  8.1 40.4 %copy-start.3 = (bf16[1,2,32,512]{3,2,1,0:T(8,128)(2,1)S(1)}, bf16[1,2,32,512]{3,2,1,0:T(8,128)(2,1)}, u32[]{:S(2)}) copy-start(bf16[1,2,32,512]{3,2,1,0:T(8,128)(2,1)} %param.19) | copy-start | bytes 196612
  8.1 56.3 %copy-start.6 = (s32[128]{0:T(128)S(1)}, s32[128]{0:T(128)}, u32[]{:S(2)}) copy-start(s32[128]{0:T(128)} %param.18) | copy-start | bytes 1540
  43.9 18.5 %all-to-all-start.1 = ((f32[128,1,1056]{2,1,0:T(1,128)}), f32[128,1,1056]{2,1,0:T(1,128)S(1)}, u32[]{:S(2)}, u32[]{:S(2)}) async-start(f32[128,1,1056]{2,1,0:T(1,128)} %broadcast_in_dim.16), calls=%async_computation.1 | async-start | bytes 1179648 | tf_op jit(solution)/shard_map/all_to_all | solution.py:52
  48.5 160.9 %all-gather.3.cloned.1.call-start = ((), (), s32[]{:S(2)}) async-start(), calls=%async_computation.4 | async-start | bytes 16908288 | tf_op jit(solution)/shard_map/all_gather | solution.py:175
  71.8 1.4 collective-permute-start
  73.2 10.8 %collective-permute-start.3 = (f32[2,32,512]{2,1,0:T(8,128)S(1)}, f32[2,32,512]{2,1,0:T(8,128)S(1)}, u32[]{:S(2)}, u32[]{:S(2)}) collective-permute-start(f32[2,32,512]{2,1,0:T(8,128)S(1)} %add.116), channel_id=1, source_target_pairs={{0,3},{1,2},{2,1},{3,0},{4,7},{5,6},{6,5},{7,4},{8,11},{9,10},{10,... | collective-permute-start | bytes 393224 | tf_op jit(solution)/shard_map/ppermute | solution.py:42
  75.2 8.8 %collective-permute-start.2 = (f32[2,32,512]{2,1,0:T(8,128)S(1)}, f32[2,32,512]{2,1,0:T(8,128)S(1)}, u32[]{:S(2)}, u32[]{:S(2)}) collective-permute-start(f32[2,32,512]{2,1,0:T(8,128)S(1)} %add.116), channel_id=1, source_target_pairs={{0,2},{1,3},{2,0},{3,1},{4,6},{5,7},{6,4},{7,5},{8,10},{9,11},{10,... | collective-permute-start | bytes 393224 | tf_op jit(solution)/shard_map/ppermute | solution.py:42
  76.1 8.4 %collective-permute-start.1 = (f32[2,32,512]{2,1,0:T(8,128)S(1)}, f32[2,32,512]{2,1,0:T(8,128)S(1)}, u32[]{:S(2)}, u32[]{:S(2)}) collective-permute-start(f32[2,32,512]{2,1,0:T(8,128)S(1)} %add.116), channel_id=1, source_target_pairs={{0,1},{1,0},{2,3},{3,2},{4,5},{5,4},{6,7},{7,6},{8,9},{9,8},{10,11... | collective-permute-start | bytes 393224 | tf_op jit(solution)/shard_map/ppermute | solution.py:42
  84.5 9.0 %collective-permute-start.6 = (f32[2,32,512]{2,1,0:T(8,128)S(1)}, f32[2,32,512]{2,1,0:T(8,128)S(1)}, u32[]{:S(2)}, u32[]{:S(2)}) collective-permute-start(f32[2,32,512]{2,1,0:T(8,128)S(1)} %add_add_fusion.3), channel_id=1, source_target_pairs={{0,24},{4,28},{8,16},{12,20},{16,8},{20,12},{24,0},{28,4},{32,56},... | collective-permute-start | bytes 393224 | tf_op jit(solution)/shard_map/ppermute | solution.py:42
  85.5 8.0 %collective-permute-start.5 = (f32[2,32,512]{2,1,0:T(8,128)S(1)}, f32[2,32,512]{2,1,0:T(8,128)S(1)}, u32[]{:S(2)}, u32[]{:S(2)}) collective-permute-start(f32[2,32,512]{2,1,0:T(8,128)S(1)} %add_add_fusion.3), channel_id=1, source_target_pairs={{0,16},{4,20},{8,24},{12,28},{16,0},{20,4},{24,8},{28,12},{32,48},... | collective-permute-start | bytes 393224 | tf_op jit(solution)/shard_map/ppermute | solution.py:42
  87.4 6.8 %collective-permute-start.4 = (f32[2,32,512]{2,1,0:T(8,128)S(1)}, f32[2,32,512]{2,1,0:T(8,128)S(1)}, u32[]{:S(2)}, u32[]{:S(2)}) collective-permute-start(f32[2,32,512]{2,1,0:T(8,128)S(1)} %add_add_fusion.3), channel_id=1, source_target_pairs={{0,8},{4,12},{8,0},{12,4},{16,24},{20,28},{24,16},{28,20},{32,40},... | collective-permute-start | bytes 393224 | tf_op jit(solution)/shard_map/ppermute | solution.py:42
  94.2 12.0 %collective-permute-start.9 = (f32[2,32,512]{2,1,0:T(8,128)S(1)}, f32[2,32,512]{2,1,0:T(8,128)S(1)}, u32[]{:S(2)}, u32[]{:S(2)}) collective-permute-start(f32[2,32,512]{2,1,0:T(8,128)S(1)} %add_add_fusion.2), channel_id=1, source_target_pairs={{0,96},{4,100},{8,104},{12,108},{16,112},{20,116},{24,120},{28,124... | collective-permute-start | bytes 393224 | tf_op jit(solution)/shard_map/ppermute | solution.py:42
  95.4 10.8 %collective-permute-start.8 = (f32[2,32,512]{2,1,0:T(8,128)S(1)}, f32[2,32,512]{2,1,0:T(8,128)S(1)}, u32[]{:S(2)}, u32[]{:S(2)}) collective-permute-start(f32[2,32,512]{2,1,0:T(8,128)S(1)} %add_add_fusion.2), channel_id=1, source_target_pairs={{0,64},{4,68},{8,72},{12,76},{16,80},{20,84},{24,88},{28,92},{32,9... | collective-permute-start | bytes 393224 | tf_op jit(solution)/shard_map/ppermute | solution.py:42
  97.1 9.1 %collective-permute-start.7 = (f32[2,32,512]{2,1,0:T(8,128)S(1)}, f32[2,32,512]{2,1,0:T(8,128)S(1)}, u32[]{:S(2)}, u32[]{:S(2)}) collective-permute-start(f32[2,32,512]{2,1,0:T(8,128)S(1)} %add_add_fusion.2), channel_id=1, source_target_pairs={{0,32},{4,36},{8,40},{12,44},{16,48},{20,52},{24,56},{28,60},{32,0... | collective-permute-start | bytes 393224 | tf_op jit(solution)/shard_map/ppermute | solution.py:42
  106.5 42.6 %copy-start.4 = (f32[2,2048]{1,0:T(2,128)S(1)}, f32[2,2048]{1,0:T(2,128)}, u32[]{:S(2)}) copy-start(f32[2,2048]{1,0:T(2,128)} %param.16) | copy-start | bytes 49156
  106.5 42.6 %copy-start.5 = (f32[2,2048]{1,0:T(2,128)S(1)}, f32[2,2048]{1,0:T(2,128)}, u32[]{:S(2)}) copy-start(f32[2,2048]{1,0:T(2,128)} %param.17) | copy-start | bytes 49156
  116.3 26.5 %all-to-all-start.2 = ((f32[128,1,1024]{2,1,0:T(1,128)}), f32[128,1,1024]{2,1,0:T(1,128)S(1)}, u32[]{:S(2)}, u32[]{:S(2)}) async-start(f32[128,1,1024]{2,1,0:T(1,128)} %all_to_all.27), calls=%async_computation.2 | async-start | bytes 1048576 | tf_op jit(solution)/shard_map/all_to_all | solution.py:49
  144.2 17.8 %all-to-all-start.3 = ((f32[128,1,1024]{2,1,0:T(1,128)}), f32[128,1,1024]{2,1,0:T(1,128)S(1)}, u32[]{:S(2)}, u32[]{:S(2)}) async-start(f32[128,1,1024]{2,1,0:T(1,128)} %broadcast_in_dim.17), calls=%async_computation.3 | async-start | bytes 1048576 | tf_op jit(solution)/shard_map/all_to_all | solution.py:52
  171.4 6.3 %collective-permute-start.10 = (f32[2,32,512]{2,1,0:T(8,128)S(1)}, f32[2,32,512]{2,1,0:T(8,128)S(1)}, u32[]{:S(2)}, u32[]{:S(2)}) collective-permute-start(f32[2,32,512]{2,1,0:T(8,128)S(1)} %fusion.4), channel_id=1, source_target_pairs={{0,4},{4,0},{8,12},{12,8},{16,20},{20,16},{24,28},{28,24},{32,36},... | collective-permute-start | bytes 393224 | tf_op jit(solution)/shard_map/ppermute | solution.py:40
  177.7 9.6 %collective-permute-start.13 = (f32[2,32,512]{2,1,0:T(8,128)S(1)}, f32[2,32,512]{2,1,0:T(8,128)S(1)}, u32[]{:S(2)}, u32[]{:S(2)}) collective-permute-start(f32[2,32,512]{2,1,0:T(8,128)S(1)} %add.126), channel_id=1, source_target_pairs={{0,3},{1,2},{2,1},{3,0},{4,7},{5,6},{6,5},{7,4},{8,11},{9,10},{10,... | collective-permute-start | bytes 393224 | tf_op jit(solution)/shard_map/ppermute | solution.py:42
  179.2 8.2 %collective-permute-start.12 = (f32[2,32,512]{2,1,0:T(8,128)S(1)}, f32[2,32,512]{2,1,0:T(8,128)S(1)}, u32[]{:S(2)}, u32[]{:S(2)}) collective-permute-start(f32[2,32,512]{2,1,0:T(8,128)S(1)} %add.126), channel_id=1, source_target_pairs={{0,2},{1,3},{2,0},{3,1},{4,6},{5,7},{6,4},{7,5},{8,10},{9,11},{10,... | collective-permute-start | bytes 393224 | tf_op jit(solution)/shard_map/ppermute | solution.py:42
  180.5 7.5 %collective-permute-start.11 = (f32[2,32,512]{2,1,0:T(8,128)S(1)}, f32[2,32,512]{2,1,0:T(8,128)S(1)}, u32[]{:S(2)}, u32[]{:S(2)}) collective-permute-start(f32[2,32,512]{2,1,0:T(8,128)S(1)} %add.126), channel_id=1, source_target_pairs={{0,1},{1,0},{2,3},{3,2},{4,5},{5,4},{6,7},{7,6},{8,9},{9,8},{10,11... | collective-permute-start | bytes 393224 | tf_op jit(solution)/shard_map/ppermute | solution.py:42
  188.0 9.2 %collective-permute-start.16 = (f32[2,32,512]{2,1,0:T(8,128)S(1)}, f32[2,32,512]{2,1,0:T(8,128)S(1)}, u32[]{:S(2)}, u32[]{:S(2)}) collective-permute-start(f32[2,32,512]{2,1,0:T(8,128)S(1)} %add_add_fusion.1), channel_id=1, source_target_pairs={{0,24},{4,28},{8,16},{12,20},{16,8},{20,12},{24,0},{28,4},{32,56},... | collective-permute-start | bytes 393224 | tf_op jit(solution)/shard_map/ppermute | solution.py:42
  189.1 8.1 %collective-permute-start.15 = (f32[2,32,512]{2,1,0:T(8,128)S(1)}, f32[2,32,512]{2,1,0:T(8,128)S(1)}, u32[]{:S(2)}, u32[]{:S(2)}) collective-permute-start(f32[2,32,512]{2,1,0:T(8,128)S(1)} %add_add_fusion.1), channel_id=1, source_target_pairs={{0,16},{4,20},{8,24},{12,28},{16,0},{20,4},{24,8},{28,12},{32,48},... | collective-permute-start | bytes 393224 | tf_op jit(solution)/shard_map/ppermute | solution.py:42
  191.0 6.2 %collective-permute-start.14 = (f32[2,32,512]{2,1,0:T(8,128)S(1)}, f32[2,32,512]{2,1,0:T(8,128)S(1)}, u32[]{:S(2)}, u32[]{:S(2)}) collective-permute-start(f32[2,32,512]{2,1,0:T(8,128)S(1)} %add_add_fusion.1), channel_id=1, source_target_pairs={{0,8},{4,12},{8,0},{12,4},{16,24},{20,28},{24,16},{28,20},{32,40},... | collective-permute-start | bytes 393224 | tf_op jit(solution)/shard_map/ppermute | solution.py:42
  197.2 4.3 %copy-start.2 = (f32[2,1,32,32]{2,3,1,0:T(8,128)}, f32[2,1,32,32]{2,3,1,0:T(8,128)S(1)}, u32[]{:S(2)}) copy-start(f32[2,1,32,32]{2,3,1,0:T(8,128)S(1)} %custom-call.10) | copy-start | bytes 24580
  197.3 6.3 %collective-permute-start.19 = (f32[2,32,512]{2,1,0:T(8,128)S(1)}, f32[2,32,512]{2,1,0:T(8,128)S(1)}, u32[]{:S(2)}, u32[]{:S(2)}) collective-permute-start(f32[2,32,512]{2,1,0:T(8,128)S(1)} %add_add_fusion), channel_id=1, source_target_pairs={{0,96},{4,100},{8,104},{12,108},{16,112},{20,116},{24,120},{28,124... | collective-permute-start | bytes 393224 | tf_op jit(solution)/shard_map/ppermute | solution.py:42
  198.5 6.5 %collective-permute-start.18 = (f32[2,32,512]{2,1,0:T(8,128)S(1)}, f32[2,32,512]{2,1,0:T(8,128)S(1)}, u32[]{:S(2)}, u32[]{:S(2)}) collective-permute-start(f32[2,32,512]{2,1,0:T(8,128)S(1)} %add_add_fusion), channel_id=1, source_target_pairs={{0,64},{4,68},{8,72},{12,76},{16,80},{20,84},{24,88},{28,92},{32,9... | collective-permute-start | bytes 393224 | tf_op jit(solution)/shard_map/ppermute | solution.py:42
  200.1 5.7 %collective-permute-start.17 = (f32[2,32,512]{2,1,0:T(8,128)S(1)}, f32[2,32,512]{2,1,0:T(8,128)S(1)}, u32[]{:S(2)}, u32[]{:S(2)}) collective-permute-start(f32[2,32,512]{2,1,0:T(8,128)S(1)} %add_add_fusion), channel_id=1, source_target_pairs={{0,32},{4,36},{8,40},{12,44},{16,48},{20,52},{24,56},{28,60},{32,0... | collective-permute-start | bytes 393224 | tf_op jit(solution)/shard_map/ppermute | solution.py:42
Sparse Core Ops, SparseCore 0:
  64.4 85.1 all-gather.2

commit v8 on v7

--- a/solution.py
+++ b/solution.py
@@ -91,7 +91,7 @@
 
         lax.fori_loop(0, pieces, start, 0)
 
-    upd = jnp.dot(left_rows[0], right_t[0], precision=HI, preferred_element_type=jnp.float32)
+    upd = jnp.dot(left_rows[0], right_t[0], precision=MID, preferred_element_type=jnp.float32)
     merged = grads[0].astype(jnp.float32) + errs[0]
     out_err[0] = merged - upd
     ubuf[...] = upd

time: 235 us -> 234 us (level)
  no operation moved by 1% of the time
where the time goes in v8:
time: 234 us
  waiting for transfers between devices  56.8 us (24%)
  starting transfers between devices  42.7 us (18%)
  matrix products  36.2 us (15%)
  other arithmetic  29 us (12%)
  blocking collectives  24.9 us (11%)
  between operations  19.7 us (8%)
  Pallas kernels  17.5 us (7%)
  local copies, waits for them, and re-layouts  6.98 us (3%)
    all_to_all x2, waiting for transfers between devices, sum_all_to_all(): return lax.all_to_all(spread, axes, 0, 0, tiled=False).reshape(-1)  25.4 us
    ppermute x18, starting transfers between devices, sum_radix4(): r1, r2, r3 = [lax.ppermute(x, axis, perm) for axis, perm in parts]  25.2 us
    all_to_all x1, blocking collectives, sum_all_to_all(): rows = lax.all_to_all(x.reshape(count, -1), axes, 0, 0, tiled=False)  24.9 us
    ppermute x18, waiting for transfers between devices, sum_radix4(): r1, r2, r3 = [lax.ppermute(x, axis, perm) for axis, perm in parts]  18.3 us
    pallas_call x1, Pallas kernels, tail(): pl.pallas_call(tail_kernel, grid_spec=spec, out_shape=[jax.ShapeDtypeStru...  17.5 us
    dot_general x2, matrix products, left_t(): return jnp.einsum('mdk,mrk->mrd', merged, right_t, precision=MID)  16.8 us
    dot_general x2, matrix products, right_t_of(): return jnp.einsum('mdk,mrd->mrk', merged, left_tr, precision=MID)  14.4 us
    all_to_all x1, waiting for transfers between devices, sum_all_to_all(): rows = lax.all_to_all(x.reshape(count, -1), axes, 0, 0, tiled=False)  12.8 us
  transfers between devices with their start and end apart: 24, of which 14 were waited for; matrix products, arithmetic and copies ran while one was open for 24% of the time, Pallas kernels for 0%

profile of v8, /device:TPU:0, one launch (start us, length us, event | category | flops | bytes accessed | tf_op | source)
XLA Modules:
  0.0 233.7 jit_solution(11239260197213496136)
XLA Ops:
  8.1 8.4 %fusion.7 = f32[2,2048,32]{1,2,0:T(8,128)S(1)} fusion(f32[2,512,32]{1,2,0:T(8,128)S(1)} %copy-done, f32[1,2,2048,512]{3,2,1,0:T(8,128)} %param.13, bf16[1,2,2048,512]{3,2,1,0:T(8,128)(2,1)} %param.12), kind=kOutput, calls=%fused_computation.12 | convolution fusion | flops 406847488 | bytes 13238272 | tf_op jit(solution)/shard_map/mdk,mrk->mrd/dot_general | solution.py:65
  17.5 24.9 %all_to_all.32 = f32[128,1,1056]{2,1,0:T(1,128)S(1)} all-to-all(f32[128,1,1056]{2,1,0:T(1,128)S(1)} %all_to_all.26), channel_id=1, replica_groups=mesh['dp'=32,'group'=4] {'dp','group'}, dimensions={0} | all-to-all | bytes 1081344 | tf_op jit(solution)/shard_map/all_to_all | solution.py:49
  43.9 4.6 %all-to-all-start.1 = ((f32[128,1,1056]{2,1,0:T(1,128)}), f32[128,1,1056]{2,1,0:T(1,128)S(1)}, u32[]{:S(2)}, u32[]{:S(2)}) async-start(f32[128,1,1056]{2,1,0:T(1,128)} %broadcast_in_dim.16), calls=%async_computation.1 | async-start | bytes 1179648 | tf_op jit(solution)/shard_map/all_to_all | solution.py:52
  49.2 13.1 %all-to-all-done.1 = f32[128,1,1056]{2,1,0:T(1,128)S(1)} async-done(((f32[128,1,1056]{2,1,0:T(1,128)}), f32[128,1,1056]{2,1,0:T(1,128)S(1)}, u32[]{:S(2)}, u32[]{:S(2)}) %all-to-all-start.1) | async-done | bytes 540704 | tf_op jit(solution)/shard_map/all_to_all | solution.py:52
  62.4 1.4 reduce.6
  64.6 7.2 %fusion.6 = f32[2,32,512]{2,1,0:T(8,128)S(1)} fusion(f32[2,32,2048]{2,1,0:T(8,128)S(1)} %reshape.81, f32[1,2,2048,512]{3,2,1,0:T(8,128)} %param.13, bf16[1,2,2048,512]{3,2,1,0:T(8,128)(2,1)} %param.12), kind=kOutput, calls=%fused_computation.11 | convolution fusion | flops 406847488 | bytes 13238272 | tf_op jit(solution)/shard_map/mdk,mrd->mrk/dot_general | solution.py:69
  73.2 2.0 collective-permute-start.3
  76.1 1.4 collective-permute-start.1
  77.6 5.9 %custom-call.13 = f32[2,32,32]{2,1,0:T(8,128)S(1)} custom-call(f32[2,32,32]{2,1,0:T(8,128)S(1)} %fusion.24), custom_call_target="Cholesky" | custom-call | tf_op jit(solution)/shard_map/jit(cholesky)/cholesky | solution.py:57
  85.5 1.9 collective-permute-start.5
  88.9 4.7 %collective-permute-done.6 = f32[2,32,512]{2,1,0:T(8,128)S(1)} collective-permute-done((f32[2,32,512]{2,1,0:T(8,128)S(1)}, f32[2,32,512]{2,1,0:T(8,128)S(1)}, u32[]{:S(2)}, u32[]{:S(2)}) %collective-permute-start.6) | collective-permute-done | bytes 131104 | tf_op jit(solution)/shard_map/ppermute | solution.py:42
  95.4 1.7 collective-permute-start.8
  97.1 1.3 collective-permute-start.7
  98.5 4.9 %custom-call.14 = f32[2,1,32,32]{2,3,1,0:T(8,128)S(1)} custom-call(f32[2,1,32,32]{3,2,1,0:T(8,128)S(1)} %select_bitcast_fusion), custom_call_target="InvertDiagBlocksLowerTriangular" | custom-call | tf_op jit(solution)/shard_map/jit(_solve_triangular)/vmap()/triangular_solve | solution.py:61
  103.4 2.8 %collective-permute-done.9 = f32[2,32,512]{2,1,0:T(8,128)S(1)} collective-permute-done((f32[2,32,512]{2,1,0:T(8,128)S(1)}, f32[2,32,512]{2,1,0:T(8,128)S(1)}, u32[]{:S(2)}, u32[]{:S(2)}) %collective-permute-start.9) | collective-permute-done | bytes 131104 | tf_op jit(solution)/shard_map/ppermute | solution.py:42
  106.6 8.3 %fusion.5 = f32[2,32,2048]{2,1,0:T(8,128)S(1)} fusion(f32[2,32,512]{2,1,0:T(8,128)S(1)} %convolution_multiply_fusion.1, f32[1,2,2048,512]{3,2,1,0:T(8,128)} %param.13, bf16[1,2,2048,512]{3,2,1,0:T(8,128)(2,1)} %param.12), kind=kOutput, calls=%fused_computation.10 | convolution fusion | flops 406847488 | bytes 13238272 | tf_op jit(solution)/shard_map/mdk,mrk->mrd/dot_general | solution.py:65
  114.9 1.4 all_to_all.27
  116.3 7.1 %all-to-all-start.2 = ((f32[128,1,1024]{2,1,0:T(1,128)}), f32[128,1,1024]{2,1,0:T(1,128)S(1)}, u32[]{:S(2)}, u32[]{:S(2)}) async-start(f32[128,1,1024]{2,1,0:T(1,128)} %all_to_all.27), calls=%async_computation.2 | async-start | bytes 1048576 | tf_op jit(solution)/shard_map/all_to_all | solution.py:49
  130.0 12.8 %all-to-all-done.2 = f32[128,1,1024]{2,1,0:T(1,128)S(1)} async-done(((f32[128,1,1024]{2,1,0:T(1,128)}), f32[128,1,1024]{2,1,0:T(1,128)S(1)}, u32[]{:S(2)}, u32[]{:S(2)}) %all-to-all-start.2) | async-done | bytes 524320 | tf_op jit(solution)/shard_map/all_to_all | solution.py:49
  144.2 4.8 %all-to-all-start.3 = ((f32[128,1,1024]{2,1,0:T(1,128)}), f32[128,1,1024]{2,1,0:T(1,128)S(1)}, u32[]{:S(2)}, u32[]{:S(2)}) async-start(f32[128,1,1024]{2,1,0:T(1,128)} %broadcast_in_dim.17), calls=%async_computation.3 | async-start | bytes 1048576 | tf_op jit(solution)/shard_map/all_to_all | solution.py:52
  149.8 12.3 %all-to-all-done.3 = f32[128,1,1024]{2,1,0:T(1,128)S(1)} async-done(((f32[128,1,1024]{2,1,0:T(1,128)}), f32[128,1,1024]{2,1,0:T(1,128)S(1)}, u32[]{:S(2)}, u32[]{:S(2)}) %all-to-all-start.3) | async-done | bytes 524320 | tf_op jit(solution)/shard_map/all_to_all | solution.py:52
  164.2 7.2 %fusion.4 = f32[2,32,512]{2,1,0:T(8,128)S(1)} fusion(f32[2,32,2048]{2,1,0:T(8,128)S(1)} %reshape_reshape.4, f32[1,2,2048,512]{3,2,1,0:T(8,128)} %param.13, bf16[1,2,2048,512]{3,2,1,0:T(8,128)(2,1)} %param.12), kind=kOutput, calls=%fused_computation.9 | convolution fusion | flops 406847488 | bytes 13238272 | tf_op jit(solution)/shard_map/mdk,mrd->mrk/dot_general | solution.py:69
  171.8 5.9 %custom-call.15 = f32[2,32,32]{2,1,0:T(8,128)S(1)} custom-call(f32[2,32,32]{2,1,0:T(8,128)S(1)} %fusion.22), custom_call_target="Cholesky" | custom-call | tf_op jit(solution)/shard_map/jit(cholesky)/cholesky | solution.py:57
  177.7 1.4 collective-permute-start.13
  180.5 1.4 collective-permute-start.11
  182.0 5.3 %collective-permute-done.13 = f32[2,32,512]{2,1,0:T(8,128)S(1)} collective-permute-done((f32[2,32,512]{2,1,0:T(8,128)S(1)}, f32[2,32,512]{2,1,0:T(8,128)S(1)}, u32[]{:S(2)}, u32[]{:S(2)}) %collective-permute-start.13) | collective-permute-done | bytes 131104 | tf_op jit(solution)/shard_map/ppermute | solution.py:42
  189.1 1.9 collective-permute-start.15
  192.3 4.9 %custom-call.10 = f32[2,1,32,32]{2,3,1,0:T(8,128)S(1)} custom-call(f32[2,1,32,32]{3,2,1,0:T(8,128)S(1)} %fusion.25), custom_call_target="InvertDiagBlocksLowerTriangular" | custom-call | tf_op jit(solution)/shard_map/jit(_solve_triangular)/vmap()/triangular_solve | solution.py:61
  198.5 1.6 collective-permute-start.18
  200.1 1.4 collective-permute-start.17
  203.6 1.4 collective-permute-done.18
  209.4 17.5 %shard_map.128 = (f32[2,2048,512]{2,1,0:T(8,128)}, bf16[2,2048,512]{2,1,0:T(8,128)(2,1)}) custom-call(s32[128]{0:T(128)S(1)} %add_clamp_fusion.table, bf16[2,2048,512]{2,1,0:T(8,128)(2,1)} %bitcast.106, f32[2,2048,512]{2,1,0:T(8,128)} %bitcast.105, f32[2,2048,32]{2,1,0:T(8,128)S(1)} %bitcast.104, f32[2,32,512]{2,1,0:T(8,128)S(1)} %convolution_multiply_fusion.right_t, ...), custom_call_target="tpu_custom_call" | custom-call | flops 134217728 | bytes 33554432 | tf_op jit(solution)/shard_map/pallas_call | solution.py:135
  (91 shorter events, 31.1 us)
Async XLA Ops:
  7.2 0.9 copy-start
  8.1 40.4 %copy-start.1 = (f32[1,2,32,512]{3,2,1,0:T(8,128)S(1)}, f32[1,2,32,512]{3,2,1,0:T(8,128)}, u32[]{:S(2)}) copy-start(f32[1,2,32,512]{3,2,1,0:T(8,128)} %param.20) | copy-start | bytes 393220
  8.1 40.4 %copy-start.3 = (bf16[1,2,32,512]{3,2,1,0:T(8,128)(2,1)S(1)}, bf16[1,2,32,512]{3,2,1,0:T(8,128)(2,1)}, u32[]{:S(2)}) copy-start(bf16[1,2,32,512]{3,2,1,0:T(8,128)(2,1)} %param.19) | copy-start | bytes 196612
  8.1 56.3 %copy-start.6 = (s32[128]{0:T(128)S(1)}, s32[128]{0:T(128)}, u32[]{:S(2)}) copy-start(s32[128]{0:T(128)} %param.18) | copy-start | bytes 1540
  43.9 18.5 %all-to-all-start.1 = ((f32[128,1,1056]{2,1,0:T(1,128)}), f32[128,1,1056]{2,1,0:T(1,128)S(1)}, u32[]{:S(2)}, u32[]{:S(2)}) async-start(f32[128,1,1056]{2,1,0:T(1,128)} %broadcast_in_dim.16), calls=%async_computation.1 | async-start | bytes 1179648 | tf_op jit(solution)/shard_map/all_to_all | solution.py:52
  48.5 160.9 %all-gather.3.cloned.1.call-start = ((), (), s32[]{:S(2)}) async-start(), calls=%async_computation.4 | async-start | bytes 16908288 | tf_op jit(solution)/shard_map/all_gather | solution.py:175
  71.8 1.4 collective-permute-start
  73.2 10.8 %collective-permute-start.3 = (f32[2,32,512]{2,1,0:T(8,128)S(1)}, f32[2,32,512]{2,1,0:T(8,128)S(1)}, u32[]{:S(2)}, u32[]{:S(2)}) collective-permute-start(f32[2,32,512]{2,1,0:T(8,128)S(1)} %add.116), channel_id=1, source_target_pairs={{0,3},{1,2},{2,1},{3,0},{4,7},{5,6},{6,5},{7,4},{8,11},{9,10},{10,... | collective-permute-start | bytes 393224 | tf_op jit(solution)/shard_map/ppermute | solution.py:42
  75.2 8.8 %collective-permute-start.2 = (f32[2,32,512]{2,1,0:T(8,128)S(1)}, f32[2,32,512]{2,1,0:T(8,128)S(1)}, u32[]{:S(2)}, u32[]{:S(2)}) collective-permute-start(f32[2,32,512]{2,1,0:T(8,128)S(1)} %add.116), channel_id=1, source_target_pairs={{0,2},{1,3},{2,0},{3,1},{4,6},{5,7},{6,4},{7,5},{8,10},{9,11},{10,... | collective-permute-start | bytes 393224 | tf_op jit(solution)/shard_map/ppermute | solution.py:42
  76.1 8.4 %collective-permute-start.1 = (f32[2,32,512]{2,1,0:T(8,128)S(1)}, f32[2,32,512]{2,1,0:T(8,128)S(1)}, u32[]{:S(2)}, u32[]{:S(2)}) collective-permute-start(f32[2,32,512]{2,1,0:T(8,128)S(1)} %add.116), channel_id=1, source_target_pairs={{0,1},{1,0},{2,3},{3,2},{4,5},{5,4},{6,7},{7,6},{8,9},{9,8},{10,11... | collective-permute-start | bytes 393224 | tf_op jit(solution)/shard_map/ppermute | solution.py:42
  84.5 9.0 %collective-permute-start.6 = (f32[2,32,512]{2,1,0:T(8,128)S(1)}, f32[2,32,512]{2,1,0:T(8,128)S(1)}, u32[]{:S(2)}, u32[]{:S(2)}) collective-permute-start(f32[2,32,512]{2,1,0:T(8,128)S(1)} %add_add_fusion.3), channel_id=1, source_target_pairs={{0,24},{4,28},{8,16},{12,20},{16,8},{20,12},{24,0},{28,4},{32,56},... | collective-permute-start | bytes 393224 | tf_op jit(solution)/shard_map/ppermute | solution.py:42
  85.5 8.0 %collective-permute-start.5 = (f32[2,32,512]{2,1,0:T(8,128)S(1)}, f32[2,32,512]{2,1,0:T(8,128)S(1)}, u32[]{:S(2)}, u32[]{:S(2)}) collective-permute-start(f32[2,32,512]{2,1,0:T(8,128)S(1)} %add_add_fusion.3), channel_id=1, source_target_pairs={{0,16},{4,20},{8,24},{12,28},{16,0},{20,4},{24,8},{28,12},{32,48},... | collective-permute-start | bytes 393224 | tf_op jit(solution)/shard_map/ppermute | solution.py:42
  87.4 6.8 %collective-permute-start.4 = (f32[2,32,512]{2,1,0:T(8,128)S(1)}, f32[2,32,512]{2,1,0:T(8,128)S(1)}, u32[]{:S(2)}, u32[]{:S(2)}) collective-permute-start(f32[2,32,512]{2,1,0:T(8,128)S(1)} %add_add_fusion.3), channel_id=1, source_target_pairs={{0,8},{4,12},{8,0},{12,4},{16,24},{20,28},{24,16},{28,20},{32,40},... | collective-permute-start | bytes 393224 | tf_op jit(solution)/shard_map/ppermute | solution.py:42
  94.2 12.0 %collective-permute-start.9 = (f32[2,32,512]{2,1,0:T(8,128)S(1)}, f32[2,32,512]{2,1,0:T(8,128)S(1)}, u32[]{:S(2)}, u32[]{:S(2)}) collective-permute-start(f32[2,32,512]{2,1,0:T(8,128)S(1)} %add_add_fusion.2), channel_id=1, source_target_pairs={{0,96},{4,100},{8,104},{12,108},{16,112},{20,116},{24,120},{28,124... | collective-permute-start | bytes 393224 | tf_op jit(solution)/shard_map/ppermute | solution.py:42
  95.4 10.8 %collective-permute-start.8 = (f32[2,32,512]{2,1,0:T(8,128)S(1)}, f32[2,32,512]{2,1,0:T(8,128)S(1)}, u32[]{:S(2)}, u32[]{:S(2)}) collective-permute-start(f32[2,32,512]{2,1,0:T(8,128)S(1)} %add_add_fusion.2), channel_id=1, source_target_pairs={{0,64},{4,68},{8,72},{12,76},{16,80},{20,84},{24,88},{28,92},{32,9... | collective-permute-start | bytes 393224 | tf_op jit(solution)/shard_map/ppermute | solution.py:42
  97.1 9.1 %collective-permute-start.7 = (f32[2,32,512]{2,1,0:T(8,128)S(1)}, f32[2,32,512]{2,1,0:T(8,128)S(1)}, u32[]{:S(2)}, u32[]{:S(2)}) collective-permute-start(f32[2,32,512]{2,1,0:T(8,128)S(1)} %add_add_fusion.2), channel_id=1, source_target_pairs={{0,32},{4,36},{8,40},{12,44},{16,48},{20,52},{24,56},{28,60},{32,0... | collective-permute-start | bytes 393224 | tf_op jit(solution)/shard_map/ppermute | solution.py:42
  106.5 42.6 %copy-start.4 = (f32[2,2048]{1,0:T(2,128)S(1)}, f32[2,2048]{1,0:T(2,128)}, u32[]{:S(2)}) copy-start(f32[2,2048]{1,0:T(2,128)} %param.16) | copy-start | bytes 49156
  106.5 42.6 %copy-start.5 = (f32[2,2048]{1,0:T(2,128)S(1)}, f32[2,2048]{1,0:T(2,128)}, u32[]{:S(2)}) copy-start(f32[2,2048]{1,0:T(2,128)} %param.17) | copy-start | bytes 49156
  116.3 26.5 %all-to-all-start.2 = ((f32[128,1,1024]{2,1,0:T(1,128)}), f32[128,1,1024]{2,1,0:T(1,128)S(1)}, u32[]{:S(2)}, u32[]{:S(2)}) async-start(f32[128,1,1024]{2,1,0:T(1,128)} %all_to_all.27), calls=%async_computation.2 | async-start | bytes 1048576 | tf_op jit(solution)/shard_map/all_to_all | solution.py:49
  144.2 17.8 %all-to-all-start.3 = ((f32[128,1,1024]{2,1,0:T(1,128)}), f32[128,1,1024]{2,1,0:T(1,128)S(1)}, u32[]{:S(2)}, u32[]{:S(2)}) async-start(f32[128,1,1024]{2,1,0:T(1,128)} %broadcast_in_dim.17), calls=%async_computation.3 | async-start | bytes 1048576 | tf_op jit(solution)/shard_map/all_to_all | solution.py:52
  171.4 6.3 %collective-permute-start.10 = (f32[2,32,512]{2,1,0:T(8,128)S(1)}, f32[2,32,512]{2,1,0:T(8,128)S(1)}, u32[]{:S(2)}, u32[]{:S(2)}) collective-permute-start(f32[2,32,512]{2,1,0:T(8,128)S(1)} %fusion.4), channel_id=1, source_target_pairs={{0,4},{4,0},{8,12},{12,8},{16,20},{20,16},{24,28},{28,24},{32,36},... | collective-permute-start | bytes 393224 | tf_op jit(solution)/shard_map/ppermute | solution.py:40
  177.7 9.6 %collective-permute-start.13 = (f32[2,32,512]{2,1,0:T(8,128)S(1)}, f32[2,32,512]{2,1,0:T(8,128)S(1)}, u32[]{:S(2)}, u32[]{:S(2)}) collective-permute-start(f32[2,32,512]{2,1,0:T(8,128)S(1)} %add.126), channel_id=1, source_target_pairs={{0,3},{1,2},{2,1},{3,0},{4,7},{5,6},{6,5},{7,4},{8,11},{9,10},{10,... | collective-permute-start | bytes 393224 | tf_op jit(solution)/shard_map/ppermute | solution.py:42
  179.2 8.2 %collective-permute-start.12 = (f32[2,32,512]{2,1,0:T(8,128)S(1)}, f32[2,32,512]{2,1,0:T(8,128)S(1)}, u32[]{:S(2)}, u32[]{:S(2)}) collective-permute-start(f32[2,32,512]{2,1,0:T(8,128)S(1)} %add.126), channel_id=1, source_target_pairs={{0,2},{1,3},{2,0},{3,1},{4,6},{5,7},{6,4},{7,5},{8,10},{9,11},{10,... | collective-permute-start | bytes 393224 | tf_op jit(solution)/shard_map/ppermute | solution.py:42
  180.5 7.5 %collective-permute-start.11 = (f32[2,32,512]{2,1,0:T(8,128)S(1)}, f32[2,32,512]{2,1,0:T(8,128)S(1)}, u32[]{:S(2)}, u32[]{:S(2)}) collective-permute-start(f32[2,32,512]{2,1,0:T(8,128)S(1)} %add.126), channel_id=1, source_target_pairs={{0,1},{1,0},{2,3},{3,2},{4,5},{5,4},{6,7},{7,6},{8,9},{9,8},{10,11... | collective-permute-start | bytes 393224 | tf_op jit(solution)/shard_map/ppermute | solution.py:42
  188.0 9.2 %collective-permute-start.16 = (f32[2,32,512]{2,1,0:T(8,128)S(1)}, f32[2,32,512]{2,1,0:T(8,128)S(1)}, u32[]{:S(2)}, u32[]{:S(2)}) collective-permute-start(f32[2,32,512]{2,1,0:T(8,128)S(1)} %add_add_fusion.1), channel_id=1, source_target_pairs={{0,24},{4,28},{8,16},{12,20},{16,8},{20,12},{24,0},{28,4},{32,56},... | collective-permute-start | bytes 393224 | tf_op jit(solution)/shard_map/ppermute | solution.py:42
  189.1 8.1 %collective-permute-start.15 = (f32[2,32,512]{2,1,0:T(8,128)S(1)}, f32[2,32,512]{2,1,0:T(8,128)S(1)}, u32[]{:S(2)}, u32[]{:S(2)}) collective-permute-start(f32[2,32,512]{2,1,0:T(8,128)S(1)} %add_add_fusion.1), channel_id=1, source_target_pairs={{0,16},{4,20},{8,24},{12,28},{16,0},{20,4},{24,8},{28,12},{32,48},... | collective-permute-start | bytes 393224 | tf_op jit(solution)/shard_map/ppermute | solution.py:42
  191.0 6.2 %collective-permute-start.14 = (f32[2,32,512]{2,1,0:T(8,128)S(1)}, f32[2,32,512]{2,1,0:T(8,128)S(1)}, u32[]{:S(2)}, u32[]{:S(2)}) collective-permute-start(f32[2,32,512]{2,1,0:T(8,128)S(1)} %add_add_fusion.1), channel_id=1, source_target_pairs={{0,8},{4,12},{8,0},{12,4},{16,24},{20,28},{24,16},{28,20},{32,40},... | collective-permute-start | bytes 393224 | tf_op jit(solution)/shard_map/ppermute | solution.py:42
  197.2 4.3 %copy-start.2 = (f32[2,1,32,32]{2,3,1,0:T(8,128)}, f32[2,1,32,32]{2,3,1,0:T(8,128)S(1)}, u32[]{:S(2)}) copy-start(f32[2,1,32,32]{2,3,1,0:T(8,128)S(1)} %custom-call.10) | copy-start | bytes 24580
  197.3 6.3 %collective-permute-start.19 = (f32[2,32,512]{2,1,0:T(8,128)S(1)}, f32[2,32,512]{2,1,0:T(8,128)S(1)}, u32[]{:S(2)}, u32[]{:S(2)}) collective-permute-start(f32[2,32,512]{2,1,0:T(8,128)S(1)} %add_add_fusion), channel_id=1, source_target_pairs={{0,96},{4,100},{8,104},{12,108},{16,112},{20,116},{24,120},{28,124... | collective-permute-start | bytes 393224 | tf_op jit(solution)/shard_map/ppermute | solution.py:42
  198.5 6.5 %collective-permute-start.18 = (f32[2,32,512]{2,1,0:T(8,128)S(1)}, f32[2,32,512]{2,1,0:T(8,128)S(1)}, u32[]{:S(2)}, u32[]{:S(2)}) collective-permute-start(f32[2,32,512]{2,1,0:T(8,128)S(1)} %add_add_fusion), channel_id=1, source_target_pairs={{0,64},{4,68},{8,72},{12,76},{16,80},{20,84},{24,88},{28,92},{32,9... | collective-permute-start | bytes 393224 | tf_op jit(solution)/shard_map/ppermute | solution.py:42
  200.1 5.7 %collective-permute-start.17 = (f32[2,32,512]{2,1,0:T(8,128)S(1)}, f32[2,32,512]{2,1,0:T(8,128)S(1)}, u32[]{:S(2)}, u32[]{:S(2)}) collective-permute-start(f32[2,32,512]{2,1,0:T(8,128)S(1)} %add_add_fusion), channel_id=1, source_target_pairs={{0,32},{4,36},{8,40},{12,44},{16,48},{20,52},{24,56},{28,60},{32,0... | collective-permute-start | bytes 393224 | tf_op jit(solution)/shard_map/ppermute | solution.py:42
Sparse Core Ops, SparseCore 0:
  64.4 85.1 all-gather.2

commit v9 on v8

--- a/solution.py
+++ b/solution.py
@@ -69,7 +69,7 @@
     return jnp.einsum("mdk,mrd->mrk", merged, left_tr, precision=MID)
 
 
-TAIL_ROWS = 512
+TAIL_ROWS = 1024
 
 
 def tail_kernel(table, grads, errs, left_rows, right_t, carried, out_err, out_w, cbuf, ubuf, sems):

time: 234 us -> 232 us (level)
  Pallas kernels: 17.5 us -> 14.8 us
    pallas_call x1, Pallas kernels: 17.5 us -> 14.8 us  [tail(): pl.pallas_call(tail_kernel, grid_spec=spec, out_shape=[jax.ShapeDtypeStru...]
  transfers between devices with their start and end apart: 24 -> 24, of which waited for: 14 -> 14; matrix products, arithmetic and copies ran while one was open for 24% -> 25% of each run, Pallas kernels for 0% -> 0%
where the time goes in v9:
time: 232 us; the launch traced here: 231 us
  waiting for transfers between devices  56.8 us (24%)
  starting transfers between devices  42.7 us (18%)
  matrix products  36.2 us (16%)
  other arithmetic  29 us (12%)
  blocking collectives  24.9 us (11%)
  between operations  19.7 us (8%)
  Pallas kernels  14.8 us (6%)
  local copies, waits for them, and re-layouts  6.98 us (3%)
    all_to_all x2, waiting for transfers between devices, sum_all_to_all(): return lax.all_to_all(spread, axes, 0, 0, tiled=False).reshape(-1)  25.4 us
    ppermute x18, starting transfers between devices, sum_radix4(): r1, r2, r3 = [lax.ppermute(x, axis, perm) for axis, perm in parts]  25.2 us
    all_to_all x1, blocking collectives, sum_all_to_all(): rows = lax.all_to_all(x.reshape(count, -1), axes, 0, 0, tiled=False)  24.9 us
    ppermute x18, waiting for transfers between devices, sum_radix4(): r1, r2, r3 = [lax.ppermute(x, axis, perm) for axis, perm in parts]  18.3 us
    dot_general x2, matrix products, left_t(): return jnp.einsum('mdk,mrk->mrd', merged, right_t, precision=MID)  16.8 us
    pallas_call x1, Pallas kernels, tail(): pl.pallas_call(tail_kernel, grid_spec=spec, out_shape=[jax.ShapeDtypeStru...  14.8 us
    dot_general x2, matrix products, right_t_of(): return jnp.einsum('mdk,mrd->mrk', merged, left_tr, precision=MID)  14.4 us
    all_to_all x1, waiting for transfers between devices, sum_all_to_all(): rows = lax.all_to_all(x.reshape(count, -1), axes, 0, 0, tiled=False)  12.8 us
  transfers between devices with their start and end apart: 24, of which 14 were waited for; matrix products, arithmetic and copies ran while one was open for 25% of the time, Pallas kernels for 0%

profile of v9, /device:TPU:0, one launch (start us, length us, event | category | flops | bytes accessed | tf_op | source)
XLA Modules:
  0.0 231.1 jit_solution(16969872408931919874)
XLA Ops:
  8.1 8.4 %fusion.7 = f32[2,2048,32]{1,2,0:T(8,128)S(1)} fusion(f32[2,512,32]{1,2,0:T(8,128)S(1)} %copy-done, f32[1,2,2048,512]{3,2,1,0:T(8,128)} %param.13, bf16[1,2,2048,512]{3,2,1,0:T(8,128)(2,1)} %param.12), kind=kOutput, calls=%fused_computation.12 | convolution fusion | flops 406847488 | bytes 13238272 | tf_op jit(solution)/shard_map/mdk,mrk->mrd/dot_general | solution.py:65
  17.5 24.9 %all_to_all.32 = f32[128,1,1056]{2,1,0:T(1,128)S(1)} all-to-all(f32[128,1,1056]{2,1,0:T(1,128)S(1)} %all_to_all.26), channel_id=1, replica_groups=mesh['dp'=32,'group'=4] {'dp','group'}, dimensions={0} | all-to-all | bytes 1081344 | tf_op jit(solution)/shard_map/all_to_all | solution.py:49
  43.9 4.6 %all-to-all-start.1 = ((f32[128,1,1056]{2,1,0:T(1,128)}), f32[128,1,1056]{2,1,0:T(1,128)S(1)}, u32[]{:S(2)}, u32[]{:S(2)}) async-start(f32[128,1,1056]{2,1,0:T(1,128)} %broadcast_in_dim.16), calls=%async_computation.1 | async-start | bytes 1179648 | tf_op jit(solution)/shard_map/all_to_all | solution.py:52
  49.2 13.1 %all-to-all-done.1 = f32[128,1,1056]{2,1,0:T(1,128)S(1)} async-done(((f32[128,1,1056]{2,1,0:T(1,128)}), f32[128,1,1056]{2,1,0:T(1,128)S(1)}, u32[]{:S(2)}, u32[]{:S(2)}) %all-to-all-start.1) | async-done | bytes 540704 | tf_op jit(solution)/shard_map/all_to_all | solution.py:52
  62.4 1.4 reduce.6
  64.6 7.2 %fusion.6 = f32[2,32,512]{2,1,0:T(8,128)S(1)} fusion(f32[2,32,2048]{2,1,0:T(8,128)S(1)} %reshape.81, f32[1,2,2048,512]{3,2,1,0:T(8,128)} %param.13, bf16[1,2,2048,512]{3,2,1,0:T(8,128)(2,1)} %param.12), kind=kOutput, calls=%fused_computation.11 | convolution fusion | flops 406847488 | bytes 13238272 | tf_op jit(solution)/shard_map/mdk,mrd->mrk/dot_general | solution.py:69
  73.2 2.0 collective-permute-start.3
  76.1 1.4 collective-permute-start.1
  77.6 5.9 %custom-call.13 = f32[2,32,32]{2,1,0:T(8,128)S(1)} custom-call(f32[2,32,32]{2,1,0:T(8,128)S(1)} %fusion.24), custom_call_target="Cholesky" | custom-call | tf_op jit(solution)/shard_map/jit(cholesky)/cholesky | solution.py:57
  85.5 1.9 collective-permute-start.5
  88.9 4.7 %collective-permute-done.6 = f32[2,32,512]{2,1,0:T(8,128)S(1)} collective-permute-done((f32[2,32,512]{2,1,0:T(8,128)S(1)}, f32[2,32,512]{2,1,0:T(8,128)S(1)}, u32[]{:S(2)}, u32[]{:S(2)}) %collective-permute-start.6) | collective-permute-done | bytes 131104 | tf_op jit(solution)/shard_map/ppermute | solution.py:42
  95.4 1.7 collective-permute-start.8
  97.1 1.3 collective-permute-start.7
  98.5 4.9 %custom-call.14 = f32[2,1,32,32]{2,3,1,0:T(8,128)S(1)} custom-call(f32[2,1,32,32]{3,2,1,0:T(8,128)S(1)} %select_bitcast_fusion), custom_call_target="InvertDiagBlocksLowerTriangular" | custom-call | tf_op jit(solution)/shard_map/jit(_solve_triangular)/vmap()/triangular_solve | solution.py:61
  103.4 2.8 %collective-permute-done.9 = f32[2,32,512]{2,1,0:T(8,128)S(1)} collective-permute-done((f32[2,32,512]{2,1,0:T(8,128)S(1)}, f32[2,32,512]{2,1,0:T(8,128)S(1)}, u32[]{:S(2)}, u32[]{:S(2)}) %collective-permute-start.9) | collective-permute-done | bytes 131104 | tf_op jit(solution)/shard_map/ppermute | solution.py:42
  106.6 8.3 %fusion.5 = f32[2,32,2048]{2,1,0:T(8,128)S(1)} fusion(f32[2,32,512]{2,1,0:T(8,128)S(1)} %convolution_multiply_fusion.1, f32[1,2,2048,512]{3,2,1,0:T(8,128)} %param.13, bf16[1,2,2048,512]{3,2,1,0:T(8,128)(2,1)} %param.12), kind=kOutput, calls=%fused_computation.10 | convolution fusion | flops 406847488 | bytes 13238272 | tf_op jit(solution)/shard_map/mdk,mrk->mrd/dot_general | solution.py:65
  114.9 1.4 all_to_all.27
  116.3 7.1 %all-to-all-start.2 = ((f32[128,1,1024]{2,1,0:T(1,128)}), f32[128,1,1024]{2,1,0:T(1,128)S(1)}, u32[]{:S(2)}, u32[]{:S(2)}) async-start(f32[128,1,1024]{2,1,0:T(1,128)} %all_to_all.27), calls=%async_computation.2 | async-start | bytes 1048576 | tf_op jit(solution)/shard_map/all_to_all | solution.py:49
  130.0 12.8 %all-to-all-done.2 = f32[128,1,1024]{2,1,0:T(1,128)S(1)} async-done(((f32[128,1,1024]{2,1,0:T(1,128)}), f32[128,1,1024]{2,1,0:T(1,128)S(1)}, u32[]{:S(2)}, u32[]{:S(2)}) %all-to-all-start.2) | async-done | bytes 524320 | tf_op jit(solution)/shard_map/all_to_all | solution.py:49
  144.2 4.8 %all-to-all-start.3 = ((f32[128,1,1024]{2,1,0:T(1,128)}), f32[128,1,1024]{2,1,0:T(1,128)S(1)}, u32[]{:S(2)}, u32[]{:S(2)}) async-start(f32[128,1,1024]{2,1,0:T(1,128)} %broadcast_in_dim.17), calls=%async_computation.3 | async-start | bytes 1048576 | tf_op jit(solution)/shard_map/all_to_all | solution.py:52
  149.8 12.3 %all-to-all-done.3 = f32[128,1,1024]{2,1,0:T(1,128)S(1)} async-done(((f32[128,1,1024]{2,1,0:T(1,128)}), f32[128,1,1024]{2,1,0:T(1,128)S(1)}, u32[]{:S(2)}, u32[]{:S(2)}) %all-to-all-start.3) | async-done | bytes 524320 | tf_op jit(solution)/shard_map/all_to_all | solution.py:52
  164.2 7.2 %fusion.4 = f32[2,32,512]{2,1,0:T(8,128)S(1)} fusion(f32[2,32,2048]{2,1,0:T(8,128)S(1)} %reshape_reshape.4, f32[1,2,2048,512]{3,2,1,0:T(8,128)} %param.13, bf16[1,2,2048,512]{3,2,1,0:T(8,128)(2,1)} %param.12), kind=kOutput, calls=%fused_computation.9 | convolution fusion | flops 406847488 | bytes 13238272 | tf_op jit(solution)/shard_map/mdk,mrd->mrk/dot_general | solution.py:69
  171.8 5.9 %custom-call.15 = f32[2,32,32]{2,1,0:T(8,128)S(1)} custom-call(f32[2,32,32]{2,1,0:T(8,128)S(1)} %fusion.22), custom_call_target="Cholesky" | custom-call | tf_op jit(solution)/shard_map/jit(cholesky)/cholesky | solution.py:57
  177.7 1.4 collective-permute-start.13
  180.5 1.4 collective-permute-start.11
  182.0 5.3 %collective-permute-done.13 = f32[2,32,512]{2,1,0:T(8,128)S(1)} collective-permute-done((f32[2,32,512]{2,1,0:T(8,128)S(1)}, f32[2,32,512]{2,1,0:T(8,128)S(1)}, u32[]{:S(2)}, u32[]{:S(2)}) %collective-permute-start.13) | collective-permute-done | bytes 131104 | tf_op jit(solution)/shard_map/ppermute | solution.py:42
  189.1 1.9 collective-permute-start.15
  192.3 4.9 %custom-call.10 = f32[2,1,32,32]{2,3,1,0:T(8,128)S(1)} custom-call(f32[2,1,32,32]{3,2,1,0:T(8,128)S(1)} %fusion.25), custom_call_target="InvertDiagBlocksLowerTriangular" | custom-call | tf_op jit(solution)/shard_map/jit(_solve_triangular)/vmap()/triangular_solve | solution.py:61
  198.5 1.6 collective-permute-start.18
  200.1 1.4 collective-permute-start.17
  203.6 1.4 collective-permute-done.18
  209.4 14.8 %shard_map.128 = (f32[2,2048,512]{2,1,0:T(8,128)}, bf16[2,2048,512]{2,1,0:T(8,128)(2,1)}) custom-call(s32[128]{0:T(128)S(1)} %add_clamp_fusion.table, bf16[2,2048,512]{2,1,0:T(8,128)(2,1)} %bitcast.106, f32[2,2048,512]{2,1,0:T(8,128)} %bitcast.105, f32[2,2048,32]{2,1,0:T(8,128)S(1)} %bitcast.104, f32[2,32,512]{2,1,0:T(8,128)S(1)} %convolution_multiply_fusion.right_t, ...), custom_call_target="tpu_custom_call" | custom-call | flops 134217728 | bytes 33554432 | tf_op jit(solution)/shard_map/pallas_call | solution.py:135
  (91 shorter events, 31.1 us)
Async XLA Ops:
  7.2 0.9 copy-start
  8.1 40.4 %copy-start.1 = (f32[1,2,32,512]{3,2,1,0:T(8,128)S(1)}, f32[1,2,32,512]{3,2,1,0:T(8,128)}, u32[]{:S(2)}) copy-start(f32[1,2,32,512]{3,2,1,0:T(8,128)} %param.20) | copy-start | bytes 393220
  8.1 40.4 %copy-start.3 = (bf16[1,2,32,512]{3,2,1,0:T(8,128)(2,1)S(1)}, bf16[1,2,32,512]{3,2,1,0:T(8,128)(2,1)}, u32[]{:S(2)}) copy-start(bf16[1,2,32,512]{3,2,1,0:T(8,128)(2,1)} %param.19) | copy-start | bytes 196612
  8.1 56.3 %copy-start.6 = (s32[128]{0:T(128)S(1)}, s32[128]{0:T(128)}, u32[]{:S(2)}) copy-start(s32[128]{0:T(128)} %param.18) | copy-start | bytes 1540
  43.9 18.5 %all-to-all-start.1 = ((f32[128,1,1056]{2,1,0:T(1,128)}), f32[128,1,1056]{2,1,0:T(1,128)S(1)}, u32[]{:S(2)}, u32[]{:S(2)}) async-start(f32[128,1,1056]{2,1,0:T(1,128)} %broadcast_in_dim.16), calls=%async_computation.1 | async-start | bytes 1179648 | tf_op jit(solution)/shard_map/all_to_all | solution.py:52
  48.5 160.9 %all-gather.3.cloned.1.call-start = ((), (), s32[]{:S(2)}) async-start(), calls=%async_computation.4 | async-start | bytes 16908288 | tf_op jit(solution)/shard_map/all_gather | solution.py:175
  71.8 1.4 collective-permute-start
  73.2 10.8 %collective-permute-start.3 = (f32[2,32,512]{2,1,0:T(8,128)S(1)}, f32[2,32,512]{2,1,0:T(8,128)S(1)}, u32[]{:S(2)}, u32[]{:S(2)}) collective-permute-start(f32[2,32,512]{2,1,0:T(8,128)S(1)} %add.116), channel_id=1, source_target_pairs={{0,3},{1,2},{2,1},{3,0},{4,7},{5,6},{6,5},{7,4},{8,11},{9,10},{10,... | collective-permute-start | bytes 393224 | tf_op jit(solution)/shard_map/ppermute | solution.py:42
  75.2 8.8 %collective-permute-start.2 = (f32[2,32,512]{2,1,0:T(8,128)S(1)}, f32[2,32,512]{2,1,0:T(8,128)S(1)}, u32[]{:S(2)}, u32[]{:S(2)}) collective-permute-start(f32[2,32,512]{2,1,0:T(8,128)S(1)} %add.116), channel_id=1, source_target_pairs={{0,2},{1,3},{2,0},{3,1},{4,6},{5,7},{6,4},{7,5},{8,10},{9,11},{10,... | collective-permute-start | bytes 393224 | tf_op jit(solution)/shard_map/ppermute | solution.py:42
  76.1 8.4 %collective-permute-start.1 = (f32[2,32,512]{2,1,0:T(8,128)S(1)}, f32[2,32,512]{2,1,0:T(8,128)S(1)}, u32[]{:S(2)}, u32[]{:S(2)}) collective-permute-start(f32[2,32,512]{2,1,0:T(8,128)S(1)} %add.116), channel_id=1, source_target_pairs={{0,1},{1,0},{2,3},{3,2},{4,5},{5,4},{6,7},{7,6},{8,9},{9,8},{10,11... | collective-permute-start | bytes 393224 | tf_op jit(solution)/shard_map/ppermute | solution.py:42
  84.5 9.0 %collective-permute-start.6 = (f32[2,32,512]{2,1,0:T(8,128)S(1)}, f32[2,32,512]{2,1,0:T(8,128)S(1)}, u32[]{:S(2)}, u32[]{:S(2)}) collective-permute-start(f32[2,32,512]{2,1,0:T(8,128)S(1)} %add_add_fusion.3), channel_id=1, source_target_pairs={{0,24},{4,28},{8,16},{12,20},{16,8},{20,12},{24,0},{28,4},{32,56},... | collective-permute-start | bytes 393224 | tf_op jit(solution)/shard_map/ppermute | solution.py:42
  85.5 8.0 %collective-permute-start.5 = (f32[2,32,512]{2,1,0:T(8,128)S(1)}, f32[2,32,512]{2,1,0:T(8,128)S(1)}, u32[]{:S(2)}, u32[]{:S(2)}) collective-permute-start(f32[2,32,512]{2,1,0:T(8,128)S(1)} %add_add_fusion.3), channel_id=1, source_target_pairs={{0,16},{4,20},{8,24},{12,28},{16,0},{20,4},{24,8},{28,12},{32,48},... | collective-permute-start | bytes 393224 | tf_op jit(solution)/shard_map/ppermute | solution.py:42
  87.4 6.8 %collective-permute-start.4 = (f32[2,32,512]{2,1,0:T(8,128)S(1)}, f32[2,32,512]{2,1,0:T(8,128)S(1)}, u32[]{:S(2)}, u32[]{:S(2)}) collective-permute-start(f32[2,32,512]{2,1,0:T(8,128)S(1)} %add_add_fusion.3), channel_id=1, source_target_pairs={{0,8},{4,12},{8,0},{12,4},{16,24},{20,28},{24,16},{28,20},{32,40},... | collective-permute-start | bytes 393224 | tf_op jit(solution)/shard_map/ppermute | solution.py:42
  94.2 12.0 %collective-permute-start.9 = (f32[2,32,512]{2,1,0:T(8,128)S(1)}, f32[2,32,512]{2,1,0:T(8,128)S(1)}, u32[]{:S(2)}, u32[]{:S(2)}) collective-permute-start(f32[2,32,512]{2,1,0:T(8,128)S(1)} %add_add_fusion.2), channel_id=1, source_target_pairs={{0,96},{4,100},{8,104},{12,108},{16,112},{20,116},{24,120},{28,124... | collective-permute-start | bytes 393224 | tf_op jit(solution)/shard_map/ppermute | solution.py:42
  95.4 10.8 %collective-permute-start.8 = (f32[2,32,512]{2,1,0:T(8,128)S(1)}, f32[2,32,512]{2,1,0:T(8,128)S(1)}, u32[]{:S(2)}, u32[]{:S(2)}) collective-permute-start(f32[2,32,512]{2,1,0:T(8,128)S(1)} %add_add_fusion.2), channel_id=1, source_target_pairs={{0,64},{4,68},{8,72},{12,76},{16,80},{20,84},{24,88},{28,92},{32,9... | collective-permute-start | bytes 393224 | tf_op jit(solution)/shard_map/ppermute | solution.py:42
  97.1 9.1 %collective-permute-start.7 = (f32[2,32,512]{2,1,0:T(8,128)S(1)}, f32[2,32,512]{2,1,0:T(8,128)S(1)}, u32[]{:S(2)}, u32[]{:S(2)}) collective-permute-start(f32[2,32,512]{2,1,0:T(8,128)S(1)} %add_add_fusion.2), channel_id=1, source_target_pairs={{0,32},{4,36},{8,40},{12,44},{16,48},{20,52},{24,56},{28,60},{32,0... | collective-permute-start | bytes 393224 | tf_op jit(solution)/shard_map/ppermute | solution.py:42
  106.5 42.6 %copy-start.4 = (f32[2,2048]{1,0:T(2,128)S(1)}, f32[2,2048]{1,0:T(2,128)}, u32[]{:S(2)}) copy-start(f32[2,2048]{1,0:T(2,128)} %param.16) | copy-start | bytes 49156
  106.5 42.6 %copy-start.5 = (f32[2,2048]{1,0:T(2,128)S(1)}, f32[2,2048]{1,0:T(2,128)}, u32[]{:S(2)}) copy-start(f32[2,2048]{1,0:T(2,128)} %param.17) | copy-start | bytes 49156
  116.3 26.5 %all-to-all-start.2 = ((f32[128,1,1024]{2,1,0:T(1,128)}), f32[128,1,1024]{2,1,0:T(1,128)S(1)}, u32[]{:S(2)}, u32[]{:S(2)}) async-start(f32[128,1,1024]{2,1,0:T(1,128)} %all_to_all.27), calls=%async_computation.2 | async-start | bytes 1048576 | tf_op jit(solution)/shard_map/all_to_all | solution.py:49
  144.2 17.8 %all-to-all-start.3 = ((f32[128,1,1024]{2,1,0:T(1,128)}), f32[128,1,1024]{2,1,0:T(1,128)S(1)}, u32[]{:S(2)}, u32[]{:S(2)}) async-start(f32[128,1,1024]{2,1,0:T(1,128)} %broadcast_in_dim.17), calls=%async_computation.3 | async-start | bytes 1048576 | tf_op jit(solution)/shard_map/all_to_all | solution.py:52
  171.4 6.3 %collective-permute-start.10 = (f32[2,32,512]{2,1,0:T(8,128)S(1)}, f32[2,32,512]{2,1,0:T(8,128)S(1)}, u32[]{:S(2)}, u32[]{:S(2)}) collective-permute-start(f32[2,32,512]{2,1,0:T(8,128)S(1)} %fusion.4), channel_id=1, source_target_pairs={{0,4},{4,0},{8,12},{12,8},{16,20},{20,16},{24,28},{28,24},{32,36},... | collective-permute-start | bytes 393224 | tf_op jit(solution)/shard_map/ppermute | solution.py:40
  177.7 9.6 %collective-permute-start.13 = (f32[2,32,512]{2,1,0:T(8,128)S(1)}, f32[2,32,512]{2,1,0:T(8,128)S(1)}, u32[]{:S(2)}, u32[]{:S(2)}) collective-permute-start(f32[2,32,512]{2,1,0:T(8,128)S(1)} %add.126), channel_id=1, source_target_pairs={{0,3},{1,2},{2,1},{3,0},{4,7},{5,6},{6,5},{7,4},{8,11},{9,10},{10,... | collective-permute-start | bytes 393224 | tf_op jit(solution)/shard_map/ppermute | solution.py:42
  179.2 8.2 %collective-permute-start.12 = (f32[2,32,512]{2,1,0:T(8,128)S(1)}, f32[2,32,512]{2,1,0:T(8,128)S(1)}, u32[]{:S(2)}, u32[]{:S(2)}) collective-permute-start(f32[2,32,512]{2,1,0:T(8,128)S(1)} %add.126), channel_id=1, source_target_pairs={{0,2},{1,3},{2,0},{3,1},{4,6},{5,7},{6,4},{7,5},{8,10},{9,11},{10,... | collective-permute-start | bytes 393224 | tf_op jit(solution)/shard_map/ppermute | solution.py:42
  180.5 7.5 %collective-permute-start.11 = (f32[2,32,512]{2,1,0:T(8,128)S(1)}, f32[2,32,512]{2,1,0:T(8,128)S(1)}, u32[]{:S(2)}, u32[]{:S(2)}) collective-permute-start(f32[2,32,512]{2,1,0:T(8,128)S(1)} %add.126), channel_id=1, source_target_pairs={{0,1},{1,0},{2,3},{3,2},{4,5},{5,4},{6,7},{7,6},{8,9},{9,8},{10,11... | collective-permute-start | bytes 393224 | tf_op jit(solution)/shard_map/ppermute | solution.py:42
  188.0 9.2 %collective-permute-start.16 = (f32[2,32,512]{2,1,0:T(8,128)S(1)}, f32[2,32,512]{2,1,0:T(8,128)S(1)}, u32[]{:S(2)}, u32[]{:S(2)}) collective-permute-start(f32[2,32,512]{2,1,0:T(8,128)S(1)} %add_add_fusion.1), channel_id=1, source_target_pairs={{0,24},{4,28},{8,16},{12,20},{16,8},{20,12},{24,0},{28,4},{32,56},... | collective-permute-start | bytes 393224 | tf_op jit(solution)/shard_map/ppermute | solution.py:42
  189.1 8.1 %collective-permute-start.15 = (f32[2,32,512]{2,1,0:T(8,128)S(1)}, f32[2,32,512]{2,1,0:T(8,128)S(1)}, u32[]{:S(2)}, u32[]{:S(2)}) collective-permute-start(f32[2,32,512]{2,1,0:T(8,128)S(1)} %add_add_fusion.1), channel_id=1, source_target_pairs={{0,16},{4,20},{8,24},{12,28},{16,0},{20,4},{24,8},{28,12},{32,48},... | collective-permute-start | bytes 393224 | tf_op jit(solution)/shard_map/ppermute | solution.py:42
  191.0 6.2 %collective-permute-start.14 = (f32[2,32,512]{2,1,0:T(8,128)S(1)}, f32[2,32,512]{2,1,0:T(8,128)S(1)}, u32[]{:S(2)}, u32[]{:S(2)}) collective-permute-start(f32[2,32,512]{2,1,0:T(8,128)S(1)} %add_add_fusion.1), channel_id=1, source_target_pairs={{0,8},{4,12},{8,0},{12,4},{16,24},{20,28},{24,16},{28,20},{32,40},... | collective-permute-start | bytes 393224 | tf_op jit(solution)/shard_map/ppermute | solution.py:42
  197.2 4.3 %copy-start.2 = (f32[2,1,32,32]{2,3,1,0:T(8,128)}, f32[2,1,32,32]{2,3,1,0:T(8,128)S(1)}, u32[]{:S(2)}) copy-start(f32[2,1,32,32]{2,3,1,0:T(8,128)S(1)} %custom-call.10) | copy-start | bytes 24580
  197.3 6.3 %collective-permute-start.19 = (f32[2,32,512]{2,1,0:T(8,128)S(1)}, f32[2,32,512]{2,1,0:T(8,128)S(1)}, u32[]{:S(2)}, u32[]{:S(2)}) collective-permute-start(f32[2,32,512]{2,1,0:T(8,128)S(1)} %add_add_fusion), channel_id=1, source_target_pairs={{0,96},{4,100},{8,104},{12,108},{16,112},{20,116},{24,120},{28,124... | collective-permute-start | bytes 393224 | tf_op jit(solution)/shard_map/ppermute | solution.py:42
  198.5 6.5 %collective-permute-start.18 = (f32[2,32,512]{2,1,0:T(8,128)S(1)}, f32[2,32,512]{2,1,0:T(8,128)S(1)}, u32[]{:S(2)}, u32[]{:S(2)}) collective-permute-start(f32[2,32,512]{2,1,0:T(8,128)S(1)} %add_add_fusion), channel_id=1, source_target_pairs={{0,64},{4,68},{8,72},{12,76},{16,80},{20,84},{24,88},{28,92},{32,9... | collective-permute-start | bytes 393224 | tf_op jit(solution)/shard_map/ppermute | solution.py:42
  200.1 5.7 %collective-permute-start.17 = (f32[2,32,512]{2,1,0:T(8,128)S(1)}, f32[2,32,512]{2,1,0:T(8,128)S(1)}, u32[]{:S(2)}, u32[]{:S(2)}) collective-permute-start(f32[2,32,512]{2,1,0:T(8,128)S(1)} %add_add_fusion), channel_id=1, source_target_pairs={{0,32},{4,36},{8,40},{12,44},{16,48},{20,52},{24,56},{28,60},{32,0... | collective-permute-start | bytes 393224 | tf_op jit(solution)/shard_map/ppermute | solution.py:42
Sparse Core Ops, SparseCore 0:
  64.4 85.1 all-gather.2

commit v10 on v9

--- a/solution.py
+++ b/solution.py
@@ -69,7 +69,7 @@
     return jnp.einsum("mdk,mrd->mrk", merged, left_tr, precision=MID)
 
 
-TAIL_ROWS = 1024
+TAIL_ROWS = 2048
 
 
 def tail_kernel(table, grads, errs, left_rows, right_t, carried, out_err, out_w, cbuf, ubuf, sems):
@@ -141,7 +141,7 @@
         ],
         cost_estimate=cost,
         compiler_params=pltpu.CompilerParams(
-            dimension_semantics=("arbitrary", "arbitrary"), vmem_limit_bytes=48 * 1024 * 1024
+            dimension_semantics=("arbitrary", "arbitrary"), vmem_limit_bytes=56 * 1024 * 1024
         ),
     )(table, grads, errs, left_rows, right_t, carried)
 

time: 232 us -> 230 us (level)
  transfers between devices with their start and end apart: 24 -> 24, of which waited for: 14 -> 13; matrix products, arithmetic and copies ran while one was open for 25% -> 25% of each run, Pallas kernels for 0% -> 0%
where the time goes in v10:
time: 230 us; the launch traced here: 229 us
  waiting for transfers between devices  54.9 us (24%)
  starting transfers between devices  42.7 us (19%)
  matrix products  35.4 us (15%)
  other arithmetic  29.6 us (13%)
  blocking collectives  24.9 us (11%)
  between operations  19.6 us (9%)
  Pallas kernels  13.6 us (6%)
  local copies, waits for them, and re-layouts  8.33 us (4%)
    all_to_all x2, waiting for transfers between devices, sum_all_to_all(): return lax.all_to_all(spread, axes, 0, 0, tiled=False).reshape(-1)  25.4 us
    ppermute x18, starting transfers between devices, sum_radix4(): r1, r2, r3 = [lax.ppermute(x, axis, perm) for axis, perm in parts]  25.2 us
    all_to_all x1, blocking collectives, sum_all_to_all(): rows = lax.all_to_all(x.reshape(count, -1), axes, 0, 0, tiled=False)  24.9 us
    ppermute x18, waiting for transfers between devices, sum_radix4(): r1, r2, r3 = [lax.ppermute(x, axis, perm) for axis, perm in parts]  16.9 us
    dot_general x2, matrix products, left_t(): return jnp.einsum('mdk,mrk->mrd', merged, right_t, precision=MID)  16.8 us
    dot_general x2, matrix products, right_t_of(): return jnp.einsum('mdk,mrd->mrk', merged, left_tr, precision=MID)  14.4 us
    pallas_call x1, Pallas kernels, tail(): pl.pallas_call(tail_kernel, grid_spec=spec, out_shape=[jax.ShapeDtypeStru...  13.6 us
    all_to_all x1, waiting for transfers between devices, sum_all_to_all(): rows = lax.all_to_all(x.reshape(count, -1), axes, 0, 0, tiled=False)  12.2 us
  transfers between devices with their start and end apart: 24, of which 13 were waited for; matrix products, arithmetic and copies ran while one was open for 25% of the time, Pallas kernels for 0%

profile of v10, /device:TPU:0, one launch (start us, length us, event | category | flops | bytes accessed | tf_op | source)
XLA Modules:
  0.0 229.1 jit_solution(13747159204930938141)
XLA Ops:
  8.1 8.4 %fusion.7 = f32[2,2048,32]{1,2,0:T(8,128)S(1)} fusion(f32[2,512,32]{1,2,0:T(8,128)S(1)} %copy-done, f32[1,2,2048,512]{3,2,1,0:T(8,128)} %param.13, bf16[1,2,2048,512]{3,2,1,0:T(8,128)(2,1)} %param.12), kind=kOutput, calls=%fused_computation.12 | convolution fusion | flops 406847488 | bytes 13238272 | tf_op jit(solution)/shard_map/mdk,mrk->mrd/dot_general | solution.py:65
  17.5 24.9 %all_to_all.32 = f32[128,1,1056]{2,1,0:T(1,128)S(1)} all-to-all(f32[128,1,1056]{2,1,0:T(1,128)S(1)} %all_to_all.26), channel_id=1, replica_groups=mesh['dp'=32,'group'=4] {'dp','group'}, dimensions={0} | all-to-all | bytes 1081344 | tf_op jit(solution)/shard_map/all_to_all | solution.py:49
  43.9 4.6 %all-to-all-start.1 = ((f32[128,1,1056]{2,1,0:T(1,128)}), f32[128,1,1056]{2,1,0:T(1,128)S(1)}, u32[]{:S(2)}, u32[]{:S(2)}) async-start(f32[128,1,1056]{2,1,0:T(1,128)} %broadcast_in_dim.16), calls=%async_computation.1 | async-start | bytes 1179648 | tf_op jit(solution)/shard_map/all_to_all | solution.py:52
  49.2 13.1 %all-to-all-done.1 = f32[128,1,1056]{2,1,0:T(1,128)S(1)} async-done(((f32[128,1,1056]{2,1,0:T(1,128)}), f32[128,1,1056]{2,1,0:T(1,128)S(1)}, u32[]{:S(2)}, u32[]{:S(2)}) %all-to-all-start.1) | async-done | bytes 540704 | tf_op jit(solution)/shard_map/all_to_all | solution.py:52
  62.4 1.4 reduce.6
  64.6 7.2 %fusion.6 = f32[2,32,512]{2,1,0:T(8,128)S(1)} fusion(f32[2,32,2048]{2,1,0:T(8,128)S(1)} %reshape.81, f32[1,2,2048,512]{3,2,1,0:T(8,128)} %param.13, bf16[1,2,2048,512]{3,2,1,0:T(8,128)(2,1)} %param.12), kind=kOutput, calls=%fused_computation.11 | convolution fusion | flops 406847488 | bytes 13238272 | tf_op jit(solution)/shard_map/mdk,mrd->mrk/dot_general | solution.py:69
  73.2 2.0 collective-permute-start.3
  76.1 1.4 collective-permute-start.1
  77.6 5.9 %custom-call.13 = f32[2,32,32]{2,1,0:T(8,128)S(1)} custom-call(f32[2,32,32]{2,1,0:T(8,128)S(1)} %fusion.24), custom_call_target="Cholesky" | custom-call | tf_op jit(solution)/shard_map/jit(cholesky)/cholesky | solution.py:57
  85.5 1.9 collective-permute-start.5
  88.9 4.7 %collective-permute-done.6 = f32[2,32,512]{2,1,0:T(8,128)S(1)} collective-permute-done((f32[2,32,512]{2,1,0:T(8,128)S(1)}, f32[2,32,512]{2,1,0:T(8,128)S(1)}, u32[]{:S(2)}, u32[]{:S(2)}) %collective-permute-start.6) | collective-permute-done | bytes 131104 | tf_op jit(solution)/shard_map/ppermute | solution.py:42
  95.4 1.7 collective-permute-start.8
  97.1 1.3 collective-permute-start.7
  98.5 4.9 %custom-call.14 = f32[2,1,32,32]{2,3,1,0:T(8,128)S(1)} custom-call(f32[2,1,32,32]{3,2,1,0:T(8,128)S(1)} %select_bitcast_fusion), custom_call_target="InvertDiagBlocksLowerTriangular" | custom-call | tf_op jit(solution)/shard_map/jit(_solve_triangular)/vmap()/triangular_solve | solution.py:61
  103.4 2.8 %collective-permute-done.9 = f32[2,32,512]{2,1,0:T(8,128)S(1)} collective-permute-done((f32[2,32,512]{2,1,0:T(8,128)S(1)}, f32[2,32,512]{2,1,0:T(8,128)S(1)}, u32[]{:S(2)}, u32[]{:S(2)}) %collective-permute-start.9) | collective-permute-done | bytes 131104 | tf_op jit(solution)/shard_map/ppermute | solution.py:42
  106.6 8.3 %fusion.5 = f32[2,32,2048]{2,1,0:T(8,128)S(1)} fusion(f32[2,32,512]{2,1,0:T(8,128)S(1)} %convolution_multiply_fusion.1, f32[1,2,2048,512]{3,2,1,0:T(8,128)} %param.13, bf16[1,2,2048,512]{3,2,1,0:T(8,128)(2,1)} %param.12), kind=kOutput, calls=%fused_computation.10 | convolution fusion | flops 406847488 | bytes 13238272 | tf_op jit(solution)/shard_map/mdk,mrk->mrd/dot_general | solution.py:65
  114.9 1.4 all_to_all.27
  116.3 7.1 %all-to-all-start.2 = ((f32[128,1,1024]{2,1,0:T(1,128)}), f32[128,1,1024]{2,1,0:T(1,128)S(1)}, u32[]{:S(2)}, u32[]{:S(2)}) async-start(f32[128,1,1024]{2,1,0:T(1,128)} %all_to_all.27), calls=%async_computation.2 | async-start | bytes 1048576 | tf_op jit(solution)/shard_map/all_to_all | solution.py:49
  130.6 12.2 %all-to-all-done.2 = f32[128,1,1024]{2,1,0:T(1,128)S(1)} async-done(((f32[128,1,1024]{2,1,0:T(1,128)}), f32[128,1,1024]{2,1,0:T(1,128)S(1)}, u32[]{:S(2)}, u32[]{:S(2)}) %all-to-all-start.2) | async-done | bytes 524320 | tf_op jit(solution)/shard_map/all_to_all | solution.py:49
  144.2 4.8 %all-to-all-start.3 = ((f32[128,1,1024]{2,1,0:T(1,128)}), f32[128,1,1024]{2,1,0:T(1,128)S(1)}, u32[]{:S(2)}, u32[]{:S(2)}) async-start(f32[128,1,1024]{2,1,0:T(1,128)} %broadcast_in_dim.17), calls=%async_computation.3 | async-start | bytes 1048576 | tf_op jit(solution)/shard_map/all_to_all | solution.py:52
  149.8 12.3 %all-to-all-done.3 = f32[128,1,1024]{2,1,0:T(1,128)S(1)} async-done(((f32[128,1,1024]{2,1,0:T(1,128)}), f32[128,1,1024]{2,1,0:T(1,128)S(1)}, u32[]{:S(2)}, u32[]{:S(2)}) %all-to-all-start.3) | async-done | bytes 524320 | tf_op jit(solution)/shard_map/all_to_all | solution.py:52
  164.1 7.2 %fusion.4 = f32[2,32,512]{2,1,0:T(8,128)S(1)} fusion(f32[2,32,2048]{2,1,0:T(8,128)S(1)} %reshape_reshape.4, f32[1,2,2048,512]{3,2,1,0:T(8,128)} %param.13, bf16[1,2,2048,512]{3,2,1,0:T(8,128)(2,1)} %param.12), kind=kOutput, calls=%fused_computation.9 | convolution fusion | flops 406847488 | bytes 13238272 | tf_op jit(solution)/shard_map/mdk,mrd->mrk/dot_general | solution.py:69
  171.8 5.9 %custom-call.15 = f32[2,32,32]{2,1,0:T(8,128)S(1)} custom-call(f32[2,32,32]{2,1,0:T(8,128)S(1)} %fusion.22), custom_call_target="Cholesky" | custom-call | tf_op jit(solution)/shard_map/jit(cholesky)/cholesky | solution.py:57
  177.7 1.4 collective-permute-start.13
  180.4 1.4 collective-permute-start.11
  182.0 5.3 %collective-permute-done.13 = f32[2,32,512]{2,1,0:T(8,128)S(1)} collective-permute-done((f32[2,32,512]{2,1,0:T(8,128)S(1)}, f32[2,32,512]{2,1,0:T(8,128)S(1)}, u32[]{:S(2)}, u32[]{:S(2)}) %collective-permute-start.13) | collective-permute-done | bytes 131104 | tf_op jit(solution)/shard_map/ppermute | solution.py:42
  189.1 1.9 collective-permute-start.15
  192.2 4.9 %custom-call.10 = f32[2,1,32,32]{2,3,1,0:T(8,128)S(1)} custom-call(f32[2,1,32,32]{3,2,1,0:T(8,128)S(1)} %fusion.25), custom_call_target="InvertDiagBlocksLowerTriangular" | custom-call | tf_op jit(solution)/shard_map/jit(_solve_triangular)/vmap()/triangular_solve | solution.py:61
  198.4 1.6 collective-permute-start.18
  200.0 1.4 collective-permute-start.17
  202.0 2.0 copy.42
  208.6 13.6 %shard_map.128 = (f32[2,2048,512]{2,1,0:T(8,128)}, bf16[2,2048,512]{2,1,0:T(8,128)(2,1)}) custom-call(s32[128]{0:T(128)} %add_clamp_fusion.table, bf16[2,2048,512]{2,1,0:T(8,128)(2,1)} %bitcast.105, f32[2,2048,512]{2,1,0:T(8,128)} %bitcast.104, f32[2,2048,32]{2,1,0:T(8,128)} %bitcast.106, f32[2,32,512]{2,1,0:T(8,128)} %copy-done.1, ...), custom_call_target="tpu_custom_call" | custom-call | flops 134217728 | bytes 33554432 | tf_op jit(solution)/shard_map/pallas_call | solution.py:135
  (91 shorter events, 30.5 us)
Async XLA Ops:
  7.2 0.9 copy-start
  8.1 40.4 %copy-start.2 = (f32[1,2,32,512]{3,2,1,0:T(8,128)S(1)}, f32[1,2,32,512]{3,2,1,0:T(8,128)}, u32[]{:S(2)}) copy-start(f32[1,2,32,512]{3,2,1,0:T(8,128)} %param.20) | copy-start | bytes 393220
  8.1 40.4 %copy-start.3 = (bf16[1,2,32,512]{3,2,1,0:T(8,128)(2,1)S(1)}, bf16[1,2,32,512]{3,2,1,0:T(8,128)(2,1)}, u32[]{:S(2)}) copy-start(bf16[1,2,32,512]{3,2,1,0:T(8,128)(2,1)} %param.19) | copy-start | bytes 196612
  8.1 56.3 %copy-start.6 = (s32[128]{0:T(128)S(1)}, s32[128]{0:T(128)}, u32[]{:S(2)}) copy-start(s32[128]{0:T(128)} %param.18) | copy-start | bytes 1540
  43.9 18.5 %all-to-all-start.1 = ((f32[128,1,1056]{2,1,0:T(1,128)}), f32[128,1,1056]{2,1,0:T(1,128)S(1)}, u32[]{:S(2)}, u32[]{:S(2)}) async-start(f32[128,1,1056]{2,1,0:T(1,128)} %broadcast_in_dim.16), calls=%async_computation.1 | async-start | bytes 1179648 | tf_op jit(solution)/shard_map/all_to_all | solution.py:52
  48.5 160.1 %all-gather.3.cloned.1.call-start = ((), (), s32[]{:S(2)}) async-start(), calls=%async_computation.4 | async-start | bytes 16908288 | tf_op jit(solution)/shard_map/all_gather | solution.py:175
  71.8 1.4 collective-permute-start
  73.2 10.8 %collective-permute-start.3 = (f32[2,32,512]{2,1,0:T(8,128)S(1)}, f32[2,32,512]{2,1,0:T(8,128)S(1)}, u32[]{:S(2)}, u32[]{:S(2)}) collective-permute-start(f32[2,32,512]{2,1,0:T(8,128)S(1)} %add.116), channel_id=1, source_target_pairs={{0,3},{1,2},{2,1},{3,0},{4,7},{5,6},{6,5},{7,4},{8,11},{9,10},{10,... | collective-permute-start | bytes 393224 | tf_op jit(solution)/shard_map/ppermute | solution.py:42
  75.2 8.8 %collective-permute-start.2 = (f32[2,32,512]{2,1,0:T(8,128)S(1)}, f32[2,32,512]{2,1,0:T(8,128)S(1)}, u32[]{:S(2)}, u32[]{:S(2)}) collective-permute-start(f32[2,32,512]{2,1,0:T(8,128)S(1)} %add.116), channel_id=1, source_target_pairs={{0,2},{1,3},{2,0},{3,1},{4,6},{5,7},{6,4},{7,5},{8,10},{9,11},{10,... | collective-permute-start | bytes 393224 | tf_op jit(solution)/shard_map/ppermute | solution.py:42
  76.1 8.4 %collective-permute-start.1 = (f32[2,32,512]{2,1,0:T(8,128)S(1)}, f32[2,32,512]{2,1,0:T(8,128)S(1)}, u32[]{:S(2)}, u32[]{:S(2)}) collective-permute-start(f32[2,32,512]{2,1,0:T(8,128)S(1)} %add.116), channel_id=1, source_target_pairs={{0,1},{1,0},{2,3},{3,2},{4,5},{5,4},{6,7},{7,6},{8,9},{9,8},{10,11... | collective-permute-start | bytes 393224 | tf_op jit(solution)/shard_map/ppermute | solution.py:42
  84.5 9.0 %collective-permute-start.6 = (f32[2,32,512]{2,1,0:T(8,128)S(1)}, f32[2,32,512]{2,1,0:T(8,128)S(1)}, u32[]{:S(2)}, u32[]{:S(2)}) collective-permute-start(f32[2,32,512]{2,1,0:T(8,128)S(1)} %add_add_fusion.3), channel_id=1, source_target_pairs={{0,24},{4,28},{8,16},{12,20},{16,8},{20,12},{24,0},{28,4},{32,56},... | collective-permute-start | bytes 393224 | tf_op jit(solution)/shard_map/ppermute | solution.py:42
  85.5 8.0 %collective-permute-start.5 = (f32[2,32,512]{2,1,0:T(8,128)S(1)}, f32[2,32,512]{2,1,0:T(8,128)S(1)}, u32[]{:S(2)}, u32[]{:S(2)}) collective-permute-start(f32[2,32,512]{2,1,0:T(8,128)S(1)} %add_add_fusion.3), channel_id=1, source_target_pairs={{0,16},{4,20},{8,24},{12,28},{16,0},{20,4},{24,8},{28,12},{32,48},... | collective-permute-start | bytes 393224 | tf_op jit(solution)/shard_map/ppermute | solution.py:42
  87.4 6.8 %collective-permute-start.4 = (f32[2,32,512]{2,1,0:T(8,128)S(1)}, f32[2,32,512]{2,1,0:T(8,128)S(1)}, u32[]{:S(2)}, u32[]{:S(2)}) collective-permute-start(f32[2,32,512]{2,1,0:T(8,128)S(1)} %add_add_fusion.3), channel_id=1, source_target_pairs={{0,8},{4,12},{8,0},{12,4},{16,24},{20,28},{24,16},{28,20},{32,40},... | collective-permute-start | bytes 393224 | tf_op jit(solution)/shard_map/ppermute | solution.py:42
  94.2 12.0 %collective-permute-start.9 = (f32[2,32,512]{2,1,0:T(8,128)S(1)}, f32[2,32,512]{2,1,0:T(8,128)S(1)}, u32[]{:S(2)}, u32[]{:S(2)}) collective-permute-start(f32[2,32,512]{2,1,0:T(8,128)S(1)} %add_add_fusion.2), channel_id=1, source_target_pairs={{0,96},{4,100},{8,104},{12,108},{16,112},{20,116},{24,120},{28,124... | collective-permute-start | bytes 393224 | tf_op jit(solution)/shard_map/ppermute | solution.py:42
  95.4 10.8 %collective-permute-start.8 = (f32[2,32,512]{2,1,0:T(8,128)S(1)}, f32[2,32,512]{2,1,0:T(8,128)S(1)}, u32[]{:S(2)}, u32[]{:S(2)}) collective-permute-start(f32[2,32,512]{2,1,0:T(8,128)S(1)} %add_add_fusion.2), channel_id=1, source_target_pairs={{0,64},{4,68},{8,72},{12,76},{16,80},{20,84},{24,88},{28,92},{32,9... | collective-permute-start | bytes 393224 | tf_op jit(solution)/shard_map/ppermute | solution.py:42
  97.1 9.1 %collective-permute-start.7 = (f32[2,32,512]{2,1,0:T(8,128)S(1)}, f32[2,32,512]{2,1,0:T(8,128)S(1)}, u32[]{:S(2)}, u32[]{:S(2)}) collective-permute-start(f32[2,32,512]{2,1,0:T(8,128)S(1)} %add_add_fusion.2), channel_id=1, source_target_pairs={{0,32},{4,36},{8,40},{12,44},{16,48},{20,52},{24,56},{28,60},{32,0... | collective-permute-start | bytes 393224 | tf_op jit(solution)/shard_map/ppermute | solution.py:42
  106.5 42.6 %copy-start.4 = (f32[2,2048]{1,0:T(2,128)S(1)}, f32[2,2048]{1,0:T(2,128)}, u32[]{:S(2)}) copy-start(f32[2,2048]{1,0:T(2,128)} %param.16) | copy-start | bytes 49156
  106.5 42.6 %copy-start.5 = (f32[2,2048]{1,0:T(2,128)S(1)}, f32[2,2048]{1,0:T(2,128)}, u32[]{:S(2)}) copy-start(f32[2,2048]{1,0:T(2,128)} %param.17) | copy-start | bytes 49156
  116.3 26.5 %all-to-all-start.2 = ((f32[128,1,1024]{2,1,0:T(1,128)}), f32[128,1,1024]{2,1,0:T(1,128)S(1)}, u32[]{:S(2)}, u32[]{:S(2)}) async-start(f32[128,1,1024]{2,1,0:T(1,128)} %all_to_all.27), calls=%async_computation.2 | async-start | bytes 1048576 | tf_op jit(solution)/shard_map/all_to_all | solution.py:49
  144.2 17.8 %all-to-all-start.3 = ((f32[128,1,1024]{2,1,0:T(1,128)}), f32[128,1,1024]{2,1,0:T(1,128)S(1)}, u32[]{:S(2)}, u32[]{:S(2)}) async-start(f32[128,1,1024]{2,1,0:T(1,128)} %broadcast_in_dim.17), calls=%async_computation.3 | async-start | bytes 1048576 | tf_op jit(solution)/shard_map/all_to_all | solution.py:52
  171.3 6.3 %collective-permute-start.10 = (f32[2,32,512]{2,1,0:T(8,128)S(1)}, f32[2,32,512]{2,1,0:T(8,128)S(1)}, u32[]{:S(2)}, u32[]{:S(2)}) collective-permute-start(f32[2,32,512]{2,1,0:T(8,128)S(1)} %fusion.4), channel_id=1, source_target_pairs={{0,4},{4,0},{8,12},{12,8},{16,20},{20,16},{24,28},{28,24},{32,36},... | collective-permute-start | bytes 393224 | tf_op jit(solution)/shard_map/ppermute | solution.py:40
  177.7 9.6 %collective-permute-start.13 = (f32[2,32,512]{2,1,0:T(8,128)S(1)}, f32[2,32,512]{2,1,0:T(8,128)S(1)}, u32[]{:S(2)}, u32[]{:S(2)}) collective-permute-start(f32[2,32,512]{2,1,0:T(8,128)S(1)} %add.126), channel_id=1, source_target_pairs={{0,3},{1,2},{2,1},{3,0},{4,7},{5,6},{6,5},{7,4},{8,11},{9,10},{10,... | collective-permute-start | bytes 393224 | tf_op jit(solution)/shard_map/ppermute | solution.py:42
  179.1 8.2 %collective-permute-start.12 = (f32[2,32,512]{2,1,0:T(8,128)S(1)}, f32[2,32,512]{2,1,0:T(8,128)S(1)}, u32[]{:S(2)}, u32[]{:S(2)}) collective-permute-start(f32[2,32,512]{2,1,0:T(8,128)S(1)} %add.126), channel_id=1, source_target_pairs={{0,2},{1,3},{2,0},{3,1},{4,6},{5,7},{6,4},{7,5},{8,10},{9,11},{10,... | collective-permute-start | bytes 393224 | tf_op jit(solution)/shard_map/ppermute | solution.py:42
  180.4 7.5 %collective-permute-start.11 = (f32[2,32,512]{2,1,0:T(8,128)S(1)}, f32[2,32,512]{2,1,0:T(8,128)S(1)}, u32[]{:S(2)}, u32[]{:S(2)}) collective-permute-start(f32[2,32,512]{2,1,0:T(8,128)S(1)} %add.126), channel_id=1, source_target_pairs={{0,1},{1,0},{2,3},{3,2},{4,5},{5,4},{6,7},{7,6},{8,9},{9,8},{10,11... | collective-permute-start | bytes 393224 | tf_op jit(solution)/shard_map/ppermute | solution.py:42
  188.0 9.2 %collective-permute-start.16 = (f32[2,32,512]{2,1,0:T(8,128)S(1)}, f32[2,32,512]{2,1,0:T(8,128)S(1)}, u32[]{:S(2)}, u32[]{:S(2)}) collective-permute-start(f32[2,32,512]{2,1,0:T(8,128)S(1)} %add_add_fusion.1), channel_id=1, source_target_pairs={{0,24},{4,28},{8,16},{12,20},{16,8},{20,12},{24,0},{28,4},{32,56},... | collective-permute-start | bytes 393224 | tf_op jit(solution)/shard_map/ppermute | solution.py:42
  189.1 8.1 %collective-permute-start.15 = (f32[2,32,512]{2,1,0:T(8,128)S(1)}, f32[2,32,512]{2,1,0:T(8,128)S(1)}, u32[]{:S(2)}, u32[]{:S(2)}) collective-permute-start(f32[2,32,512]{2,1,0:T(8,128)S(1)} %add_add_fusion.1), channel_id=1, source_target_pairs={{0,16},{4,20},{8,24},{12,28},{16,0},{20,4},{24,8},{28,12},{32,48},... | collective-permute-start | bytes 393224 | tf_op jit(solution)/shard_map/ppermute | solution.py:42
  191.0 6.2 %collective-permute-start.14 = (f32[2,32,512]{2,1,0:T(8,128)S(1)}, f32[2,32,512]{2,1,0:T(8,128)S(1)}, u32[]{:S(2)}, u32[]{:S(2)}) collective-permute-start(f32[2,32,512]{2,1,0:T(8,128)S(1)} %add_add_fusion.1), channel_id=1, source_target_pairs={{0,8},{4,12},{8,0},{12,4},{16,24},{20,28},{24,16},{28,20},{32,40},... | collective-permute-start | bytes 393224 | tf_op jit(solution)/shard_map/ppermute | solution.py:42
  197.2 6.8 %collective-permute-start.19 = (f32[2,32,512]{2,1,0:T(8,128)S(1)}, f32[2,32,512]{2,1,0:T(8,128)S(1)}, u32[]{:S(2)}, u32[]{:S(2)}) collective-permute-start(f32[2,32,512]{2,1,0:T(8,128)S(1)} %add_add_fusion), channel_id=1, source_target_pairs={{0,96},{4,100},{8,104},{12,108},{16,112},{20,116},{24,120},{28,124... | collective-permute-start | bytes 393224 | tf_op jit(solution)/shard_map/ppermute | solution.py:42
  198.4 6.5 %collective-permute-start.18 = (f32[2,32,512]{2,1,0:T(8,128)S(1)}, f32[2,32,512]{2,1,0:T(8,128)S(1)}, u32[]{:S(2)}, u32[]{:S(2)}) collective-permute-start(f32[2,32,512]{2,1,0:T(8,128)S(1)} %add_add_fusion), channel_id=1, source_target_pairs={{0,64},{4,68},{8,72},{12,76},{16,80},{20,84},{24,88},{28,92},{32,9... | collective-permute-start | bytes 393224 | tf_op jit(solution)/shard_map/ppermute | solution.py:42
  200.0 5.7 %collective-permute-start.17 = (f32[2,32,512]{2,1,0:T(8,128)S(1)}, f32[2,32,512]{2,1,0:T(8,128)S(1)}, u32[]{:S(2)}, u32[]{:S(2)}) collective-permute-start(f32[2,32,512]{2,1,0:T(8,128)S(1)} %add_add_fusion), channel_id=1, source_target_pairs={{0,32},{4,36},{8,40},{12,44},{16,48},{20,52},{24,56},{28,60},{32,0... | collective-permute-start | bytes 393224 | tf_op jit(solution)/shard_map/ppermute | solution.py:42
  206.1 2.6 %copy-start.1 = (f32[2,32,512]{2,1,0:T(8,128)}, f32[2,32,512]{2,1,0:T(8,128)S(1)}, u32[]{:S(2)}) copy-start(f32[2,32,512]{2,1,0:T(8,128)S(1)} %convolution_multiply_fusion.right_t) | copy-start | bytes 393220
Sparse Core Ops, SparseCore 0:
  64.4 85.1 all-gather.2
